TPU v7x, 32 devices: a whole 2x2x4 slice. The times are simulated.
32 devices in a mesh: wide: 8 (over y, x, core), narrow: 4 (over z).
Axes of the slice: x: 2, y: 2, z: 4, core: 2. Of those that a mesh axis runs over, the one named last changes fastest.
Arguments:
- tokens: bfloat16 [2048, 3072], P('wide'), may hold values from -6 to 6
- gain: bfloat16 [3072], replicated, may hold values from 0.5 to 1.5
- w_qkv: bfloat16 [3072, 3, 3072], P('wide', None, 'narrow'), may hold values from -0.109375 to 0.109375
- w_out: bfloat16 [3072, 3072], P('wide', 'narrow'), may hold values from -3 to 3
- cache: bfloat16 [256, 64, 2, 3072], P('wide', None, None, 'narrow'), may hold values from -104 to 104
- lengths: int32 [4], replicated, may hold values from 1 to 3584, as said below
- order: int32 [32], replicated, may hold values from 0 to 31, each once
- pages: int32 [256], replicated, may hold values from 0 to 255, each once
Outputs:
- mixed: bfloat16 [2048, 3072], P('wide', 'narrow')
Inputs may be any that keep to these rules, and one draw needn't show every extreme that they name: `lengths`: some request has exactly 3584 cached positions. `order`: each query block index once. `pages`: each cache block once.
All inputs are finite; a program needn't handle non-finite values.
Results may differ from a plain program's by a relative error of at most 0.02.
The roundings to bfloat16 on the way count: a program that leaves them out, or rounds other values in their place, can miss the bound.
Values may be sent and summed in bfloat16 or wider, within the bound.
No kernel may reach another device: no remote copies, remote signals or barrier semaphores. Data moves between devices by JAX's collectives and lax.ppermute only.
A program may use at most 192 MiB of HBM per device.

v0:
```python
import jax
import jax.numpy as jnp
from jax import lax
from jax.sharding import PartitionSpec as P

HD = 96


negative = -1e30
beyond = 1073741824


def rotate(values, positions):
    half_dim = values.shape[-1] // 2
    frequency = 10000.0 ** (-2.0 * jnp.arange(half_dim, dtype=jnp.float32) / values.shape[-1])
    angles = positions.astype(jnp.float32)[:, None] * frequency[None, :]
    cos_part = jnp.cos(angles)[:, None, :]
    sin_part = jnp.sin(angles)[:, None, :]
    lower_half = values[..., :half_dim]
    upper_half = values[..., half_dim:]
    return jnp.concatenate(
        [
            lower_half * cos_part - upper_half * sin_part,
            upper_half * cos_part + lower_half * sin_part,
        ],
        axis=-1,
    )


def lookup(small_table, key_index):
    matches = key_index[..., None] == jnp.arange(small_table.shape[0], dtype=jnp.int32)
    return jnp.sum(jnp.where(matches, small_table, 0), axis=-1)


def group_rows(onehot, terms, form):
    upper_part = terms.astype(jnp.bfloat16)
    lower_part = (terms - upper_part.astype(jnp.float32)).astype(jnp.bfloat16)
    first_sum = jnp.einsum(form, onehot, upper_part, preferred_element_type=jnp.float32)
    return first_sum + jnp.einsum(form, onehot, lower_part, preferred_element_type=jnp.float32)


def attend(chosen, key_rows, values, block_req, block_pos, query_pos, requests):
    score_scale = key_rows.shape[-1] ** (-0.5)
    scores = (
        jnp.einsum("lqhe,lkhe->lhqk", chosen, key_rows, preferred_element_type=jnp.float32)
        * score_scale
    )
    allowed = block_pos[:, None, None, :] <= query_pos[:, None, :, None]
    masked = jnp.where(allowed, scores, negative)
    block_max = jnp.max(masked, axis=3)
    owners = block_req[:, None] == jnp.arange(requests, dtype=jnp.int32)[None, :]
    dev_max = jnp.max(jnp.where(owners[:, :, None, None], block_max[:, None], negative), axis=0)
    local_max = dev_max[block_req]
    exp_terms = jnp.where(allowed, jnp.exp(masked - local_max[..., None]), 0.0)
    den_terms = jnp.sum(exp_terms, axis=3)
    weights = exp_terms.astype(jnp.bfloat16)
    num_terms = jnp.einsum("lhqk,lkhe->lqhe", weights, values, preferred_element_type=jnp.float32)
    onehot = owners.astype(jnp.bfloat16)
    dev_num = group_rows(onehot, num_terms, "lr,lqhe->rqhe")
    dev_den = group_rows(onehot, den_terms, "lr,lhq->rqh")
    return (jnp.transpose(dev_max, (0, 2, 1)), dev_num, dev_den)


def slice_head(array_in, head_idx):
    return lax.dynamic_slice_in_dim(array_in, head_idx, 1, 2)


def body(tokens, gain, w_qkv, w_out, cache, lengths, order, pages):
    wide_count = lax.axis_size("wide")
    wide_index = lax.axis_index("wide")
    tok_rows = tokens.shape[0]
    cache_count = cache.shape[0]
    blk_len = cache.shape[1]
    lane_width = cache.shape[3]
    head_count = lane_width // HD
    slot_count = tok_rows // blk_len
    block_total = order.shape[0]
    req_count = lengths.shape[0]
    per_request = block_total // req_count
    fresh_len = per_request * blk_len
    table_len = pages.shape[0] // req_count
    tok_float = tokens.astype(jnp.float32)
    inv_rms = lax.rsqrt(jnp.mean(tok_float * tok_float, axis=1, keepdims=True) + 1e-05)
    normed = (tok_float * inv_rms * gain.astype(jnp.float32)[None, :]).astype(jnp.bfloat16)
    part_in = lax.all_gather(w_qkv, "wide", axis=0, tiled=True)
    part_out = lax.all_gather(w_out, "wide", axis=0, tiled=True)
    acc_sum = jnp.einsum("tk,kcj->tcj", normed, part_in, preferred_element_type=jnp.float32)
    blk_idx = jnp.arange(blk_len, dtype=jnp.int32)
    slot_blocks = lax.dynamic_slice_in_dim(order, wide_index * slot_count, slot_count)
    slot_req = slot_blocks // per_request
    slot_start = lookup(lengths, slot_req) + slot_blocks % per_request * blk_len
    slot_pos = slot_start[:, None] + blk_idx[None, :]
    positions = slot_pos.reshape(tok_rows)
    queries = (
        rotate(acc_sum[:, 0].reshape(tok_rows, head_count, HD), positions)
        .astype(jnp.bfloat16)
        .reshape(tok_rows, lane_width)
    )
    keys_new = (
        rotate(acc_sum[:, 1].reshape(tok_rows, head_count, HD), positions)
        .astype(jnp.bfloat16)
        .reshape(slot_count, blk_len, head_count, HD)
    )
    vals_new = acc_sum[:, 2].astype(jnp.bfloat16).reshape(slot_count, blk_len, head_count, HD)
    all_queries = lax.all_gather(queries, "wide", axis=0, tiled=True)
    block_ids = jnp.arange(block_total, dtype=jnp.int32)
    slot_of = jnp.sum(
        jnp.where(order[None, :] == block_ids[:, None], block_ids[None, :], 0), axis=1
    )
    ordered = all_queries.reshape(block_total, blk_len, lane_width)[slot_of].reshape(
        req_count, fresh_len, head_count, HD
    )
    cache_ids = wide_index * cache_count + jnp.arange(cache_count, dtype=jnp.int32)
    page_ids = jnp.arange(pages.shape[0], dtype=jnp.int32)
    entries = jnp.sum(jnp.where(pages[None, :] == cache_ids[:, None], page_ids[None, :], 0), axis=1)
    cache_req = entries // table_len
    cache_pos = (entries % table_len)[:, None] * blk_len + blk_idx[None, :]
    cache_pos = jnp.where(cache_pos < lookup(lengths, cache_req)[:, None], cache_pos, beyond)
    block_req = jnp.concatenate([cache_req, slot_req])
    block_pos = jnp.concatenate([cache_pos, slot_pos])
    key_rows = jnp.concatenate(
        [cache[:, :, 0].reshape(cache_count, blk_len, head_count, HD), keys_new]
    )
    values = jnp.concatenate(
        [cache[:, :, 1].reshape(cache_count, blk_len, head_count, HD), vals_new]
    )
    chosen = ordered[block_req]
    query_pos = (
        lookup(lengths, block_req)[:, None] + jnp.arange(fresh_len, dtype=jnp.int32)[None, :]
    )

    def head_part(head_idx):
        return attend(
            slice_head(chosen, head_idx),
            slice_head(key_rows, head_idx),
            slice_head(values, head_idx),
            block_req,
            block_pos,
            query_pos,
            req_count,
        )

    head_max, head_num, head_den = lax.map(head_part, jnp.arange(head_count, dtype=jnp.int32))
    all_rows = req_count * fresh_len
    dev_max = jnp.transpose(head_max[..., 0], (1, 2, 0)).reshape(all_rows, head_count)
    dev_num = jnp.transpose(head_num[:, :, :, 0], (1, 2, 0, 3)).reshape(all_rows, head_count, HD)
    dev_den = jnp.transpose(head_den[..., 0], (1, 2, 0)).reshape(all_rows, head_count)
    sent_max = dev_max.reshape(wide_count, tok_rows, head_count)
    sent_num = dev_num.reshape(wide_count, tok_rows, lane_width)
    sent_den = dev_den.reshape(wide_count, tok_rows, head_count)
    got_max, got_num, got_den = (
        lax.all_to_all(sent_max, "wide", split_axis=0, concat_axis=0, tiled=True),
        lax.all_to_all(sent_num, "wide", split_axis=0, concat_axis=0, tiled=True),
        lax.all_to_all(sent_den, "wide", split_axis=0, concat_axis=0, tiled=True),
    )
    top_max = jnp.max(got_max, axis=0)
    factor = jnp.exp(got_max - top_max[None])
    num_own = jnp.sum(
        got_num.reshape(wide_count, tok_rows, head_count, HD) * factor[..., None], axis=0
    ).reshape(tok_rows, lane_width)
    den_own = jnp.sum(got_den * factor, axis=0)
    attention = (
        (num_own.reshape(tok_rows, head_count, HD) / den_own[..., None])
        .astype(jnp.bfloat16)
        .reshape(tok_rows, lane_width)
    )
    out_part = lax.dot_general(
        attention, part_out, (((1,), (1,)), ((), ())), preferred_element_type=jnp.float32
    )
    return lax.psum_scatter(
        out_part.astype(jnp.bfloat16), "narrow", scatter_dimension=1, tiled=True
    )


def solution(mesh):
    in_specs = (
        P("wide", None),
        P(),
        P("wide", None, "narrow"),
        P("wide", "narrow"),
        P("wide", None, None, "narrow"),
        P(),
        P(),
        P(),
    )
    out_specs = P("wide", "narrow")
    return jax.shard_map(body, mesh=mesh, in_specs=in_specs, out_specs=out_specs, check_vma=False)
```

profile of v0, /device:TPU:0, one launch (start us, length us, event | category | flops | bytes accessed | tf_op | source)
XLA Modules:
  0.0 541.1 jit_solution(3883787900699118251)
XLA Ops:
  11.8 78.9 %all-gather.4.cloned.1.call-done = bf16[3072,3,768]{2,0,1:T(8,128)(2,1)} async-done(((bf16[384,3,768]{2,0,1:T(8,128)(2,1)}), bf16[3072,3,768]{2,0,1:T(8,128)(2,1)}) %all-gather.4.cloned.1.call-update) | async-done | bytes 14155792 | tf_op jit(solution)/shard_map/all_gather | solution.py:85
  90.8 8.0 %fusion.53 = f32[256,3,768]{2,0,1:T(8,128)S(1)} fusion(bf16[3072,3,768]{2,0,1:T(8,128)(2,1)} %all-gather.4.cloned.1.call-done, bf16[256,3072]{1,0:T(8,128)(2,1)} %param.10, f32[3072]{0:T(1024)S(1)} %convert_element_type.74, f32[256]{0:T(256)S(1)} %add_rsqrt_fusion), kind=kOutput, calls=%fused_computation.67 | convolution fusion | flops 3627024384 | bytes 18101248 | tf_op jit(solution)/shard_map/tk,kcj->tcj/dot_general | solution.py:87
  103.9 31.1 %slice_reduce_fusion = (bf16[32,64,768]{2,1,0:T(8,128)(2,1)S(1)}, bf16[32,64,768]{2,1,0:T(8,128)(2,1)}) fusion(bf16[32,64,2,768]{3,2,1,0:T(2,128)(2,1)} %param.14), kind=kLoop, calls=%fused_computation.56 | loop fusion | bytes 12582912 | tf_op jit(solution)/shard_map/slice | solution.py:125
  135.0 8.2 %reshape_squeeze.13 = bf16[32,64,8,96]{3,2,1,0:T(8,128)(2,1)} reshape(bf16[32,64,768]{2,1,0:T(8,128)(2,1)} %get-tuple-element.148) | data formatting | bytes 6291456 | tf_op jit(solution)/shard_map/reshape;squeeze | solution.py:122
  143.2 5.4 reshape_squeeze.15
  166.3 4.6 copy.69
  173.6 5.4 reshape.331
  179.0 5.8 %copy.70 = bf16[4,512,8,96]{1,3,2,0:T(8,128)(2,1)S(1)} copy(bf16[4,512,8,96]{3,2,1,0:T(8,128)(2,1)} %reshape.331) | data formatting | bytes 6291456 | tf_op jit(solution)/shard_map/reshape | solution.py:110
  184.8 11.4 %gather_fusion.2 = bf16[36,512,8,96]{1,3,2,0:T(8,128)(2,1)} fusion(bf16[4,512,8,96]{1,3,2,0:T(8,128)(2,1)S(1)} %copy.70, s32[1024]{0:T(1024)S(1)} %pad_clamp_fusion.1), kind=kCustom, calls=%fused_computation.2 | custom fusion | bytes 56623248 | tf_op jit(solution)/shard_map/gather | solution.py:127
  196.2 192.4 %while.15 = (s32[]{:T(128)}, f32[8,4,512,1]{2,0,1,3:T(8,128)}, f32[8,4,512,1,96]{2,1,4,3,0:T(4,128)}, f32[8,4,512,1]{2,0,1,3:T(8,128)S(1)}, s32[36]{0:T(128)S(1)...) while((s32[]{:T(128)}, f32[8,4,512,1]{2,0,1,3:T(8,128)}, ...), condition=%wide.region_10.11_spmd.clone, body=%wide.region_6.10_spmd.clone.sunk | while | flops 509732608 | bytes 71870680 | solution.py:143
  198.8 5.6 %fusion.92 = (f32[36,512]{1,0:T(8,128)S(1)}, f32[36,512,64]{1,2,0:T(8,128)}) fusion(s32[36,512]{1,0:T(8,128)S(1)} %iota_add_fusion.4, s32[36,64]{1,0:T(8,128)S(1)} %get-tuple-element.295, bf16[36,512,8,96]{1,3,2,0:T(8,128)(2,1)} %get-tuple-element.297, s32[]{:T(128)S(6)} %select_n.201, bf16[36,64,8,96]{3,1,0,2:T(8,128)(2,1)} %get-tuple-element.298), kind=kOutput, calls=%fused_computation.13.clone.1 | convolution fusion | flops 231192576 | bytes 9005056 | tf_op jit(solution)/shard_map/while/body/eval_jaxpr/lqhe,lkhe->lhqk/dot_general | solution.py:45
  206.8 4.1 fusion.94
  222.8 5.6 %fusion.92 = (f32[36,512]{1,0:T(8,128)S(1)}, f32[36,512,64]{1,2,0:T(8,128)}) fusion(s32[36,512]{1,0:T(8,128)S(1)} %iota_add_fusion.4, s32[36,64]{1,0:T(8,128)S(1)} %get-tuple-element.295, bf16[36,512,8,96]{1,3,2,0:T(8,128)(2,1)} %get-tuple-element.297, s32[]{:T(128)S(6)} %select_n.201, bf16[36,64,8,96]{3,1,0,2:T(8,128)(2,1)} %get-tuple-element.298), kind=kOutput, calls=%fused_computation.13.clone.1 | convolution fusion | flops 231192576 | bytes 9005056 | tf_op jit(solution)/shard_map/while/body/eval_jaxpr/lqhe,lkhe->lhqk/dot_general | solution.py:45
  230.8 4.1 fusion.94
  246.9 5.6 %fusion.92 = (f32[36,512]{1,0:T(8,128)S(1)}, f32[36,512,64]{1,2,0:T(8,128)}) fusion(s32[36,512]{1,0:T(8,128)S(1)} %iota_add_fusion.4, s32[36,64]{1,0:T(8,128)S(1)} %get-tuple-element.295, bf16[36,512,8,96]{1,3,2,0:T(8,128)(2,1)} %get-tuple-element.297, s32[]{:T(128)S(6)} %select_n.201, bf16[36,64,8,96]{3,1,0,2:T(8,128)(2,1)} %get-tuple-element.298), kind=kOutput, calls=%fused_computation.13.clone.1 | convolution fusion | flops 231192576 | bytes 9005056 | tf_op jit(solution)/shard_map/while/body/eval_jaxpr/lqhe,lkhe->lhqk/dot_general | solution.py:45
  254.9 4.1 fusion.94
  271.0 5.6 %fusion.92 = (f32[36,512]{1,0:T(8,128)S(1)}, f32[36,512,64]{1,2,0:T(8,128)}) fusion(s32[36,512]{1,0:T(8,128)S(1)} %iota_add_fusion.4, s32[36,64]{1,0:T(8,128)S(1)} %get-tuple-element.295, bf16[36,512,8,96]{1,3,2,0:T(8,128)(2,1)} %get-tuple-element.297, s32[]{:T(128)S(6)} %select_n.201, bf16[36,64,8,96]{3,1,0,2:T(8,128)(2,1)} %get-tuple-element.298), kind=kOutput, calls=%fused_computation.13.clone.1 | convolution fusion | flops 231192576 | bytes 9005056 | tf_op jit(solution)/shard_map/while/body/eval_jaxpr/lqhe,lkhe->lhqk/dot_general | solution.py:45
  279.0 4.1 fusion.94
  295.0 5.6 %fusion.92 = (f32[36,512]{1,0:T(8,128)S(1)}, f32[36,512,64]{1,2,0:T(8,128)}) fusion(s32[36,512]{1,0:T(8,128)S(1)} %iota_add_fusion.4, s32[36,64]{1,0:T(8,128)S(1)} %get-tuple-element.295, bf16[36,512,8,96]{1,3,2,0:T(8,128)(2,1)} %get-tuple-element.297, s32[]{:T(128)S(6)} %select_n.201, bf16[36,64,8,96]{3,1,0,2:T(8,128)(2,1)} %get-tuple-element.298), kind=kOutput, calls=%fused_computation.13.clone.1 | convolution fusion | flops 231192576 | bytes 9005056 | tf_op jit(solution)/shard_map/while/body/eval_jaxpr/lqhe,lkhe->lhqk/dot_general | solution.py:45
  303.0 4.1 fusion.94
  319.1 5.6 %fusion.92 = (f32[36,512]{1,0:T(8,128)S(1)}, f32[36,512,64]{1,2,0:T(8,128)}) fusion(s32[36,512]{1,0:T(8,128)S(1)} %iota_add_fusion.4, s32[36,64]{1,0:T(8,128)S(1)} %get-tuple-element.295, bf16[36,512,8,96]{1,3,2,0:T(8,128)(2,1)} %get-tuple-element.297, s32[]{:T(128)S(6)} %select_n.201, bf16[36,64,8,96]{3,1,0,2:T(8,128)(2,1)} %get-tuple-element.298), kind=kOutput, calls=%fused_computation.13.clone.1 | convolution fusion | flops 231192576 | bytes 9005056 | tf_op jit(solution)/shard_map/while/body/eval_jaxpr/lqhe,lkhe->lhqk/dot_general | solution.py:45
  343.1 5.6 %fusion.92 = (f32[36,512]{1,0:T(8,128)S(1)}, f32[36,512,64]{1,2,0:T(8,128)}) fusion(s32[36,512]{1,0:T(8,128)S(1)} %iota_add_fusion.4, s32[36,64]{1,0:T(8,128)S(1)} %get-tuple-element.295, bf16[36,512,8,96]{1,3,2,0:T(8,128)(2,1)} %get-tuple-element.297, s32[]{:T(128)S(6)} %select_n.201, bf16[36,64,8,96]{3,1,0,2:T(8,128)(2,1)} %get-tuple-element.298), kind=kOutput, calls=%fused_computation.13.clone.1 | convolution fusion | flops 231192576 | bytes 9005056 | tf_op jit(solution)/shard_map/while/body/eval_jaxpr/lqhe,lkhe->lhqk/dot_general | solution.py:45
  351.1 4.1 fusion.94
  367.2 5.6 %fusion.92 = (f32[36,512]{1,0:T(8,128)S(1)}, f32[36,512,64]{1,2,0:T(8,128)}) fusion(s32[36,512]{1,0:T(8,128)S(1)} %iota_add_fusion.4, s32[36,64]{1,0:T(8,128)S(1)} %get-tuple-element.295, bf16[36,512,8,96]{1,3,2,0:T(8,128)(2,1)} %get-tuple-element.297, s32[]{:T(128)S(6)} %select_n.201, bf16[36,64,8,96]{3,1,0,2:T(8,128)(2,1)} %get-tuple-element.298), kind=kOutput, calls=%fused_computation.13.clone.1 | convolution fusion | flops 231192576 | bytes 9005056 | tf_op jit(solution)/shard_map/while/body/eval_jaxpr/lqhe,lkhe->lhqk/dot_general | solution.py:45
  375.2 4.1 fusion.94
  388.6 7.7 %all_to_all.15 = f32[8,256,8]{1,2,0:T(8,128)S(1)} all-to-all(f32[8,256,8]{1,2,0:T(8,128)S(1)} %bitcast.138), channel_id=1, replica_groups=mesh['wide'=8,'narrow'=4] {'wide'}, dimensions={0} | all-to-all | bytes 131072 | tf_op jit(solution)/shard_map/all_to_all | solution.py:154
  399.9 7.9 %reshape_reshape.9 = f32[8,256,768]{1,0,2:T(8,128)} reshape(f32[4,512,8,96]{1,0,3,2:T(4,128)} %bitcast.132) | data formatting | bytes 12582912 | tf_op jit(solution)/shard_map/reshape;reshape | solution.py:149
  407.7 7.5 %copy.77 = f32[8,256,768]{1,2,0:T(8,128)} copy(f32[8,256,768]{1,0,2:T(8,128)} %reshape_reshape.9) | data formatting | bytes 12582912 | tf_op jit(solution)/shard_map/reshape;reshape | solution.py:149
  415.2 4.8 all-to-all-start
  420.1 71.5 %all-to-all-done = f32[8,256,768]{1,2,0:T(8,128)} async-done(((f32[8,256,768]{1,2,0:T(8,128)}), f32[8,256,768]{1,2,0:T(8,128)}, u32[]{:S(2)}, u32[]{:S(2)}) %all-to-all-start) | async-done | bytes 6291488 | tf_op jit(solution)/shard_map/all_to_all | solution.py:153
  495.0 4.9 convolution_convert_fusion
  500.0 34.6 %reduce-scatter.2.cloned.1.call-done = bf16[256,768]{1,0:T(8,128)(2,1)} async-done(((bf16[256,3072]{1,0:T(8,128)(2,1)}), bf16[256,768]{1,0:T(8,128)(2,1)}) %reduce-scatter.2.cloned.1.call-update) | async-done | bytes 393232 | tf_op jit(solution)/shard_map/reduce_scatter | solution.py:170
  (258 shorter events, 140.5 us)
Async XLA Ops:
  6.5 84.2 %all-gather.4.cloned.1.call-start = ((), (), s32[]{:S(2)}) async-start(), calls=%async_computation.4 | async-start | bytes 15925248 | tf_op jit(solution)/shard_map/all_gather | solution.py:85
  7.3 159.0 %all-gather.6.cloned.1.call-start = ((), (), s32[]{:S(2)}) async-start(), calls=%async_computation.5 | async-start | bytes 3538944 | tf_op jit(solution)/shard_map/all_gather | solution.py:105
  98.8 1.5 copy-start
  98.8 4.5 copy-start.1
  98.8 4.8 copy-start.3
  98.8 4.9 copy-start.2
  102.5 392.5 %all-gather.8.cloned.1.call-start = ((), (), s32[]{:S(2)}) async-start(), calls=%async_computation.6 | async-start | bytes 5308416 | tf_op jit(solution)/shard_map/all_gather | solution.py:86
  212.0 6.3 %slice-start = ((s8[4718592]{0:T(1024)(128)(4,1)}), s8[4194304]{0:T(1024)(128)(4,1)S(1)}, s32[]{:S(2)}) async-start(s8[4718592]{0:T(1024)(128)(4,1)} %bitcast.129), calls=%async_computation.8 | async-start | bytes 8388608 | tf_op jit(solution)/shard_map/while
  214.4 3.9 slice-start.1
  236.0 6.3 %slice-start = ((s8[4718592]{0:T(1024)(128)(4,1)}), s8[4194304]{0:T(1024)(128)(4,1)S(1)}, s32[]{:S(2)}) async-start(s8[4718592]{0:T(1024)(128)(4,1)} %bitcast.129), calls=%async_computation.8 | async-start | bytes 8388608 | tf_op jit(solution)/shard_map/while
  238.5 3.9 slice-start.1
  260.1 6.3 %slice-start = ((s8[4718592]{0:T(1024)(128)(4,1)}), s8[4194304]{0:T(1024)(128)(4,1)S(1)}, s32[]{:S(2)}) async-start(s8[4718592]{0:T(1024)(128)(4,1)} %bitcast.129), calls=%async_computation.8 | async-start | bytes 8388608 | tf_op jit(solution)/shard_map/while
  262.5 3.9 slice-start.1
  284.2 6.3 %slice-start = ((s8[4718592]{0:T(1024)(128)(4,1)}), s8[4194304]{0:T(1024)(128)(4,1)S(1)}, s32[]{:S(2)}) async-start(s8[4718592]{0:T(1024)(128)(4,1)} %bitcast.129), calls=%async_computation.8 | async-start | bytes 8388608 | tf_op jit(solution)/shard_map/while
  286.6 3.9 slice-start.1
  308.3 6.3 %slice-start = ((s8[4718592]{0:T(1024)(128)(4,1)}), s8[4194304]{0:T(1024)(128)(4,1)S(1)}, s32[]{:S(2)}) async-start(s8[4718592]{0:T(1024)(128)(4,1)} %bitcast.129), calls=%async_computation.8 | async-start | bytes 8388608 | tf_op jit(solution)/shard_map/while
  310.7 3.9 slice-start.1
  332.3 6.3 %slice-start = ((s8[4718592]{0:T(1024)(128)(4,1)}), s8[4194304]{0:T(1024)(128)(4,1)S(1)}, s32[]{:S(2)}) async-start(s8[4718592]{0:T(1024)(128)(4,1)} %bitcast.129), calls=%async_computation.8 | async-start | bytes 8388608 | tf_op jit(solution)/shard_map/while
  334.7 3.9 slice-start.1
  356.3 6.3 %slice-start = ((s8[4718592]{0:T(1024)(128)(4,1)}), s8[4194304]{0:T(1024)(128)(4,1)S(1)}, s32[]{:S(2)}) async-start(s8[4718592]{0:T(1024)(128)(4,1)} %bitcast.129), calls=%async_computation.8 | async-start | bytes 8388608 | tf_op jit(solution)/shard_map/while
  358.8 3.9 slice-start.1
  380.4 6.3 %slice-start = ((s8[4718592]{0:T(1024)(128)(4,1)}), s8[4194304]{0:T(1024)(128)(4,1)S(1)}, s32[]{:S(2)}) async-start(s8[4718592]{0:T(1024)(128)(4,1)} %bitcast.129), calls=%async_computation.8 | async-start | bytes 8388608 | tf_op jit(solution)/shard_map/while
  382.8 3.9 slice-start.1
  396.3 18.9 %all-to-all-start.1 = ((f32[8,256,8]{1,2,0:T(8,128)}), f32[8,256,8]{1,2,0:T(8,128)S(1)}, u32[]{:S(2)}, u32[]{:S(2)}) async-start(f32[8,256,8]{1,2,0:T(8,128)} %bitcast.16), calls=%async_computation.1 | async-start | bytes 131072 | tf_op jit(solution)/shard_map/all_to_all | solution.py:152
  415.2 76.4 %all-to-all-start = ((f32[8,256,768]{1,2,0:T(8,128)}), f32[8,256,768]{1,2,0:T(8,128)}, u32[]{:S(2)}, u32[]{:S(2)}) async-start(f32[8,256,768]{1,2,0:T(8,128)} %copy.77), calls=%async_computation | async-start | bytes 12582912 | tf_op jit(solution)/shard_map/all_to_all | solution.py:153
  420.0 114.6 %reduce-scatter.2.cloned.1.call-start = ((), (), s32[]{:S(2)}) async-start(), calls=%async_computation.7 | async-start | bytes 1966080 | tf_op jit(solution)/shard_map/reduce_scatter | solution.py:170
Sparse Core Ops, SparseCore 0:
  9.3 81.4 all-gather.3
  102.6 32.8 all-gather.5
  137.4 38.9 all-gather.7
  500.1 34.4 reduce-scatter.1
where the time goes:
time: 543 us; the launch traced here: 541 us
  waiting for transfers between devices  186 us (34%)
  matrix products  138 us (25%)
  local copies, waits for them, and re-layouts  126 us (23%)
  other arithmetic  45.2 us (8%)
  loops' own time  16.2 us (3%)
  between operations  13.4 us (2%)
  starting transfers between devices  8.49 us (2%)
  blocking collectives  7.65 us (1%)
    all_gather x1, waiting for transfers between devices, body(): part_in = lax.all_gather(w_qkv, 'wide', axis=0, tiled=True)  78.9 us
    all_to_all x1, waiting for transfers between devices, body(): lax.all_to_all(sent_num, 'wide', split_axis=0, concat_axis=0, tiled=True)  71.5 us
    dot_general x8, matrix products, attend(): jnp.einsum('lqhe,lkhe->lhqk', chosen, key_rows, preferred_element_type=jn...  44.8 us
    reduce_scatter x1, waiting for transfers between devices, body(): lax.psum_scatter(out_part.astype(jnp.bfloat16), 'narrow', scatter_dimensi...  34.6 us
    dot_general x8, matrix products, attend(): jnp.einsum('lhqk,lkhe->lqhe', weights, values, preferred_element_type=jnp...  32.7 us
    slice x1, local copies, waits for them, and re-layouts, body(): cache[:, :, 1].reshape(cache_count, blk_len, head_count, HD)  31.1 us
    dot_general x16, matrix products, group_rows(): jnp.einsum(form, onehot, upper_part, preferred_element_type=jnp.float32)  27.6 us
    dot_general x16, matrix products, group_rows(): jnp.einsum(form, onehot, lower_part, preferred_element_type=jnp.float32)  20.2 us
  transfers between devices with their start and end apart: 6, of which 3 were waited for; matrix products, arithmetic and copies ran while one was open for 54% of the time, Pallas kernels for 0%

commit v1 on v0

v1 whole, which is shorter than its diff:
```python
import jax
import jax.numpy as jnp
from jax import lax
from jax.experimental import pallas as pl
from jax.experimental.pallas import tpu as pltpu
from jax.sharding import PartitionSpec as P

HD = 96


negative = -1e30
beyond = 1073741824


def rotate(values, positions):
    half_dim = values.shape[-1] // 2
    frequency = 10000.0 ** (-2.0 * jnp.arange(half_dim, dtype=jnp.float32) / values.shape[-1])
    angles = positions.astype(jnp.float32)[:, None] * frequency[None, :]
    cos_part = jnp.cos(angles)[:, None, :]
    sin_part = jnp.sin(angles)[:, None, :]
    lower_half = values[..., :half_dim]
    upper_half = values[..., half_dim:]
    return jnp.concatenate(
        [
            lower_half * cos_part - upper_half * sin_part,
            upper_half * cos_part + lower_half * sin_part,
        ],
        axis=-1,
    )


def lookup(small_table, key_index):
    matches = key_index[..., None] == jnp.arange(small_table.shape[0], dtype=jnp.int32)
    return jnp.sum(jnp.where(matches, small_table, 0), axis=-1)


def attend_kernel(carry_in):
    def kernel(req_ref, base_ref, limit_ref, len_ref, *refs):
        if carry_in:
            q_ref, k_ref, v_ref, m0_ref, l0_ref, o0_ref, m_ref, l_ref, o_ref = refs
        else:
            q_ref, k_ref, v_ref, m_ref, l_ref, o_ref = refs
        step = pl.program_id(0)

        @pl.when(step == 0)
        def _():
            if carry_in:
                m_ref[...] = m0_ref[...]
                l_ref[...] = l0_ref[...]
                o_ref[...] = o0_ref[...]
            else:
                m_ref[...] = jnp.full(m_ref.shape, negative, jnp.float32)
                l_ref[...] = jnp.zeros(l_ref.shape, jnp.float32)
                o_ref[...] = jnp.zeros(o_ref.shape, jnp.float32)

        req = req_ref[step]
        base = base_ref[step]
        limit = limit_ref[step]
        qlen = len_ref[req]
        queries = q_ref[req]
        keys = k_ref[0]
        vals = v_ref[0]
        blk_len = keys.shape[1]
        q_len = queries.shape[1]
        scale = keys.shape[-1] ** (-0.5)
        scores = (
            jnp.einsum("hkd,hqd->hkq", keys, queries, preferred_element_type=jnp.float32)
            * scale
        )
        key_pos = base + lax.broadcasted_iota(jnp.int32, (blk_len, q_len), 0)
        query_pos = qlen + lax.broadcasted_iota(jnp.int32, (blk_len, q_len), 1)
        allowed = ((key_pos < limit) & (key_pos <= query_pos))[None]
        masked = jnp.where(allowed, scores, negative)
        m_old = m_ref[req]
        m_new = jnp.maximum(m_old, jnp.max(masked, axis=1, keepdims=True))
        exp_terms = jnp.where(allowed, jnp.exp(masked - m_new), 0.0)
        alpha = jnp.exp(m_old - m_new)
        l_ref[req] = alpha * l_ref[req] + jnp.sum(exp_terms, axis=1, keepdims=True)
        weighted = jnp.einsum(
            "hdk,hkq->hdq", vals, exp_terms.astype(jnp.bfloat16),
            preferred_element_type=jnp.float32,
        )
        o_ref[req] = alpha * o_ref[req] + weighted
        m_ref[req] = m_new

    return kernel


def attend_blocks(queries, keys, vals_t, blk_req, blk_base, blk_limit, lengths, carry=None):
    req_count, head_count, q_len, head_dim = queries.shape
    blk_count, _, blk_len, _ = keys.shape
    vmem = pltpu.MemorySpace.VMEM
    whole = pl.BlockSpec(memory_space=vmem)
    in_specs = [
        whole,
        pl.BlockSpec((1, head_count, blk_len, head_dim), lambda j, *_: (j, 0, 0, 0)),
        pl.BlockSpec((1, head_count, head_dim, blk_len), lambda j, *_: (j, 0, 0, 0)),
    ]
    args = [queries, keys, vals_t]
    if carry is not None:
        in_specs += [whole, whole, whole]
        args += list(carry)
    out_shape = (
        jax.ShapeDtypeStruct((req_count, head_count, 1, q_len), jnp.float32),
        jax.ShapeDtypeStruct((req_count, head_count, 1, q_len), jnp.float32),
        jax.ShapeDtypeStruct((req_count, head_count, head_dim, q_len), jnp.float32),
    )
    grid_spec = pltpu.PrefetchScalarGridSpec(
        num_scalar_prefetch=4,
        grid=(blk_count,),
        in_specs=in_specs,
        out_specs=(whole, whole, whole),
    )
    return pl.pallas_call(
        attend_kernel(carry is not None),
        out_shape=out_shape,
        grid_spec=grid_spec,
        compiler_params=pltpu.CompilerParams(
            dimension_semantics=("arbitrary",)
        ),
    )(blk_req, blk_base, blk_limit, lengths, *args)


def body(tokens, gain, w_qkv, w_out, cache, lengths, order, pages):
    wide_count = lax.axis_size("wide")
    wide_index = lax.axis_index("wide")
    tok_rows = tokens.shape[0]
    cache_count = cache.shape[0]
    blk_len = cache.shape[1]
    lane_width = cache.shape[3]
    head_count = lane_width // HD
    slot_count = tok_rows // blk_len
    block_total = order.shape[0]
    req_count = lengths.shape[0]
    per_request = block_total // req_count
    fresh_len = per_request * blk_len
    table_len = pages.shape[0] // req_count
    tok_float = tokens.astype(jnp.float32)
    inv_rms = lax.rsqrt(jnp.mean(tok_float * tok_float, axis=1, keepdims=True) + 1e-05)
    normed = (tok_float * inv_rms * gain.astype(jnp.float32)[None, :]).astype(jnp.bfloat16)

    w_q = lax.all_gather(w_qkv[:, 0], "wide", axis=0, tiled=True)
    blk_idx = jnp.arange(blk_len, dtype=jnp.int32)
    slot_blocks = lax.dynamic_slice_in_dim(order, wide_index * slot_count, slot_count)
    slot_req = slot_blocks // per_request
    slot_start = lookup(lengths, slot_req) + slot_blocks % per_request * blk_len
    slot_pos = slot_start[:, None] + blk_idx[None, :]
    positions = slot_pos.reshape(tok_rows)
    q_proj = jnp.dot(normed, w_q, preferred_element_type=jnp.float32)
    queries = (
        rotate(q_proj.reshape(tok_rows, head_count, HD), positions)
        .astype(jnp.bfloat16)
        .reshape(tok_rows, lane_width)
    )
    all_queries = lax.all_gather(queries, "wide", axis=0, tiled=True)
    all_queries, w_kv_local = lax.optimization_barrier((all_queries, w_qkv[:, 1:]))
    w_kv = lax.all_gather(w_kv_local, "wide", axis=0, tiled=True)

    block_ids = jnp.arange(block_total, dtype=jnp.int32)
    slot_of = jnp.sum(
        jnp.where(order[None, :] == block_ids[:, None], block_ids[None, :], 0), axis=1
    )
    ordered = all_queries.reshape(block_total, blk_len, lane_width)[slot_of].reshape(
        req_count, fresh_len, head_count, HD
    )
    q_heads = jnp.transpose(ordered, (0, 2, 1, 3))

    cache_ids = wide_index * cache_count + jnp.arange(cache_count, dtype=jnp.int32)
    page_ids = jnp.arange(pages.shape[0], dtype=jnp.int32)
    entries = jnp.sum(jnp.where(pages[None, :] == cache_ids[:, None], page_ids[None, :], 0), axis=1)
    cache_req = entries // table_len
    cache_base = (entries % table_len) * blk_len
    cache_limit = lookup(lengths, cache_req)
    cache_keys = jnp.transpose(
        cache[:, :, 0].reshape(cache_count, blk_len, head_count, HD), (0, 2, 1, 3)
    )
    cache_vals = jnp.transpose(
        cache[:, :, 1].reshape(cache_count, blk_len, head_count, HD), (0, 2, 3, 1)
    )
    carry = attend_blocks(
        q_heads, cache_keys, cache_vals, cache_req, cache_base, cache_limit, lengths
    )
    carry, w_out_local = lax.optimization_barrier((carry, w_out))
    part_out = lax.all_gather(w_out_local, "wide", axis=0, tiled=True)

    kv_proj = jnp.einsum("tk,kcj->tcj", normed, w_kv, preferred_element_type=jnp.float32)
    keys_new = (
        rotate(kv_proj[:, 0].reshape(tok_rows, head_count, HD), positions)
        .astype(jnp.bfloat16)
        .reshape(slot_count, blk_len, head_count, HD)
    )
    vals_new = kv_proj[:, 1].astype(jnp.bfloat16).reshape(slot_count, blk_len, head_count, HD)
    new_limit = jnp.full((slot_count,), beyond, jnp.int32)
    head_max, head_den, head_num = attend_blocks(
        q_heads,
        jnp.transpose(keys_new, (0, 2, 1, 3)),
        jnp.transpose(vals_new, (0, 2, 3, 1)),
        slot_req,
        slot_start,
        new_limit,
        lengths,
        carry=carry,
    )

    split = fresh_len // tok_rows
    sent_num = (
        head_num.reshape(req_count, head_count, HD, split, tok_rows)
        .transpose(0, 3, 1, 2, 4)
        .reshape(wide_count, head_count, HD, tok_rows)
        .astype(jnp.bfloat16)
    )
    stats = jnp.concatenate([head_max, head_den], axis=2)
    sent_stats = (
        stats.reshape(req_count, head_count, 2, split, tok_rows)
        .transpose(0, 3, 1, 2, 4)
        .reshape(wide_count, head_count, 2, tok_rows)
    )
    got_num = lax.all_to_all(sent_num, "wide", split_axis=0, concat_axis=0, tiled=True)
    got_stats = lax.all_to_all(sent_stats, "wide", split_axis=0, concat_axis=0, tiled=True)
    got_max = got_stats[:, :, 0:1]
    got_den = got_stats[:, :, 1:2]
    top_max = jnp.max(got_max, axis=0)
    factor = jnp.exp(got_max - top_max[None])
    num_own = jnp.sum(got_num.astype(jnp.float32) * factor, axis=0)
    den_own = jnp.sum(got_den * factor, axis=0)
    attention = (
        jnp.transpose((num_own / den_own).astype(jnp.bfloat16), (2, 0, 1))
        .reshape(tok_rows, lane_width)
    )
    out_part = lax.dot_general(
        attention, part_out, (((1,), (1,)), ((), ())), preferred_element_type=jnp.float32
    )
    return lax.psum_scatter(
        out_part.astype(jnp.bfloat16), "narrow", scatter_dimension=1, tiled=True
    )


def solution(mesh):
    in_specs = (
        P("wide", None),
        P(),
        P("wide", None, "narrow"),
        P("wide", "narrow"),
        P("wide", None, None, "narrow"),
        P(),
        P(),
        P(),
    )
    out_specs = P("wide", "narrow")
    return jax.shard_map(body, mesh=mesh, in_specs=in_specs, out_specs=out_specs, check_vma=False)
```

time: 543 us -> 323 us (0.59)
  matrix products: 138 us -> 14.7 us
  Pallas kernels: 0 us -> 49.3 us
  local copies, waits for them, and re-layouts: 126 us -> 77.5 us
  waiting for transfers between devices: 186 us -> 143 us
  other arithmetic: 45.2 us -> 16.7 us
  loops' own time: 16.2 us -> 0 us
  blocking collectives: 7.65 us -> 0 us
    dot_general x49 -> x2, matrix products: 133 us -> 9.76 us  [the longest x1 5.37 us: body(): jnp.einsum('tk,kcj->tcj', normed, w_kv, preferred_element_type=jnp.float32)]
    pallas_call x0 -> x2, Pallas kernels: none -> 49.3 us  [attend_blocks(): pl.pallas_call(attend_kernel(carry is not None), out_shape=out_shape, gri...]
    all_gather x2 -> x3, waiting for transfers between devices: 79 us -> 37.7 us  [the longest x1 37.7 us: body(): w_q = lax.all_gather(w_qkv[:, 0], 'wide', axis=0, tiled=True)]
    all_to_all x1, waiting for transfers between devices: 71.5 us -> 37.5 us  [body(): lax.all_to_all(sent_num, 'wide', split_axis=0, concat_axis=0, tiled=True)]
    all_gather x1, waiting for transfers between devices: 0.01 us -> 31.2 us  [body(): all_queries = lax.all_gather(queries, 'wide', axis=0, tiled=True)]
    another operation x3 -> x2, local copies, waits for them, and re-layouts: 20.7 us -> 0.91 us  [the longest x2 15.3 us: body(): sent_num = dev_num.reshape(wide_count, tok_rows, lane_width)]
    gather x9 -> x0, local copies, waits for them, and re-layouts: 16.2 us -> none  [the longest x1 11.4 us: body(): chosen = ordered[block_req]]
    another operation x1 -> x0, loops' own time: 16.2 us -> none  [body(): lax.map(head_part, jnp.arange(head_count, dtype=jnp.int32))]
  transfers between devices with their start and end apart: 6 -> 7, of which waited for: 3 -> 5; matrix products, arithmetic and copies ran while one was open for 54% -> 30% of each run, Pallas kernels for 0% -> 15%
where the time goes in v1:
time: 323 us; the launch traced here: 322 us
  waiting for transfers between devices  143 us (44%)
  local copies, waits for them, and re-layouts  77.5 us (24%)
  Pallas kernels  49.3 us (15%)
  other arithmetic  16.7 us (5%)
  matrix products  14.7 us (5%)
  between operations  13.4 us (4%)
  starting transfers between devices  7.19 us (2%)
    pallas_call x2, Pallas kernels, attend_blocks(): pl.pallas_call(attend_kernel(carry is not None), out_shape=out_shape, gri...  49.3 us
    slice x2, local copies, waits for them, and re-layouts, body(): cache[:, :, 1].reshape(cache_count, blk_len, head_count, HD)  41.5 us
    all_gather x1, waiting for transfers between devices, body(): w_q = lax.all_gather(w_qkv[:, 0], 'wide', axis=0, tiled=True)  37.7 us
    all_to_all x1, waiting for transfers between devices, body(): lax.all_to_all(sent_num, 'wide', split_axis=0, concat_axis=0, tiled=True)  37.5 us
    reduce_scatter x1, waiting for transfers between devices, body(): lax.psum_scatter(out_part.astype(jnp.bfloat16), 'narrow', scatter_dimensi...  34.7 us
    all_gather x1, waiting for transfers between devices, body(): all_queries = lax.all_gather(queries, 'wide', axis=0, tiled=True)  31.2 us
    another operation x2, local copies, waits for them, and re-layouts, body(): cache[:, :, 0].reshape(cache_count, blk_len, head_count, HD)  11.8 us
    reshape x2, local copies, waits for them, and re-layouts, body(): all_queries.reshape(block_total, blk_len, lane_width)[slot_of]  10.7 us
  transfers between devices with their start and end apart: 7, of which 5 were waited for; matrix products, arithmetic and copies ran while one was open for 30% of the time, Pallas kernels for 15%

profile of v1, /device:TPU:0, one launch (start us, length us, event | category | flops | bytes accessed | tf_op | source)
XLA Modules:
  0.0 321.5 jit_solution(7820590331458008485)
XLA Ops:
  6.5 2.0 slice.51
  8.7 0.7 and_select_fusion.3
  9.4 0.8 select_reduce_fusion.3
  11.1 1.8 fusion.2
  13.2 37.7 %all-gather.12.cloned.1.call-done = bf16[3072,1,768]{2,0,1:T(8,128)(2,1)} async-done(((bf16[384,1,768]{2,0,1:T(8,128)(2,1)}), bf16[3072,1,768]{2,0,1:T(8,128)(2,1)}) %all-gather.12.cloned.1.call-update) | async-done | bytes 4718608 | tf_op jit(solution)/shard_map/all_gather | solution.py:142
  50.9 4.4 %fusion = f32[256,768]{0,1:T(8,128)S(1)} fusion(bf16[3072,1,768]{2,0,1:T(8,128)(2,1)} %all-gather.12.cloned.1.call-done, bf16[256,3072]{1,0:T(8,128)(2,1)S(1)} %copy-done.2, f32[3072]{0:T(1024)S(1)} %convert_element_type.49, f32[256]{0:T(256)S(1)} %add_rsqrt_fusion), kind=kOutput, calls=%fused_computation.3 | convolution fusion | flops 1211105280 | bytes 7091200 | tf_op jit(solution)/shard_map/dot_general | solution.py:149
  55.4 0.8 pad_maximum_fusion.1
  56.9 1.1 slice.54
  58.0 31.2 %all-gather.6.cloned.1.call-done = bf16[2048,768]{0,1:T(8,128)(2,1)} async-done(((bf16[256,768]{0,1:T(8,128)(2,1)}), bf16[2048,768]{0,1:T(8,128)(2,1)}) %all-gather.6.cloned.1.call-update) | async-done | bytes 3145744 | tf_op jit(solution)/shard_map/all_gather | solution.py:155
  89.3 26.0 %fusion.17 = (bf16[32,64,1,768]{3,2,1,0:T(2,128)(2,1)}, bf16[32,64,768]{2,1,0:T(8,128)(2,1)S(1)}) fusion(bf16[32,64,2,768]{3,2,1,0:T(2,128)(2,1)} %param.12), kind=kLoop, calls=%fused_computation.64 | loop fusion | bytes 12582912 | tf_op jit(solution)/shard_map/slice | solution.py:178
  115.2 5.4 %reshape_squeeze.10 = bf16[32,64,8,96]{3,2,1,0:T(8,128)(2,1)} reshape(bf16[32,64,768]{2,1,0:T(8,128)(2,1)S(1)} %get-tuple-element.34) | data formatting | bytes 6291456 | tf_op jit(solution)/shard_map/reshape;squeeze | solution.py:175
  120.6 6.4 %copy.41 = bf16[32,64,8,96]{3,1,2,0:T(8,128)(2,1)} copy(bf16[32,64,8,96]{3,2,1,0:T(8,128)(2,1)} %reshape_squeeze.10) | data formatting | bytes 6291456 | tf_op jit(solution)/shard_map/reshape;squeeze | solution.py:175
  127.1 15.5 %copy.35 = bf16[32,64,1,768]{1,3,0,2:T(8,128)(2,1)} copy(bf16[32,64,1,768]{3,2,1,0:T(2,128)(2,1)} %get-tuple-element.33) | data formatting | bytes 6291456 | tf_op jit(solution)/shard_map/slice | solution.py:178
  144.1 2.9 copy.28
  147.0 2.6 gather_fusion
  149.7 5.5 %reshape.153 = bf16[4,512,8,96]{3,2,1,0:T(8,128)(2,1)} reshape(bf16[32,64,768]{2,1,0:T(8,128)(2,1)S(1)} %gather_fusion) | data formatting | bytes 6291456 | tf_op jit(solution)/shard_map/reshape | solution.py:163
  155.1 5.2 %copy.42 = bf16[4,512,8,96]{3,1,2,0:T(8,128)(2,1)} copy(bf16[4,512,8,96]{3,2,1,0:T(8,128)(2,1)} %reshape.153) | data formatting | bytes 6291456 | tf_op jit(solution)/shard_map/reshape | solution.py:163
  160.3 37.3 %shard_map.82 = (f32[4,8,1,512]{3,2,1,0:T(1,128)}, f32[4,8,1,512]{3,2,1,0:T(1,128)}, f32[4,8,96,512]{3,2,1,0:T(8,128)}) custom-call(s32[32]{0:T(128)} %copy-done.8, s32[32]{0:T(128)} %get-tuple-element.43.base_ref, s32[32]{0:T(128)} %select_reduce_fusion.2.limit_ref, s32[4]{0:T(128)} %len_ref.3, bf16[4,8,512,96]{3,2,1,0:T(8,128)(2,1)} %bitcast.46, ...), custom_call_target="tpu_custom_call" | custom-call | tf_op jit(solution)/shard_map/pallas_call | solution.py:114
  197.6 5.4 %fusion.5 = f32[256,2,768]{2,0,1:T(8,128)S(1)} fusion(bf16[3072,2,768]{2,0,1:T(8,128)(2,1)} %all-gather.8.cloned.1.call-done, bf16[256,3072]{1,0:T(8,128)(2,1)S(1)} %copy-done.3, f32[3072]{0:T(1024)S(1)} %convert_element_type.49, f32[256]{0:T(256)S(1)} %add_rsqrt_fusion), kind=kOutput, calls=%fused_computation.14 | convolution fusion | flops 2419064832 | bytes 12596224 | tf_op jit(solution)/shard_map/tk,kcj->tcj/dot_general | solution.py:186
  205.2 1.2 copy.33
  206.5 1.1 maximum_bitcast_fusion.refs_1_
  208.1 12.1 %shard_map.83 = (f32[4,8,1,512]{3,2,1,0:T(1,128)}, f32[4,8,1,512]{3,2,1,0:T(1,128)}, f32[4,8,96,512]{3,2,1,0:T(8,128)}) custom-call(s32[4]{0:T(128)} %copy-done.6, s32[4]{0:T(128)} %copy-done.5, s32[4]{0:T(128)} %broadcast_13_limit_ref.2.limit_ref, s32[4]{0:T(128)} %len_ref.3, bf16[4,8,512,96]{3,2,1,0:T(8,128)(2,1)} %bitcast.47, ...), custom_call_target="tpu_custom_call" | custom-call | tf_op jit(solution)/shard_map/pallas_call | solution.py:114
  220.1 0.9 fusion.11
  221.0 1.5 fusion.10
  222.5 3.4 %all-to-all-start.1 = ((f32[8,8,2,256]{3,2,1,0:T(2,128)}), f32[8,8,2,256]{3,2,1,0:T(2,128)S(1)}, u32[]{:S(2)}, u32[]{:S(2)}) async-start(f32[8,8,2,256]{3,2,1,0:T(2,128)} %bitcast.15), calls=%async_computation.1 | async-start | bytes 262144 | tf_op jit(solution)/shard_map/all_to_all | solution.py:219
  225.9 3.3 %convert.28 = bf16[4,8,96,512]{3,2,1,0:T(8,128)(2,1)S(1)} convert(f32[4,8,96,512]{3,2,1,0:T(8,128)} %get-tuple-element.25) | non-fusion elementwise | flops 1572864 | bytes 9437184 | tf_op jit(solution)/shard_map/convert.3
  229.7 1.9 pad_maximum_fusion
  231.6 1.5 all-to-all-done.1
  233.1 3.6 %all-to-all-start = ((bf16[8,8,96,256]{3,2,1,0:T(8,128)(2,1)}), bf16[8,8,96,256]{3,2,1,0:T(8,128)(2,1)S(1)}, u32[]{:S(2)}, u32[]{:S(2)}) async-start(bf16[8,8,96,256]{3,2,1,0:T(8,128)(2,1)} %bitcast.14), calls=%async_computation | async-start | bytes 6291456 | tf_op jit(solution)/shard_map/all_to_all | solution.py:218
  237.0 37.5 %all-to-all-done = bf16[8,8,96,256]{3,2,1,0:T(8,128)(2,1)S(1)} async-done(((bf16[8,8,96,256]{3,2,1,0:T(8,128)(2,1)}), bf16[8,8,96,256]{3,2,1,0:T(8,128)(2,1)S(1)}, u32[]{:S(2)}, u32[]{:S(2)}) %all-to-all-start) | async-done | bytes 3145760 | tf_op jit(solution)/shard_map/all_to_all | solution.py:218
  275.4 4.9 %convolution_convert_fusion = bf16[256,3072]{1,0:T(8,128)(2,1)} fusion(bf16[256,768]{0,1:T(8,128)(2,1)S(1)} %bitcast.55, bf16[3072,768]{1,0:T(8,128)(2,1)} %all-gather.10.cloned.1.call-done), kind=kOutput, calls=%fused_computation.9 | convolution fusion | flops 1208745984 | bytes 6684672 | tf_op jit(solution)/shard_map/dot_general | solution.py:230
  280.4 34.7 %reduce-scatter.2.cloned.1.call-done = bf16[256,768]{1,0:T(8,128)(2,1)} async-done(((bf16[256,3072]{1,0:T(8,128)(2,1)}), bf16[256,768]{1,0:T(8,128)(2,1)}) %reduce-scatter.2.cloned.1.call-update) | async-done | bytes 393232 | tf_op jit(solution)/shard_map/reduce_scatter | solution.py:233
  (63 shorter events, 7.8 us)
Async XLA Ops:
  6.5 44.4 %copy-start.2 = (bf16[256,3072]{1,0:T(8,128)(2,1)S(1)}, bf16[256,3072]{1,0:T(8,128)(2,1)}, u32[]{:S(2)}) copy-start(bf16[256,3072]{1,0:T(8,128)(2,1)} %param.8) | copy-start | bytes 4718596
  6.5 44.4 %all-gather.12.cloned.1.call-start = ((), (), s32[]{:S(2)}) async-start(), calls=%async_computation.7 | async-start | bytes 5308416 | tf_op jit(solution)/shard_map/all_gather | solution.py:142
  8.6 80.6 %all-gather.6.cloned.1.call-start = ((), (), s32[]{:S(2)}) async-start(), calls=%async_computation.3 | async-start | bytes 3538944 | tf_op jit(solution)/shard_map/all_gather | solution.py:155
  9.4 45.9 %copy-start.6 = (s32[4]{0:T(128)}, s32[4]{0:T(128)S(1)}, u32[]{:S(2)}) copy-start(s32[4]{0:T(128)S(1)} %get-tuple-element.31.req_ref) | copy-start | bytes 52
  10.2 45.1 %copy-start.5 = (s32[4]{0:T(128)}, s32[4]{0:T(128)S(1)}, u32[]{:S(2)}) copy-start(s32[4]{0:T(128)S(1)} %fusion.14.base_ref) | copy-start | bytes 52
  55.3 1.6 copy-start.1
  56.2 141.4 %all-gather.8.cloned.1.call-start = ((), (), s32[]{:S(2)}) async-start(), calls=%async_computation.4 | async-start | bytes 10616832 | tf_op jit(solution)/shard_map/all_gather | solution.py:157
  89.2 186.2 %all-gather.10.cloned.1.call-start = ((), (), s32[]{:S(2)}) async-start(), calls=%async_computation.5 | async-start | bytes 5308416 | tf_op jit(solution)/shard_map/all_gather | solution.py:184
  127.1 15.5 %copy-start.9 = (s32[32]{0:T(128)S(1)}, s32[32]{0:T(128)}, u32[]{:S(2)}) copy-start(s32[32]{0:T(128)} %param.14) | copy-start | bytes 388
  127.1 15.7 %copy-start.7 = (s32[256]{0:T(256)S(1)}, s32[256]{0:T(256)}, u32[]{:S(2)}) copy-start(s32[256]{0:T(256)} %param.15) | copy-start | bytes 3076
  127.1 16.5 %copy-start.4 = (s32[4]{0:T(128)S(1)}, s32[4]{0:T(128)}, u32[]{:S(2)}) copy-start(s32[4]{0:T(128)} %len_ref.3) | copy-start | bytes 52
  127.1 17.1 %copy-start = (bf16[2048,768]{0,1:T(8,128)(2,1)S(1)}, bf16[2048,768]{0,1:T(8,128)(2,1)}, u32[]{:S(2)}) copy-start(bf16[2048,768]{0,1:T(8,128)(2,1)} %all-gather.6.cloned.1.call-done) | copy-start | bytes 9437188
  143.5 3.5 %copy-start.8 = (s32[32]{0:T(128)}, s32[32]{0:T(128)S(1)}, u32[]{:S(2)}) copy-start(s32[32]{0:T(128)S(1)} %get-tuple-element.44.req_ref) | copy-start | bytes 388
  160.3 37.3 %copy-start.3 = (bf16[256,3072]{1,0:T(8,128)(2,1)S(1)}, bf16[256,3072]{1,0:T(8,128)(2,1)}, u32[]{:S(2)}) copy-start(bf16[256,3072]{1,0:T(8,128)(2,1)} %param.8) | copy-start | bytes 4718596
  222.5 10.6 %all-to-all-start.1 = ((f32[8,8,2,256]{3,2,1,0:T(2,128)}), f32[8,8,2,256]{3,2,1,0:T(2,128)S(1)}, u32[]{:S(2)}, u32[]{:S(2)}) async-start(f32[8,8,2,256]{3,2,1,0:T(2,128)} %bitcast.15), calls=%async_computation.1 | async-start | bytes 262144 | tf_op jit(solution)/shard_map/all_to_all | solution.py:219
  233.1 41.5 %all-to-all-start = ((bf16[8,8,96,256]{3,2,1,0:T(8,128)(2,1)}), bf16[8,8,96,256]{3,2,1,0:T(8,128)(2,1)S(1)}, u32[]{:S(2)}, u32[]{:S(2)}) async-start(bf16[8,8,96,256]{3,2,1,0:T(8,128)(2,1)} %bitcast.14), calls=%async_computation | async-start | bytes 6291456 | tf_op jit(solution)/shard_map/all_to_all | solution.py:218
  236.7 78.3 %reduce-scatter.2.cloned.1.call-start = ((), (), s32[]{:S(2)}) async-start(), calls=%async_computation.6 | async-start | bytes 1966080 | tf_op jit(solution)/shard_map/reduce_scatter | solution.py:233
Sparse Core Ops, SparseCore 0:
  9.2 41.6 all-gather.11
  56.4 32.8 all-gather.5
  91.1 58.8 all-gather.7
  197.7 40.8 all-gather.9
  280.5 34.4 reduce-scatter.1

commit v2 on v1

--- a/solution.py
+++ b/solution.py
@@ -34,12 +34,12 @@
     return jnp.sum(jnp.where(matches, small_table, 0), axis=-1)
 
 
-def attend_kernel(carry_in):
+def attend_kernel(carry_in, head_count, head_dim):
     def kernel(req_ref, base_ref, limit_ref, len_ref, *refs):
         if carry_in:
-            q_ref, k_ref, v_ref, m0_ref, l0_ref, o0_ref, m_ref, l_ref, o_ref = refs
+            q_ref, kv_ref, m0_ref, l0_ref, o0_ref, m_ref, l_ref, o_ref = refs
         else:
-            q_ref, k_ref, v_ref, m_ref, l_ref, o_ref = refs
+            q_ref, kv_ref, m_ref, l_ref, o_ref = refs
         step = pl.program_id(0)
 
         @pl.when(step == 0)
@@ -57,46 +57,56 @@
         base = base_ref[step]
         limit = limit_ref[step]
         qlen = len_ref[req]
-        queries = q_ref[req]
-        keys = k_ref[0]
-        vals = v_ref[0]
-        blk_len = keys.shape[1]
-        q_len = queries.shape[1]
-        scale = keys.shape[-1] ** (-0.5)
-        scores = (
-            jnp.einsum("hkd,hqd->hkq", keys, queries, preferred_element_type=jnp.float32)
-            * scale
-        )
+        blk_len = kv_ref.shape[0]
+        q_len = q_ref.shape[2]
+        scale = head_dim ** (-0.5)
         key_pos = base + lax.broadcasted_iota(jnp.int32, (blk_len, q_len), 0)
         query_pos = qlen + lax.broadcasted_iota(jnp.int32, (blk_len, q_len), 1)
-        allowed = ((key_pos < limit) & (key_pos <= query_pos))[None]
-        masked = jnp.where(allowed, scores, negative)
-        m_old = m_ref[req]
-        m_new = jnp.maximum(m_old, jnp.max(masked, axis=1, keepdims=True))
-        exp_terms = jnp.where(allowed, jnp.exp(masked - m_new), 0.0)
-        alpha = jnp.exp(m_old - m_new)
-        l_ref[req] = alpha * l_ref[req] + jnp.sum(exp_terms, axis=1, keepdims=True)
-        weighted = jnp.einsum(
-            "hdk,hkq->hdq", vals, exp_terms.astype(jnp.bfloat16),
-            preferred_element_type=jnp.float32,
-        )
-        o_ref[req] = alpha * o_ref[req] + weighted
-        m_ref[req] = m_new
+        allowed = (key_pos < limit) & (key_pos <= query_pos)
+        for head in range(head_count):
+            lanes = pl.ds(head * head_dim, head_dim)
+            queries = q_ref[req, head]
+            keys = kv_ref[:, 0, lanes]
+            vals = kv_ref[:, 1, lanes]
+            scores = (
+                lax.dot_general(
+                    keys, queries, (((1,), (1,)), ((), ())),
+                    preferred_element_type=jnp.float32,
+                )
+                * scale
+            )
+            masked = jnp.where(allowed, scores, negative)
+            m_old = m_ref[req, head]
+            m_new = jnp.maximum(m_old, jnp.max(masked, axis=0, keepdims=True))
+            exp_terms = jnp.where(allowed, jnp.exp(masked - m_new), 0.0)
+            alpha = jnp.exp(m_old - m_new)
+            l_ref[req, head] = alpha * l_ref[req, head] + jnp.sum(
+                exp_terms, axis=0, keepdims=True
+            )
+            weighted = lax.dot_general(
+                vals, exp_terms.astype(jnp.bfloat16), (((0,), (0,)), ((), ())),
+                preferred_element_type=jnp.float32,
+            )
+            o_ref[req, head] = alpha * o_ref[req, head] + weighted
+            m_ref[req, head] = m_new
 
     return kernel
 
 
-def attend_blocks(queries, keys, vals_t, blk_req, blk_base, blk_limit, lengths, carry=None):
+def attend_blocks(queries, kv, kv_index, blk_req, blk_base, blk_limit, lengths, carry=None):
     req_count, head_count, q_len, head_dim = queries.shape
-    blk_count, _, blk_len, _ = keys.shape
+    blk_count = blk_req.shape[0]
+    blk_len = kv.shape[1]
+    lane_width = kv.shape[3]
     vmem = pltpu.MemorySpace.VMEM
     whole = pl.BlockSpec(memory_space=vmem)
     in_specs = [
         whole,
-        pl.BlockSpec((1, head_count, blk_len, head_dim), lambda j, *_: (j, 0, 0, 0)),
-        pl.BlockSpec((1, head_count, head_dim, blk_len), lambda j, *_: (j, 0, 0, 0)),
+        pl.BlockSpec(
+            (None, blk_len, 2, lane_width), lambda j, *_: (kv_index(j), 0, 0, 0)
+        ),
     ]
-    args = [queries, keys, vals_t]
+    args = [queries, kv]
     if carry is not None:
         in_specs += [whole, whole, whole]
         args += list(carry)
@@ -112,12 +122,10 @@
         out_specs=(whole, whole, whole),
     )
     return pl.pallas_call(
-        attend_kernel(carry is not None),
+        attend_kernel(carry is not None, head_count, head_dim),
         out_shape=out_shape,
         grid_spec=grid_spec,
-        compiler_params=pltpu.CompilerParams(
-            dimension_semantics=("arbitrary",)
-        ),
+        compiler_params=pltpu.CompilerParams(dimension_semantics=("arbitrary",)),
     )(blk_req, blk_base, blk_limit, lengths, *args)
 
 
@@ -171,14 +179,8 @@
     cache_req = entries // table_len
     cache_base = (entries % table_len) * blk_len
     cache_limit = lookup(lengths, cache_req)
-    cache_keys = jnp.transpose(
-        cache[:, :, 0].reshape(cache_count, blk_len, head_count, HD), (0, 2, 1, 3)
-    )
-    cache_vals = jnp.transpose(
-        cache[:, :, 1].reshape(cache_count, blk_len, head_count, HD), (0, 2, 3, 1)
-    )
     carry = attend_blocks(
-        q_heads, cache_keys, cache_vals, cache_req, cache_base, cache_limit, lengths
+        q_heads, cache, lambda j: j, cache_req, cache_base, cache_limit, lengths
     )
     carry, w_out_local = lax.optimization_barrier((carry, w_out))
     part_out = lax.all_gather(w_out_local, "wide", axis=0, tiled=True)
@@ -187,14 +189,17 @@
     keys_new = (
         rotate(kv_proj[:, 0].reshape(tok_rows, head_count, HD), positions)
         .astype(jnp.bfloat16)
-        .reshape(slot_count, blk_len, head_count, HD)
-    )
-    vals_new = kv_proj[:, 1].astype(jnp.bfloat16).reshape(slot_count, blk_len, head_count, HD)
+        .reshape(tok_rows, lane_width)
+    )
+    vals_new = kv_proj[:, 1].astype(jnp.bfloat16)
     new_limit = jnp.full((slot_count,), beyond, jnp.int32)
+    kv_new = jnp.stack([keys_new, vals_new], axis=1).reshape(
+        slot_count, blk_len, 2, lane_width
+    )
     head_max, head_den, head_num = attend_blocks(
         q_heads,
-        jnp.transpose(keys_new, (0, 2, 1, 3)),
-        jnp.transpose(vals_new, (0, 2, 3, 1)),
+        kv_new,
+        lambda j: j,
         slot_req,
         slot_start,
         new_limit,
@@ -230,9 +235,13 @@
     out_part = lax.dot_general(
         attention, part_out, (((1,), (1,)), ((), ())), preferred_element_type=jnp.float32
     )
-    return lax.psum_scatter(
-        out_part.astype(jnp.bfloat16), "narrow", scatter_dimension=1, tiled=True
-    )
+    narrow_count = lax.axis_size("narrow")
+    out_cols = out_part.shape[1] // narrow_count
+    sent_out = jnp.transpose(
+        out_part.astype(jnp.bfloat16).reshape(tok_rows, narrow_count, out_cols), (1, 0, 2)
+    )
+    got_out = lax.all_to_all(sent_out, "narrow", split_axis=0, concat_axis=0, tiled=True)
+    return jnp.sum(got_out.astype(jnp.float32), axis=0).astype(jnp.bfloat16)
 
 
 def solution(mesh):

time: 323 us -> 327 us (1.012)
  local copies, waits for them, and re-layouts: 77.5 us -> 25.2 us
  Pallas kernels: 49.3 us -> 100 us
  blocking collectives: 0 us -> 38.5 us
  waiting for transfers between devices: 143 us -> 110 us
    pallas_call x2, Pallas kernels: 49.3 us -> 100 us  [attend_blocks(): pl.pallas_call(attend_kernel(carry is not None, head_count, head_dim), ou...]
    slice x3 -> x1, local copies, waits for them, and re-layouts: 41.5 us -> 0.04 us  [body(): vals_new = kv_proj[:, 1].astype(jnp.bfloat16)]
    all_to_all x0 -> x1, blocking collectives: none -> 38.5 us  [body(): lax.all_to_all(sent_out, 'narrow', split_axis=0, concat_axis=0, tiled=True)]
    reduce_scatter x1 -> x0, waiting for transfers between devices: 34.7 us -> none  [body(): lax.psum_scatter(out_part.astype(jnp.bfloat16), 'narrow', scatter_dimensi...]
    another operation x4 -> x3, local copies, waits for them, and re-layouts: 12.7 us -> 1.52 us  [the longest x2 11.8 us: body(): cache[:, :, 0].reshape(cache_count, blk_len, head_count, HD)]
    another operation x4 -> x5, other arithmetic: 5.1 us -> 6.87 us
  transfers between devices with their start and end apart: 7 -> 6, of which waited for: 5 -> 4; matrix products, arithmetic and copies ran while one was open for 30% -> 13% of each run, Pallas kernels for 15% -> 31%
where the time goes in v2:
time: 327 us; the launch traced here: 325 us
  waiting for transfers between devices  110 us (34%)
  Pallas kernels  100 us (31%)
  blocking collectives  38.5 us (12%)
  local copies, waits for them, and re-layouts  25.2 us (8%)
  other arithmetic  17.8 us (5%)
  matrix products  13.5 us (4%)
  between operations  13.5 us (4%)
  starting transfers between devices  7.33 us (2%)
    pallas_call x2, Pallas kernels, attend_blocks(): pl.pallas_call(attend_kernel(carry is not None, head_count, head_dim), ou...  100 us
    all_to_all x1, blocking collectives, body(): lax.all_to_all(sent_out, 'narrow', split_axis=0, concat_axis=0, tiled=True)  38.5 us
    all_gather x1, waiting for transfers between devices, body(): w_q = lax.all_gather(w_qkv[:, 0], 'wide', axis=0, tiled=True)  37.7 us
    all_to_all x1, waiting for transfers between devices, body(): lax.all_to_all(sent_num, 'wide', split_axis=0, concat_axis=0, tiled=True)  37.6 us
    all_gather x1, waiting for transfers between devices, body(): all_queries = lax.all_gather(queries, 'wide', axis=0, tiled=True)  31.1 us
    reshape x2, local copies, waits for them, and re-layouts, body(): all_queries.reshape(block_total, blk_len, lane_width)[slot_of]  10.6 us
  transfers between devices with their start and end apart: 6, of which 4 were waited for; matrix products, arithmetic and copies ran while one was open for 13% of the time, Pallas kernels for 31%

profile of v2, /device:TPU:0, one launch (start us, length us, event | category | flops | bytes accessed | tf_op | source)
XLA Modules:
  0.0 325.4 jit_solution(11000018144148826573)
XLA Ops:
  6.5 2.0 slice.45
  8.7 0.7 and_select_fusion.3
  9.4 0.8 select_reduce_fusion.3
  10.4 0.7 convert_element_type.58
  11.1 1.8 fusion.2
  13.2 37.7 %all-gather.12.cloned.1.call-done = bf16[3072,1,768]{2,0,1:T(8,128)(2,1)} async-done(((bf16[384,1,768]{2,0,1:T(8,128)(2,1)}), bf16[3072,1,768]{2,0,1:T(8,128)(2,1)}) %all-gather.12.cloned.1.call-update) | async-done | bytes 4718608 | tf_op jit(solution)/shard_map/all_gather | solution.py:150
  50.9 4.4 %fusion = f32[256,768]{0,1:T(8,128)S(1)} fusion(bf16[3072,1,768]{2,0,1:T(8,128)(2,1)} %all-gather.12.cloned.1.call-done, bf16[256,3072]{1,0:T(8,128)(2,1)S(1)} %copy-done.1, f32[3072]{0:T(1024)S(1)} %convert_element_type.58, f32[256]{0:T(256)S(1)} %add_rsqrt_fusion), kind=kOutput, calls=%fused_computation.2 | convolution fusion | flops 1211105280 | bytes 7091200 | tf_op jit(solution)/shard_map/dot_general | solution.py:157
  55.5 0.8 pad_maximum_fusion.2
  56.3 0.6 copy-done
  56.9 1.2 slice.48
  58.1 31.1 %all-gather.6.cloned.1.call-done = bf16[2048,768]{0,1:T(8,128)(2,1)} async-done(((bf16[256,768]{0,1:T(8,128)(2,1)}), bf16[2048,768]{0,1:T(8,128)(2,1)}) %all-gather.6.cloned.1.call-update) | async-done | bytes 3145744 | tf_op jit(solution)/shard_map/all_gather | solution.py:163
  91.0 4.7 %copy.31 = bf16[2048,768]{1,0:T(8,128)(2,1)} copy(bf16[2048,768]{0,1:T(8,128)(2,1)} %all-gather.6.cloned.1.call-done) | data formatting | bytes 6291456 | tf_op jit(solution)/shard_map/optimization_barrier | solution.py:164
  95.7 2.7 gather_fusion
  98.4 5.5 %reshape.163 = bf16[4,512,8,96]{3,2,1,0:T(8,128)(2,1)} reshape(bf16[32,64,768]{2,1,0:T(8,128)(2,1)S(1)} %gather_fusion) | data formatting | bytes 6291456 | tf_op jit(solution)/shard_map/reshape | solution.py:171
  103.9 5.1 %copy.46 = bf16[4,512,8,96]{3,1,2,0:T(8,128)(2,1)} copy(bf16[4,512,8,96]{3,2,1,0:T(8,128)(2,1)} %reshape.163) | data formatting | bytes 6291456 | tf_op jit(solution)/shard_map/reshape | solution.py:171
  109.0 82.5 %shard_map.82 = (f32[4,8,1,512]{3,2,1,0:T(1,128)}, f32[4,8,1,512]{3,2,1,0:T(1,128)}, f32[4,8,96,512]{3,2,1,0:T(8,128)}) custom-call(s32[32]{0:T(128)} %copy-done.9, s32[32]{0:T(128)} %get-tuple-element.41.base_ref, s32[32]{0:T(128)} %select_reduce_fusion.2.limit_ref, s32[4]{0:T(128)} %len_ref.3, bf16[4,8,512,96]{3,2,1,0:T(8,128)(2,1)} %bitcast.41, ...), custom_call_target="tpu_custom_call" | custom-call | tf_op jit(solution)/shard_map/pallas_call | solution.py:124
  191.6 5.4 %fusion.5 = f32[256,2,768]{2,0,1:T(8,128)S(1)} fusion(bf16[3072,2,768]{2,0,1:T(8,128)(2,1)} %all-gather.8.cloned.1.call-done, bf16[256,3072]{1,0:T(8,128)(2,1)S(1)} %copy-done.2, f32[3072]{0:T(1024)S(1)} %convert_element_type.58, f32[256]{0:T(256)S(1)} %add_rsqrt_fusion), kind=kOutput, calls=%fused_computation.13 | convolution fusion | flops 2419064832 | bytes 12596224 | tf_op jit(solution)/shard_map/tk,kcj->tcj/dot_general | solution.py:188
  197.3 0.6 copy.36
  198.4 0.9 copy.35
  199.4 2.5 pad_maximum_fusion.1.refs_1_
  202.4 17.6 %shard_map.83 = (f32[4,8,1,512]{3,2,1,0:T(1,128)}, f32[4,8,1,512]{3,2,1,0:T(1,128)}, f32[4,8,96,512]{3,2,1,0:T(8,128)}) custom-call(s32[4]{0:T(128)} %copy-done.7, s32[4]{0:T(128)} %copy-done.6, s32[4]{0:T(128)} %broadcast_13_limit_ref.2.limit_ref, s32[4]{0:T(128)} %len_ref.3, bf16[4,8,512,96]{3,2,1,0:T(8,128)(2,1)} %bitcast.42, ...), custom_call_target="tpu_custom_call" | custom-call | tf_op jit(solution)/shard_map/pallas_call | solution.py:124
  219.9 3.4 %convert.27 = bf16[4,8,96,512]{3,2,1,0:T(8,128)(2,1)S(1)} convert(f32[4,8,96,512]{3,2,1,0:T(8,128)} %get-tuple-element.25) | non-fusion elementwise | flops 1572864 | bytes 9437184 | tf_op jit(solution)/shard_map/convert.4
  223.4 0.7 fusion.10
  224.2 3.4 %all-to-all-start.1 = ((f32[8,8,2,256]{3,2,1,0:T(2,128)}), f32[8,8,2,256]{3,2,1,0:T(2,128)S(1)}, u32[]{:S(2)}, u32[]{:S(2)}) async-start(f32[8,8,2,256]{3,2,1,0:T(2,128)} %bitcast.11), calls=%async_computation.1 | async-start | bytes 262144 | tf_op jit(solution)/shard_map/all_to_all | solution.py:224
  228.0 1.9 pad_maximum_fusion
  229.9 3.1 all-to-all-done.1
  233.0 3.6 %all-to-all-start = ((bf16[8,8,96,256]{3,2,1,0:T(8,128)(2,1)}), bf16[8,8,96,256]{3,2,1,0:T(8,128)(2,1)S(1)}, u32[]{:S(2)}, u32[]{:S(2)}) async-start(bf16[8,8,96,256]{3,2,1,0:T(8,128)(2,1)} %bitcast.10), calls=%async_computation | async-start | bytes 6291456 | tf_op jit(solution)/shard_map/all_to_all | solution.py:223
  236.9 37.6 %all-to-all-done = bf16[8,8,96,256]{3,2,1,0:T(8,128)(2,1)S(1)} async-done(((bf16[8,8,96,256]{3,2,1,0:T(8,128)(2,1)}), bf16[8,8,96,256]{3,2,1,0:T(8,128)(2,1)S(1)}, u32[]{:S(2)}, u32[]{:S(2)}) %all-to-all-start) | async-done | bytes 3145760 | tf_op jit(solution)/shard_map/all_to_all | solution.py:223
  274.5 0.8 multiply_reduce_fusion
  275.4 3.8 %convolution_convert_fusion = bf16[256,3072]{1,0:T(8,128)(2,1)S(1)} fusion(bf16[256,768]{0,1:T(8,128)(2,1)S(1)} %bitcast.50, bf16[3072,768]{1,0:T(8,128)(2,1)} %all-gather.10.cloned.1.call-done), kind=kOutput, calls=%fused_computation.7 | convolution fusion | flops 1208745984 | bytes 6684672 | tf_op jit(solution)/shard_map/dot_general | solution.py:235
  279.3 38.5 %all_to_all.15 = bf16[4,256,768]{2,1,0:T(8,128)(2,1)S(1)} all-to-all(bf16[4,256,768]{2,1,0:T(8,128)(2,1)S(1)} %bitcast.44), channel_id=1, replica_groups=mesh['wide'=8,'narrow'=4] {'narrow'}, dimensions={0} | all-to-all | bytes 3145728 | tf_op jit(solution)/shard_map/all_to_all | solution.py:243
  317.8 1.1 reduce_sum.88
  (59 shorter events, 4.7 us)
Async XLA Ops:
  6.5 44.4 %copy-start.1 = (bf16[256,3072]{1,0:T(8,128)(2,1)S(1)}, bf16[256,3072]{1,0:T(8,128)(2,1)}, u32[]{:S(2)}) copy-start(bf16[256,3072]{1,0:T(8,128)(2,1)} %param.8) | copy-start | bytes 4718596
  6.5 44.4 %all-gather.12.cloned.1.call-start = ((), (), s32[]{:S(2)}) async-start(), calls=%async_computation.6 | async-start | bytes 5308416 | tf_op jit(solution)/shard_map/all_gather | solution.py:150
  8.6 80.6 %all-gather.6.cloned.1.call-start = ((), (), s32[]{:S(2)}) async-start(), calls=%async_computation.3 | async-start | bytes 3538944 | tf_op jit(solution)/shard_map/all_gather | solution.py:163
  9.4 45.9 %copy-start.7 = (s32[4]{0:T(128)}, s32[4]{0:T(128)S(1)}, u32[]{:S(2)}) copy-start(s32[4]{0:T(128)S(1)} %get-tuple-element.31.req_ref) | copy-start | bytes 52
  10.2 45.1 %copy-start.6 = (s32[4]{0:T(128)}, s32[4]{0:T(128)S(1)}, u32[]{:S(2)}) copy-start(s32[4]{0:T(128)S(1)} %fusion.14.base_ref) | copy-start | bytes 52
  55.3 1.6 copy-start
  55.3 34.2 %copy-start.10 = (s32[32]{0:T(128)S(1)}, s32[32]{0:T(128)}, u32[]{:S(2)}) copy-start(s32[32]{0:T(128)} %param.14) | copy-start | bytes 388
  55.3 34.3 %copy-start.8 = (s32[256]{0:T(256)S(1)}, s32[256]{0:T(256)}, u32[]{:S(2)}) copy-start(s32[256]{0:T(256)} %param.15) | copy-start | bytes 3076
  55.3 35.1 %copy-start.5 = (s32[4]{0:T(128)S(1)}, s32[4]{0:T(128)}, u32[]{:S(2)}) copy-start(s32[4]{0:T(128)} %len_ref.3) | copy-start | bytes 52
  56.3 135.3 %all-gather.8.cloned.1.call-start = ((), (), s32[]{:S(2)}) async-start(), calls=%async_computation.4 | async-start | bytes 10616832 | tf_op jit(solution)/shard_map/all_gather | solution.py:165
  89.3 186.2 %all-gather.10.cloned.1.call-start = ((), (), s32[]{:S(2)}) async-start(), calls=%async_computation.5 | async-start | bytes 5308416 | tf_op jit(solution)/shard_map/all_gather | solution.py:186
  90.4 5.3 %copy-start.9 = (s32[32]{0:T(128)}, s32[32]{0:T(128)S(1)}, u32[]{:S(2)}) copy-start(s32[32]{0:T(128)S(1)} %get-tuple-element.42.req_ref) | copy-start | bytes 388
  109.0 82.5 %copy-start.2 = (bf16[256,3072]{1,0:T(8,128)(2,1)S(1)}, bf16[256,3072]{1,0:T(8,128)(2,1)}, u32[]{:S(2)}) copy-start(bf16[256,3072]{1,0:T(8,128)(2,1)} %param.8) | copy-start | bytes 4718596
  219.9 3.4 %copy-start.3 = (f32[4,8,1,512]{3,2,1,0:T(1,128)S(1)}, f32[4,8,1,512]{3,2,1,0:T(1,128)}, u32[]{:S(2)}) copy-start(f32[4,8,1,512]{3,2,1,0:T(1,128)} %get-tuple-element.26) | copy-start | bytes 196612
  219.9 3.4 %copy-start.4 = (f32[4,8,1,512]{3,2,1,0:T(1,128)S(1)}, f32[4,8,1,512]{3,2,1,0:T(1,128)}, u32[]{:S(2)}) copy-start(f32[4,8,1,512]{3,2,1,0:T(1,128)} %get-tuple-element.27) | copy-start | bytes 196612
  224.2 8.8 %all-to-all-start.1 = ((f32[8,8,2,256]{3,2,1,0:T(2,128)}), f32[8,8,2,256]{3,2,1,0:T(2,128)S(1)}, u32[]{:S(2)}, u32[]{:S(2)}) async-start(f32[8,8,2,256]{3,2,1,0:T(2,128)} %bitcast.11), calls=%async_computation.1 | async-start | bytes 262144 | tf_op jit(solution)/shard_map/all_to_all | solution.py:224
  233.0 41.5 %all-to-all-start = ((bf16[8,8,96,256]{3,2,1,0:T(8,128)(2,1)}), bf16[8,8,96,256]{3,2,1,0:T(8,128)(2,1)S(1)}, u32[]{:S(2)}, u32[]{:S(2)}) async-start(bf16[8,8,96,256]{3,2,1,0:T(8,128)(2,1)} %bitcast.10), calls=%async_computation | async-start | bytes 6291456 | tf_op jit(solution)/shard_map/all_to_all | solution.py:223
Sparse Core Ops, SparseCore 0:
  9.2 41.6 all-gather.11
  56.4 32.8 all-gather.5
  91.2 58.8 all-gather.7
  191.7 38.8 all-gather.9

commit v3 on v1

--- a/solution.py
+++ b/solution.py
@@ -140,6 +140,19 @@
     normed = (tok_float * inv_rms * gain.astype(jnp.float32)[None, :]).astype(jnp.bfloat16)
 
     w_q = lax.all_gather(w_qkv[:, 0], "wide", axis=0, tiled=True)
+    cache_ids = wide_index * cache_count + jnp.arange(cache_count, dtype=jnp.int32)
+    page_ids = jnp.arange(pages.shape[0], dtype=jnp.int32)
+    entries = jnp.sum(jnp.where(pages[None, :] == cache_ids[:, None], page_ids[None, :], 0), axis=1)
+    cache_req = entries // table_len
+    cache_base = (entries % table_len) * blk_len
+    cache_limit = lookup(lengths, cache_req)
+    cache_keys = jnp.transpose(
+        cache[:, :, 0].reshape(cache_count, blk_len, head_count, HD), (0, 2, 1, 3)
+    )
+    cache_vals = jnp.transpose(
+        cache[:, :, 1].reshape(cache_count, blk_len, head_count, HD), (0, 2, 3, 1)
+    )
+    w_q, cache_keys, cache_vals = lax.optimization_barrier((w_q, cache_keys, cache_vals))
     blk_idx = jnp.arange(blk_len, dtype=jnp.int32)
     slot_blocks = lax.dynamic_slice_in_dim(order, wide_index * slot_count, slot_count)
     slot_req = slot_blocks // per_request
@@ -165,18 +178,6 @@
     )
     q_heads = jnp.transpose(ordered, (0, 2, 1, 3))
 
-    cache_ids = wide_index * cache_count + jnp.arange(cache_count, dtype=jnp.int32)
-    page_ids = jnp.arange(pages.shape[0], dtype=jnp.int32)
-    entries = jnp.sum(jnp.where(pages[None, :] == cache_ids[:, None], page_ids[None, :], 0), axis=1)
-    cache_req = entries // table_len
-    cache_base = (entries % table_len) * blk_len
-    cache_limit = lookup(lengths, cache_req)
-    cache_keys = jnp.transpose(
-        cache[:, :, 0].reshape(cache_count, blk_len, head_count, HD), (0, 2, 1, 3)
-    )
-    cache_vals = jnp.transpose(
-        cache[:, :, 1].reshape(cache_count, blk_len, head_count, HD), (0, 2, 3, 1)
-    )
     carry = attend_blocks(
         q_heads, cache_keys, cache_vals, cache_req, cache_base, cache_limit, lengths
     )

time: 323 us -> 290 us (0.90)
  waiting for transfers between devices: 143 us -> 111 us
    all_gather x1, waiting for transfers between devices: 37.7 us -> 0.02 us  [body(): w_q = lax.all_gather(w_qkv[:, 0], 'wide', axis=0, tiled=True)]
    all_gather x1, waiting for transfers between devices: 0.02 us -> 3.54 us  [body(): w_kv = lax.all_gather(w_kv_local, 'wide', axis=0, tiled=True)]
  transfers between devices with their start and end apart: 7 -> 7, of which waited for: 5 -> 5; matrix products, arithmetic and copies ran while one was open for 30% -> 33% of each run, Pallas kernels for 15% -> 17%
where the time goes in v3:
time: 290 us; the launch traced here: 289 us
  waiting for transfers between devices  111 us (38%)
  local copies, waits for them, and re-layouts  78.1 us (27%)
  Pallas kernels  49.3 us (17%)
  matrix products  14.7 us (5%)
  other arithmetic  14.5 us (5%)
  between operations  13.4 us (5%)
  starting transfers between devices  7.59 us (3%)
    pallas_call x2, Pallas kernels, attend_blocks(): pl.pallas_call(attend_kernel(carry is not None), out_shape=out_shape, gri...  49.3 us
    slice x2, local copies, waits for them, and re-layouts, body(): cache[:, :, 1].reshape(cache_count, blk_len, head_count, HD)  41.3 us
    all_to_all x1, waiting for transfers between devices, body(): lax.all_to_all(sent_num, 'wide', split_axis=0, concat_axis=0, tiled=True)  37.3 us
    reduce_scatter x1, waiting for transfers between devices, body(): lax.psum_scatter(out_part.astype(jnp.bfloat16), 'narrow', scatter_dimensi...  34.6 us
    all_gather x1, waiting for transfers between devices, body(): all_queries = lax.all_gather(queries, 'wide', axis=0, tiled=True)  33.9 us
    another operation x2, local copies, waits for them, and re-layouts, body(): cache[:, :, 0].reshape(cache_count, blk_len, head_count, HD)  10.9 us
    reshape x2, local copies, waits for them, and re-layouts, body(): all_queries.reshape(block_total, blk_len, lane_width)[slot_of]  10.6 us
  transfers between devices with their start and end apart: 7, of which 5 were waited for; matrix products, arithmetic and copies ran while one was open for 33% of the time, Pallas kernels for 17%

profile of v3, /device:TPU:0, one launch (start us, length us, event | category | flops | bytes accessed | tf_op | source)
XLA Modules:
  0.0 288.6 jit_solution(5099031933890696540)
XLA Ops:
  6.5 2.0 slice.51
  8.6 0.7 and_select_fusion.3
  9.3 0.8 select_reduce_fusion.3
  10.3 25.7 %fusion.16 = (bf16[32,64,1,768]{3,2,1,0:T(2,128)(2,1)}, bf16[32,64,768]{2,1,0:T(8,128)(2,1)S(1)}) fusion(bf16[32,64,2,768]{3,2,1,0:T(2,128)(2,1)} %param.12), kind=kLoop, calls=%fused_computation.63 | loop fusion | bytes 12582912 | tf_op jit(solution)/shard_map/slice | solution.py:153
  36.1 5.4 %reshape_squeeze.9 = bf16[32,64,8,96]{3,2,1,0:T(8,128)(2,1)} reshape(bf16[32,64,768]{2,1,0:T(8,128)(2,1)S(1)} %get-tuple-element.40) | data formatting | bytes 6291456 | tf_op jit(solution)/shard_map/reshape;squeeze | solution.py:150
  41.5 5.5 %copy.42 = bf16[32,64,8,96]{3,1,2,0:T(8,128)(2,1)} copy(bf16[32,64,8,96]{3,2,1,0:T(8,128)(2,1)} %reshape_squeeze.9) | data formatting | bytes 6291456 | tf_op jit(solution)/shard_map/reshape;squeeze | solution.py:150
  47.0 15.5 %copy.28 = bf16[32,64,1,768]{1,3,0,2:T(8,128)(2,1)} copy(bf16[32,64,1,768]{3,2,1,0:T(2,128)(2,1)} %get-tuple-element.39) | data formatting | bytes 6291456 | tf_op jit(solution)/shard_map/slice | solution.py:153
  63.2 4.4 %fusion.7 = f32[256,768]{0,1:T(8,128)S(1)} fusion(bf16[3072,768]{1,0:T(8,128)(2,1)} %bitcast.57, bf16[256,3072]{1,0:T(8,128)(2,1)S(1)} %copy-done.1, f32[3072]{0:T(1024)S(1)} %convert_element_type.49, f32[256]{0:T(256)S(1)} %add_rsqrt_fusion), kind=kOutput, calls=%fused_computation.18 | convolution fusion | flops 1211105280 | bytes 7091200 | tf_op jit(solution)/shard_map/dot_general | solution.py:162
  67.8 0.8 pad_maximum_fusion.1
  69.3 1.1 slice.56
  70.3 33.9 %all-gather.6.cloned.1.call-done = bf16[2048,768]{0,1:T(8,128)(2,1)} async-done(((bf16[256,768]{0,1:T(8,128)(2,1)}), bf16[2048,768]{0,1:T(8,128)(2,1)}) %all-gather.6.cloned.1.call-update) | async-done | bytes 3145744 | tf_op jit(solution)/shard_map/all_gather | solution.py:168
  106.1 4.6 %copy.30 = bf16[2048,768]{1,0:T(8,128)(2,1)} copy(bf16[2048,768]{0,1:T(8,128)(2,1)} %all-gather.6.cloned.1.call-done) | data formatting | bytes 6291456 | tf_op jit(solution)/shard_map/optimization_barrier | solution.py:169
  110.7 2.7 gather_fusion
  113.4 5.4 %reshape.153 = bf16[4,512,8,96]{3,2,1,0:T(8,128)(2,1)} reshape(bf16[32,64,768]{2,1,0:T(8,128)(2,1)S(1)} %gather_fusion) | data formatting | bytes 6291456 | tf_op jit(solution)/shard_map/reshape | solution.py:176
  118.8 5.2 %copy.41 = bf16[4,512,8,96]{3,1,2,0:T(8,128)(2,1)} copy(bf16[4,512,8,96]{3,2,1,0:T(8,128)(2,1)} %reshape.153) | data formatting | bytes 6291456 | tf_op jit(solution)/shard_map/reshape | solution.py:176
  124.0 37.5 %shard_map.82 = (f32[4,8,1,512]{3,2,1,0:T(1,128)}, f32[4,8,1,512]{3,2,1,0:T(1,128)}, f32[4,8,96,512]{3,2,1,0:T(8,128)}) custom-call(s32[32]{0:T(128)} %copy-done.8, s32[32]{0:T(128)} %get-tuple-element.49.base_ref, s32[32]{0:T(128)} %select_reduce_fusion.2.limit_ref, s32[4]{0:T(128)} %len_ref.3, bf16[4,8,512,96]{3,2,1,0:T(8,128)(2,1)} %bitcast.45, ...), custom_call_target="tpu_custom_call" | custom-call | tf_op jit(solution)/shard_map/pallas_call | solution.py:114
  161.5 3.5 %all-gather.8.cloned.1.call-done = bf16[3072,2,768]{2,0,1:T(8,128)(2,1)} async-done(((bf16[384,2,768]{2,0,1:T(8,128)(2,1)}), bf16[3072,2,768]{2,0,1:T(8,128)(2,1)}) %all-gather.8.cloned.1.call-update) | async-done | bytes 9437200 | tf_op jit(solution)/shard_map/all_gather | solution.py:170
  165.1 5.4 %fusion.3 = f32[256,2,768]{2,0,1:T(8,128)S(1)} fusion(bf16[3072,2,768]{2,0,1:T(8,128)(2,1)} %all-gather.8.cloned.1.call-done, bf16[256,3072]{1,0:T(8,128)(2,1)S(1)} %copy-done.2, f32[3072]{0:T(1024)S(1)} %convert_element_type.49, f32[256]{0:T(256)S(1)} %add_rsqrt_fusion), kind=kOutput, calls=%fused_computation.12 | convolution fusion | flops 2419064832 | bytes 12596224 | tf_op jit(solution)/shard_map/tk,kcj->tcj/dot_general | solution.py:187
  172.6 1.3 copy.35
  173.9 1.1 maximum_bitcast_fusion.refs_1_
  175.4 11.8 %shard_map.83 = (f32[4,8,1,512]{3,2,1,0:T(1,128)}, f32[4,8,1,512]{3,2,1,0:T(1,128)}, f32[4,8,96,512]{3,2,1,0:T(8,128)}) custom-call(s32[4]{0:T(128)} %copy-done.6, s32[4]{0:T(128)} %copy-done.5, s32[4]{0:T(128)} %broadcast_13_limit_ref.2.limit_ref, s32[4]{0:T(128)} %len_ref.3, bf16[4,8,512,96]{3,2,1,0:T(8,128)(2,1)} %bitcast.46, ...), custom_call_target="tpu_custom_call" | custom-call | tf_op jit(solution)/shard_map/pallas_call | solution.py:114
  187.3 0.8 fusion.10
  188.1 1.5 fusion.9
  189.7 3.4 %all-to-all-start.1 = ((f32[8,8,2,256]{3,2,1,0:T(2,128)}), f32[8,8,2,256]{3,2,1,0:T(2,128)S(1)}, u32[]{:S(2)}, u32[]{:S(2)}) async-start(f32[8,8,2,256]{3,2,1,0:T(2,128)} %bitcast.15), calls=%async_computation.1 | async-start | bytes 262144 | tf_op jit(solution)/shard_map/all_to_all | solution.py:220
  193.0 3.3 %convert.28 = bf16[4,8,96,512]{3,2,1,0:T(8,128)(2,1)S(1)} convert(f32[4,8,96,512]{3,2,1,0:T(8,128)} %get-tuple-element.31) | non-fusion elementwise | flops 1572864 | bytes 9437184 | tf_op jit(solution)/shard_map/convert.3
  196.7 1.9 pad_maximum_fusion
  198.7 1.6 all-to-all-done.1
  200.2 3.6 %all-to-all-start = ((bf16[8,8,96,256]{3,2,1,0:T(8,128)(2,1)}), bf16[8,8,96,256]{3,2,1,0:T(8,128)(2,1)S(1)}, u32[]{:S(2)}, u32[]{:S(2)}) async-start(bf16[8,8,96,256]{3,2,1,0:T(8,128)(2,1)} %bitcast.14), calls=%async_computation | async-start | bytes 6291456 | tf_op jit(solution)/shard_map/all_to_all | solution.py:219
  204.4 37.3 %all-to-all-done = bf16[8,8,96,256]{3,2,1,0:T(8,128)(2,1)S(1)} async-done(((bf16[8,8,96,256]{3,2,1,0:T(8,128)(2,1)}), bf16[8,8,96,256]{3,2,1,0:T(8,128)(2,1)S(1)}, u32[]{:S(2)}, u32[]{:S(2)}) %all-to-all-start) | async-done | bytes 3145760 | tf_op jit(solution)/shard_map/all_to_all | solution.py:219
  241.7 0.7 multiply_reduce_fusion
  242.6 4.9 %convolution_convert_fusion = bf16[256,3072]{1,0:T(8,128)(2,1)} fusion(bf16[256,768]{0,1:T(8,128)(2,1)S(1)} %bitcast.54, bf16[3072,768]{1,0:T(8,128)(2,1)} %all-gather.10.cloned.1.call-done), kind=kOutput, calls=%fused_computation.7 | convolution fusion | flops 1208745984 | bytes 6684672 | tf_op jit(solution)/shard_map/dot_general | solution.py:231
  247.5 34.6 %reduce-scatter.2.cloned.1.call-done = bf16[256,768]{1,0:T(8,128)(2,1)} async-done(((bf16[256,3072]{1,0:T(8,128)(2,1)}), bf16[256,768]{1,0:T(8,128)(2,1)}) %reduce-scatter.2.cloned.1.call-update) | async-done | bytes 393232 | tf_op jit(solution)/shard_map/reduce_scatter | solution.py:234
  (63 shorter events, 7.2 us)
Async XLA Ops:
  6.5 56.7 %all-gather.12.cloned.1.call-start = ((), (), s32[]{:S(2)}) async-start(), calls=%async_computation.7 | async-start | bytes 5308416 | tf_op jit(solution)/shard_map/all_gather | solution.py:142
  8.5 95.7 %all-gather.6.cloned.1.call-start = ((), (), s32[]{:S(2)}) async-start(), calls=%async_computation.3 | async-start | bytes 3538944 | tf_op jit(solution)/shard_map/all_gather | solution.py:168
  9.3 26.8 %copy-start.6 = (s32[4]{0:T(128)}, s32[4]{0:T(128)S(1)}, u32[]{:S(2)}) copy-start(s32[4]{0:T(128)S(1)} %get-tuple-element.37.req_ref) | copy-start | bytes 52
  10.2 25.9 %copy-start.5 = (s32[4]{0:T(128)}, s32[4]{0:T(128)S(1)}, u32[]{:S(2)}) copy-start(s32[4]{0:T(128)S(1)} %fusion.13.base_ref) | copy-start | bytes 52
  47.0 15.5 %copy-start.3 = (bf16[3072]{0:T(1024)(128)(2,1)S(1)}, bf16[3072]{0:T(1024)(128)(2,1)}, u32[]{:S(2)}) copy-start(bf16[3072]{0:T(1024)(128)(2,1)} %param.9) | copy-start | bytes 18436
  47.0 15.6 %copy-start.1 = (bf16[256,3072]{1,0:T(8,128)(2,1)S(1)}, bf16[256,3072]{1,0:T(8,128)(2,1)}, u32[]{:S(2)}) copy-start(bf16[256,3072]{1,0:T(8,128)(2,1)} %param.8) | copy-start | bytes 4718596
  67.6 1.6 copy-start
  67.7 36.9 %copy-start.9 = (s32[32]{0:T(128)S(1)}, s32[32]{0:T(128)}, u32[]{:S(2)}) copy-start(s32[32]{0:T(128)} %param.14) | copy-start | bytes 388
  67.7 37.0 %copy-start.7 = (s32[256]{0:T(256)S(1)}, s32[256]{0:T(256)}, u32[]{:S(2)}) copy-start(s32[256]{0:T(256)} %param.15) | copy-start | bytes 3076
  67.7 37.8 %copy-start.4 = (s32[4]{0:T(128)S(1)}, s32[4]{0:T(128)}, u32[]{:S(2)}) copy-start(s32[4]{0:T(128)} %len_ref.3) | copy-start | bytes 52
  68.6 96.4 %all-gather.8.cloned.1.call-start = ((), (), s32[]{:S(2)}) async-start(), calls=%async_computation.4 | async-start | bytes 10616832 | tf_op jit(solution)/shard_map/all_gather | solution.py:170
  104.3 138.3 %all-gather.10.cloned.1.call-start = ((), (), s32[]{:S(2)}) async-start(), calls=%async_computation.5 | async-start | bytes 5308416 | tf_op jit(solution)/shard_map/all_gather | solution.py:185
  105.5 5.3 %copy-start.8 = (s32[32]{0:T(128)}, s32[32]{0:T(128)S(1)}, u32[]{:S(2)}) copy-start(s32[32]{0:T(128)S(1)} %get-tuple-element.50.req_ref) | copy-start | bytes 388
  124.0 41.0 %copy-start.2 = (bf16[256,3072]{1,0:T(8,128)(2,1)S(1)}, bf16[256,3072]{1,0:T(8,128)(2,1)}, u32[]{:S(2)}) copy-start(bf16[256,3072]{1,0:T(8,128)(2,1)} %param.8) | copy-start | bytes 4718596
  189.7 10.6 %all-to-all-start.1 = ((f32[8,8,2,256]{3,2,1,0:T(2,128)}), f32[8,8,2,256]{3,2,1,0:T(2,128)S(1)}, u32[]{:S(2)}, u32[]{:S(2)}) async-start(f32[8,8,2,256]{3,2,1,0:T(2,128)} %bitcast.15), calls=%async_computation.1 | async-start | bytes 262144 | tf_op jit(solution)/shard_map/all_to_all | solution.py:220
  200.2 41.5 %all-to-all-start = ((bf16[8,8,96,256]{3,2,1,0:T(8,128)(2,1)}), bf16[8,8,96,256]{3,2,1,0:T(8,128)(2,1)S(1)}, u32[]{:S(2)}, u32[]{:S(2)}) async-start(bf16[8,8,96,256]{3,2,1,0:T(8,128)(2,1)} %bitcast.14), calls=%async_computation | async-start | bytes 6291456 | tf_op jit(solution)/shard_map/all_to_all | solution.py:219
  203.9 78.2 %reduce-scatter.2.cloned.1.call-start = ((), (), s32[]{:S(2)}) async-start(), calls=%async_computation.6 | async-start | bytes 1966080 | tf_op jit(solution)/shard_map/reduce_scatter | solution.py:234
Sparse Core Ops, SparseCore 0:
  9.2 41.6 all-gather.11
  68.7 35.4 all-gather.5
  106.2 58.8 all-gather.7
  166.8 40.3 all-gather.9
  247.6 34.4 reduce-scatter.1

commit v4 on v3

--- a/solution.py
+++ b/solution.py
@@ -35,7 +35,7 @@
 
 
 def attend_kernel(carry_in):
-    def kernel(req_ref, base_ref, limit_ref, len_ref, *refs):
+    def kernel(req_ref, base_ref, limit_ref, len_ref, slot_ref, *refs):
         if carry_in:
             q_ref, k_ref, v_ref, m0_ref, l0_ref, o0_ref, m_ref, l_ref, o_ref = refs
         else:
@@ -57,7 +57,10 @@
         base = base_ref[step]
         limit = limit_ref[step]
         qlen = len_ref[req]
-        queries = q_ref[req]
+        per_request = slot_ref.shape[0] // len_ref.shape[0]
+        queries = jnp.concatenate(
+            [q_ref[:, slot_ref[req * per_request + i]] for i in range(per_request)], axis=1
+        )
         keys = k_ref[0]
         vals = v_ref[0]
         blk_len = keys.shape[1]
@@ -86,9 +89,13 @@
     return kernel
 
 
-def attend_blocks(queries, keys, vals_t, blk_req, blk_base, blk_limit, lengths, carry=None):
-    req_count, head_count, q_len, head_dim = queries.shape
-    blk_count, _, blk_len, _ = keys.shape
+def attend_blocks(
+    queries, keys, vals_t, blk_req, blk_base, blk_limit, lengths, slot_of, carry=None
+):
+    head_count, _, blk_len, head_dim = queries.shape
+    req_count = lengths.shape[0]
+    q_len = slot_of.shape[0] // req_count * blk_len
+    blk_count = keys.shape[0]
     vmem = pltpu.MemorySpace.VMEM
     whole = pl.BlockSpec(memory_space=vmem)
     in_specs = [
@@ -106,7 +113,7 @@
         jax.ShapeDtypeStruct((req_count, head_count, head_dim, q_len), jnp.float32),
     )
     grid_spec = pltpu.PrefetchScalarGridSpec(
-        num_scalar_prefetch=4,
+        num_scalar_prefetch=5,
         grid=(blk_count,),
         in_specs=in_specs,
         out_specs=(whole, whole, whole),
@@ -118,7 +125,7 @@
         compiler_params=pltpu.CompilerParams(
             dimension_semantics=("arbitrary",)
         ),
-    )(blk_req, blk_base, blk_limit, lengths, *args)
+    )(blk_req, blk_base, blk_limit, lengths, slot_of, *args)
 
 
 def body(tokens, gain, w_qkv, w_out, cache, lengths, order, pages):
@@ -149,10 +156,7 @@
     cache_keys = jnp.transpose(
         cache[:, :, 0].reshape(cache_count, blk_len, head_count, HD), (0, 2, 1, 3)
     )
-    cache_vals = jnp.transpose(
-        cache[:, :, 1].reshape(cache_count, blk_len, head_count, HD), (0, 2, 3, 1)
-    )
-    w_q, cache_keys, cache_vals = lax.optimization_barrier((w_q, cache_keys, cache_vals))
+    w_q, cache_keys = lax.optimization_barrier((w_q, cache_keys))
     blk_idx = jnp.arange(blk_len, dtype=jnp.int32)
     slot_blocks = lax.dynamic_slice_in_dim(order, wide_index * slot_count, slot_count)
     slot_req = slot_blocks // per_request
@@ -160,26 +164,30 @@
     slot_pos = slot_start[:, None] + blk_idx[None, :]
     positions = slot_pos.reshape(tok_rows)
     q_proj = jnp.dot(normed, w_q, preferred_element_type=jnp.float32)
-    queries = (
+    queries = jnp.transpose(
         rotate(q_proj.reshape(tok_rows, head_count, HD), positions)
         .astype(jnp.bfloat16)
-        .reshape(tok_rows, lane_width)
-    )
-    all_queries = lax.all_gather(queries, "wide", axis=0, tiled=True)
-    all_queries, w_kv_local = lax.optimization_barrier((all_queries, w_qkv[:, 1:]))
+        .reshape(slot_count, blk_len, head_count, HD),
+        (2, 0, 1, 3),
+    )
+    all_queries = lax.all_gather(queries, "wide", axis=1, tiled=True)
+    queries, cache_v = lax.optimization_barrier((queries, cache))
+    cache_vals = jnp.transpose(
+        cache_v[:, :, 1].reshape(cache_count, blk_len, head_count, HD), (0, 2, 3, 1)
+    )
+    all_queries, cache_vals, w_kv_local = lax.optimization_barrier(
+        (all_queries, cache_vals, w_qkv[:, 1:])
+    )
     w_kv = lax.all_gather(w_kv_local, "wide", axis=0, tiled=True)
 
     block_ids = jnp.arange(block_total, dtype=jnp.int32)
     slot_of = jnp.sum(
         jnp.where(order[None, :] == block_ids[:, None], block_ids[None, :], 0), axis=1
     )
-    ordered = all_queries.reshape(block_total, blk_len, lane_width)[slot_of].reshape(
-        req_count, fresh_len, head_count, HD
-    )
-    q_heads = jnp.transpose(ordered, (0, 2, 1, 3))
+    q_heads = all_queries
 
     carry = attend_blocks(
-        q_heads, cache_keys, cache_vals, cache_req, cache_base, cache_limit, lengths
+        q_heads, cache_keys, cache_vals, cache_req, cache_base, cache_limit, lengths, slot_of
     )
     carry, w_out_local = lax.optimization_barrier((carry, w_out))
     part_out = lax.all_gather(w_out_local, "wide", axis=0, tiled=True)
@@ -200,6 +208,7 @@
         slot_start,
         new_limit,
         lengths,
+        slot_of,
         carry=carry,
     )
 

time: 290 us -> 280 us (0.966)
  local copies, waits for them, and re-layouts: 78.1 us -> 61.9 us
  waiting for transfers between devices: 111 us -> 116 us
    all_gather x1, waiting for transfers between devices: 33.9 us -> 11.3 us  [body(): all_queries = lax.all_gather(queries, 'wide', axis=1, tiled=True)]
    all_gather x1, waiting for transfers between devices: 3.54 us -> 20.5 us  [body(): w_kv = lax.all_gather(w_kv_local, 'wide', axis=0, tiled=True)]
    reshape x2 -> x0, local copies, waits for them, and re-layouts: 10.6 us -> none  [body(): all_queries.reshape(block_total, blk_len, lane_width)[slot_of]]
    all_gather x1, waiting for transfers between devices: 0.02 us -> 10.3 us  [body(): w_q = lax.all_gather(w_qkv[:, 0], 'wide', axis=0, tiled=True)]
    optimization_barrier x1 -> x0, local copies, waits for them, and re-layouts: 4.63 us -> none  [body(): lax.optimization_barrier((all_queries, w_qkv[:, 1:]))]
    slice x2 -> x3, local copies, waits for them, and re-layouts: 41.3 us -> 42.9 us  [the longest x2 24.4 us: body(): cache_v[:, :, 1].reshape(cache_count, blk_len, head_count, HD)]
  transfers between devices with their start and end apart: 7 -> 7, of which waited for: 5 -> 6; matrix products, arithmetic and copies ran while one was open for 33% -> 28% of each run, Pallas kernels for 17% -> 18%
where the time goes in v4:
time: 280 us; the launch traced here: 278 us
  waiting for transfers between devices  116 us (41%)
  local copies, waits for them, and re-layouts  61.9 us (22%)
  Pallas kernels  49.9 us (18%)
  other arithmetic  15.4 us (6%)
  matrix products  14.7 us (5%)
  between operations  13.4 us (5%)
  starting transfers between devices  7.37 us (3%)
    pallas_call x2, Pallas kernels, attend_blocks(): pl.pallas_call(attend_kernel(carry is not None), out_shape=out_shape, gri...  49.9 us
    all_to_all x1, waiting for transfers between devices, body(): lax.all_to_all(sent_num, 'wide', split_axis=0, concat_axis=0, tiled=True)  37.5 us
    reduce_scatter x1, waiting for transfers between devices, body(): lax.psum_scatter(out_part.astype(jnp.bfloat16), 'narrow', scatter_dimensi...  34.6 us
    slice x2, local copies, waits for them, and re-layouts, body(): cache_v[:, :, 1].reshape(cache_count, blk_len, head_count, HD)  24.4 us
    all_gather x1, waiting for transfers between devices, body(): w_kv = lax.all_gather(w_kv_local, 'wide', axis=0, tiled=True)  20.5 us
    slice x1, local copies, waits for them, and re-layouts, body(): cache[:, :, 0].reshape(cache_count, blk_len, head_count, HD)  18.4 us
    all_gather x1, waiting for transfers between devices, body(): all_queries = lax.all_gather(queries, 'wide', axis=1, tiled=True)  11.3 us
    another operation x2, local copies, waits for them, and re-layouts, body(): cache[:, :, 0].reshape(cache_count, blk_len, head_count, HD)  11.1 us
  transfers between devices with their start and end apart: 7, of which 6 were waited for; matrix products, arithmetic and copies ran while one was open for 28% of the time, Pallas kernels for 18%

profile of v4, /device:TPU:0, one launch (start us, length us, event | category | flops | bytes accessed | tf_op | source)
XLA Modules:
  0.0 278.4 jit_solution(5179934475142423295)
XLA Ops:
  6.5 2.0 slice.51
  8.6 0.7 and_select_fusion.3
  9.3 0.8 select_reduce_fusion.3
  10.3 18.4 %slice_reduce_fusion = bf16[32,64,768]{2,1,0:T(8,128)(2,1)S(1)} fusion(bf16[32,64,2,768]{3,2,1,0:T(2,128)(2,1)} %param.12), kind=kLoop, calls=%fused_computation.1 | loop fusion | bytes 6291456 | tf_op jit(solution)/shard_map/slice | solution.py:157
  28.8 5.5 %reshape_squeeze.9 = bf16[32,64,8,96]{3,2,1,0:T(8,128)(2,1)} reshape(bf16[32,64,768]{2,1,0:T(8,128)(2,1)S(1)} %slice_reduce_fusion) | data formatting | bytes 6291456 | tf_op jit(solution)/shard_map/reshape;squeeze | solution.py:157
  34.3 5.6 %copy.36 = bf16[32,64,8,96]{3,1,2,0:T(8,128)(2,1)} copy(bf16[32,64,8,96]{3,2,1,0:T(8,128)(2,1)} %reshape_squeeze.9) | data formatting | bytes 6291456 | tf_op jit(solution)/shard_map/reshape;squeeze | solution.py:157
  40.6 10.3 %all-gather.12.cloned.1.call-done = bf16[3072,1,768]{2,0,1:T(8,128)(2,1)} async-done(((bf16[384,1,768]{2,0,1:T(8,128)(2,1)}), bf16[3072,1,768]{2,0,1:T(8,128)(2,1)}) %all-gather.12.cloned.1.call-update) | async-done | bytes 4718608 | tf_op jit(solution)/shard_map/all_gather | solution.py:149
  50.9 4.4 %fusion.7 = f32[256,768]{0,1:T(8,128)S(1)} fusion(bf16[3072,768]{1,0:T(8,128)(2,1)} %bitcast.50, bf16[256,3072]{1,0:T(8,128)(2,1)S(1)} %copy-done.1, f32[3072]{0:T(1024)S(1)} %convert_element_type.46, f32[256]{0:T(256)S(1)} %add_rsqrt_fusion), kind=kOutput, calls=%fused_computation.17 | convolution fusion | flops 1211105280 | bytes 7091200 | tf_op jit(solution)/shard_map/dot_general | solution.py:166
  56.0 1.1 maximum_bitcast_fusion
  57.2 1.1 slice.56
  58.3 8.9 %slice.55 = bf16[32,64,1,768]{3,2,1,0:T(2,128)(2,1)} slice(bf16[32,64,2,768]{3,2,1,0:T(2,128)(2,1)} %param.12), slice={[0:32], [0:64], [1:2], [0:768]} | slice | bytes 6291456 | tf_op jit(solution)/shard_map/slice | solution.py:176
  67.2 15.5 %copy.27 = bf16[32,64,1,768]{1,3,0,2:T(8,128)(2,1)} copy(bf16[32,64,1,768]{3,2,1,0:T(2,128)(2,1)} %slice.55) | data formatting | bytes 6291456 | tf_op jit(solution)/shard_map/slice | solution.py:176
  82.7 11.3 %all-gather.6.cloned.1.call-done.refs_0_ = bf16[8,32,64,96]{3,2,1,0:T(8,128)(2,1)} async-done(((bf16[8,4,64,96]{3,2,1,0:T(8,128)(2,1)}), bf16[8,32,64,96]{3,2,1,0:T(8,128)(2,1)}) %all-gather.6.cloned.1.call-update) | async-done | bytes 3145744 | tf_op jit(solution)/shard_map/all_gather | solution.py:173
  94.3 0.6 select_reduce_fusion.1.slot_ref
  95.7 0.6 select_reduce_fusion.2.limit_ref
  96.3 37.9 %shard_map.82 = (f32[4,8,1,512]{3,2,1,0:T(1,128)}, f32[4,8,1,512]{3,2,1,0:T(1,128)}, f32[4,8,96,512]{3,2,1,0:T(8,128)}) custom-call(s32[32]{0:T(128)} %copy-done.8, s32[32]{0:T(128)} %get-tuple-element.49.base_ref, s32[32]{0:T(128)} %select_reduce_fusion.2.limit_ref, s32[4]{0:T(128)} %len_ref.3, s32[32]{0:T(128)} %select_reduce_fusion.1.slot_ref, ...), custom_call_target="tpu_custom_call" | custom-call | tf_op jit(solution)/shard_map/pallas_call | solution.py:121
  134.3 20.5 %all-gather.8.cloned.1.call-done = bf16[3072,2,768]{2,0,1:T(8,128)(2,1)} async-done(((bf16[384,2,768]{2,0,1:T(8,128)(2,1)}), bf16[3072,2,768]{2,0,1:T(8,128)(2,1)}) %all-gather.8.cloned.1.call-update) | async-done | bytes 9437200 | tf_op jit(solution)/shard_map/all_gather | solution.py:181
  154.8 5.4 %fusion.3 = f32[256,2,768]{2,0,1:T(8,128)S(1)} fusion(bf16[3072,2,768]{2,0,1:T(8,128)(2,1)} %all-gather.8.cloned.1.call-done, bf16[256,3072]{1,0:T(8,128)(2,1)S(1)} %copy-done.2, f32[3072]{0:T(1024)S(1)} %convert_element_type.46, f32[256]{0:T(256)S(1)} %add_rsqrt_fusion), kind=kOutput, calls=%fused_computation.10 | convolution fusion | flops 2419064832 | bytes 12596224 | tf_op jit(solution)/shard_map/tk,kcj->tcj/dot_general | solution.py:195
  162.3 1.2 copy.31
  163.6 1.1 maximum_bitcast_fusion.1.refs_1_
  165.2 11.9 %shard_map.83 = (f32[4,8,1,512]{3,2,1,0:T(1,128)}, f32[4,8,1,512]{3,2,1,0:T(1,128)}, f32[4,8,96,512]{3,2,1,0:T(8,128)}) custom-call(s32[4]{0:T(128)} %copy-done.6, s32[4]{0:T(128)} %copy-done.5, s32[4]{0:T(128)} %broadcast_13_limit_ref.2.limit_ref, s32[4]{0:T(128)} %len_ref.3, s32[32]{0:T(128)} %select_reduce_fusion.1.slot_ref, ...), custom_call_target="tpu_custom_call" | custom-call | tf_op jit(solution)/shard_map/pallas_call | solution.py:121
  177.1 0.8 fusion.10
  178.0 1.5 fusion.9
  179.5 3.4 %all-to-all-start.1 = ((f32[8,8,2,256]{3,2,1,0:T(2,128)}), f32[8,8,2,256]{3,2,1,0:T(2,128)S(1)}, u32[]{:S(2)}, u32[]{:S(2)}) async-start(f32[8,8,2,256]{3,2,1,0:T(2,128)} %bitcast.13), calls=%async_computation.1 | async-start | bytes 262144 | tf_op jit(solution)/shard_map/all_to_all | solution.py:229
  182.9 3.3 %convert.30 = bf16[4,8,96,512]{3,2,1,0:T(8,128)(2,1)S(1)} convert(f32[4,8,96,512]{3,2,1,0:T(8,128)} %get-tuple-element.33) | non-fusion elementwise | flops 1572864 | bytes 9437184 | tf_op jit(solution)/shard_map/convert.3
  186.6 1.9 pad_maximum_fusion
  188.5 1.6 all-to-all-done.1
  190.1 3.6 %all-to-all-start = ((bf16[8,8,96,256]{3,2,1,0:T(8,128)(2,1)}), bf16[8,8,96,256]{3,2,1,0:T(8,128)(2,1)S(1)}, u32[]{:S(2)}, u32[]{:S(2)}) async-start(bf16[8,8,96,256]{3,2,1,0:T(8,128)(2,1)} %bitcast.12), calls=%async_computation | async-start | bytes 6291456 | tf_op jit(solution)/shard_map/all_to_all | solution.py:228
  194.0 37.5 %all-to-all-done = bf16[8,8,96,256]{3,2,1,0:T(8,128)(2,1)S(1)} async-done(((bf16[8,8,96,256]{3,2,1,0:T(8,128)(2,1)}), bf16[8,8,96,256]{3,2,1,0:T(8,128)(2,1)S(1)}, u32[]{:S(2)}, u32[]{:S(2)}) %all-to-all-start) | async-done | bytes 3145760 | tf_op jit(solution)/shard_map/all_to_all | solution.py:228
  231.5 0.7 multiply_reduce_fusion
  232.4 4.9 %convolution_convert_fusion = bf16[256,3072]{1,0:T(8,128)(2,1)} fusion(bf16[256,768]{0,1:T(8,128)(2,1)S(1)} %bitcast.47, bf16[3072,768]{1,0:T(8,128)(2,1)} %all-gather.10.cloned.1.call-done), kind=kOutput, calls=%fused_computation.5 | convolution fusion | flops 1208745984 | bytes 6684672 | tf_op jit(solution)/shard_map/dot_general | solution.py:240
  237.3 34.6 %reduce-scatter.2.cloned.1.call-done = bf16[256,768]{1,0:T(8,128)(2,1)} async-done(((bf16[256,3072]{1,0:T(8,128)(2,1)}), bf16[256,768]{1,0:T(8,128)(2,1)}) %reduce-scatter.2.cloned.1.call-update) | async-done | bytes 393232 | tf_op jit(solution)/shard_map/reduce_scatter | solution.py:243
  (60 shorter events, 6.2 us)
Async XLA Ops:
  6.5 44.4 %all-gather.12.cloned.1.call-start = ((), (), s32[]{:S(2)}) async-start(), calls=%async_computation.7 | async-start | bytes 5308416 | tf_op jit(solution)/shard_map/all_gather | solution.py:149
  8.5 85.5 %all-gather.6.cloned.1.call-start = ((), (), s32[]{:S(2)}) async-start(), calls=%async_computation.3 | async-start | bytes 4718592 | tf_op jit(solution)/shard_map/all_gather | solution.py:173
  9.3 19.5 %copy-start.6 = (s32[4]{0:T(128)}, s32[4]{0:T(128)S(1)}, u32[]{:S(2)}) copy-start(s32[4]{0:T(128)S(1)} %get-tuple-element.39.req_ref) | copy-start | bytes 52
  10.2 18.6 %copy-start.5 = (s32[4]{0:T(128)}, s32[4]{0:T(128)S(1)}, u32[]{:S(2)}) copy-start(s32[4]{0:T(128)S(1)} %fusion.13.base_ref) | copy-start | bytes 52
  34.3 5.6 %copy-start.3 = (bf16[3072]{0:T(1024)(128)(2,1)S(1)}, bf16[3072]{0:T(1024)(128)(2,1)}, u32[]{:S(2)}) copy-start(bf16[3072]{0:T(1024)(128)(2,1)} %param.9) | copy-start | bytes 18436
  34.3 5.6 %copy-start.1 = (bf16[256,3072]{1,0:T(8,128)(2,1)S(1)}, bf16[256,3072]{1,0:T(8,128)(2,1)}, u32[]{:S(2)}) copy-start(bf16[256,3072]{1,0:T(8,128)(2,1)} %param.8) | copy-start | bytes 4718596
  55.3 1.9 copy-start
  57.1 97.6 %all-gather.8.cloned.1.call-start = ((), (), s32[]{:S(2)}) async-start(), calls=%async_computation.4 | async-start | bytes 10616832 | tf_op jit(solution)/shard_map/all_gather | solution.py:181
  67.2 27.1 %copy-start.9 = (s32[32]{0:T(128)S(1)}, s32[32]{0:T(128)}, u32[]{:S(2)}) copy-start(s32[32]{0:T(128)} %param.14) | copy-start | bytes 388
  67.2 27.8 %copy-start.7 = (s32[256]{0:T(256)S(1)}, s32[256]{0:T(256)}, u32[]{:S(2)}) copy-start(s32[256]{0:T(256)} %param.15) | copy-start | bytes 3076
  67.2 28.5 %copy-start.4 = (s32[4]{0:T(128)S(1)}, s32[4]{0:T(128)}, u32[]{:S(2)}) copy-start(s32[4]{0:T(128)} %len_ref.3) | copy-start | bytes 52
  94.0 138.4 %all-gather.10.cloned.1.call-start = ((), (), s32[]{:S(2)}) async-start(), calls=%async_computation.5 | async-start | bytes 5308416 | tf_op jit(solution)/shard_map/all_gather | solution.py:193
  95.7 0.6 copy-start.8
  96.3 58.4 %copy-start.2 = (bf16[256,3072]{1,0:T(8,128)(2,1)S(1)}, bf16[256,3072]{1,0:T(8,128)(2,1)}, u32[]{:S(2)}) copy-start(bf16[256,3072]{1,0:T(8,128)(2,1)} %param.8) | copy-start | bytes 4718596
  179.5 10.6 %all-to-all-start.1 = ((f32[8,8,2,256]{3,2,1,0:T(2,128)}), f32[8,8,2,256]{3,2,1,0:T(2,128)S(1)}, u32[]{:S(2)}, u32[]{:S(2)}) async-start(f32[8,8,2,256]{3,2,1,0:T(2,128)} %bitcast.13), calls=%async_computation.1 | async-start | bytes 262144 | tf_op jit(solution)/shard_map/all_to_all | solution.py:229
  190.1 41.5 %all-to-all-start = ((bf16[8,8,96,256]{3,2,1,0:T(8,128)(2,1)}), bf16[8,8,96,256]{3,2,1,0:T(8,128)(2,1)S(1)}, u32[]{:S(2)}, u32[]{:S(2)}) async-start(bf16[8,8,96,256]{3,2,1,0:T(8,128)(2,1)} %bitcast.12), calls=%async_computation | async-start | bytes 6291456 | tf_op jit(solution)/shard_map/all_to_all | solution.py:228
  193.7 78.2 %reduce-scatter.2.cloned.1.call-start = ((), (), s32[]{:S(2)}) async-start(), calls=%async_computation.6 | async-start | bytes 1966080 | tf_op jit(solution)/shard_map/reduce_scatter | solution.py:243
Sparse Core Ops, SparseCore 0:
  9.2 41.6 all-gather.11
  57.2 36.7 all-gather.5
  95.9 58.8 all-gather.7
  156.5 40.3 all-gather.9
  237.5 34.4 reduce-scatter.1

commit v5 on v4

--- a/solution.py
+++ b/solution.py
@@ -34,79 +34,92 @@
     return jnp.sum(jnp.where(matches, small_table, 0), axis=-1)
 
 
-def attend_kernel(carry_in):
+def block_step(step, scalars, q_ref, k_ref, v_ref, m_ref, l_ref, o_ref):
+    req_ref, base_ref, limit_ref, len_ref, slot_ref = scalars
+    req = req_ref[step]
+    base = base_ref[step]
+    limit = limit_ref[step]
+    qlen = len_ref[req]
+    per_request = slot_ref.shape[0] // len_ref.shape[0]
+    queries = jnp.concatenate(
+        [q_ref[:, slot_ref[req * per_request + i]] for i in range(per_request)], axis=1
+    )
+    keys = k_ref[0]
+    vals = v_ref[0]
+    blk_len = keys.shape[1]
+    q_len = queries.shape[1]
+    scale = keys.shape[-1] ** (-0.5)
+    scores = (
+        jnp.einsum("hkd,hqd->hkq", keys, queries, preferred_element_type=jnp.float32)
+        * scale
+    )
+    key_pos = base + lax.broadcasted_iota(jnp.int32, (blk_len, q_len), 0)
+    query_pos = qlen + lax.broadcasted_iota(jnp.int32, (blk_len, q_len), 1)
+    allowed = ((key_pos < limit) & (key_pos <= query_pos))[None]
+    masked = jnp.where(allowed, scores, negative)
+    m_old = m_ref[req]
+    m_new = jnp.maximum(m_old, jnp.max(masked, axis=1, keepdims=True))
+    exp_terms = jnp.where(allowed, jnp.exp(masked - m_new), 0.0)
+    alpha = jnp.exp(m_old - m_new)
+    l_ref[req] = alpha * l_ref[req] + jnp.sum(exp_terms, axis=1, keepdims=True)
+    weighted = jnp.einsum(
+        "hdk,hkq->hdq", vals, exp_terms.astype(jnp.bfloat16),
+        preferred_element_type=jnp.float32,
+    )
+    o_ref[req] = alpha * o_ref[req] + weighted
+    m_ref[req] = m_new
+
+
+def attend_kernel(cache_count):
     def kernel(req_ref, base_ref, limit_ref, len_ref, slot_ref, *refs):
-        if carry_in:
-            q_ref, k_ref, v_ref, m0_ref, l0_ref, o0_ref, m_ref, l_ref, o_ref = refs
-        else:
-            q_ref, k_ref, v_ref, m_ref, l_ref, o_ref = refs
+        q_ref, kc_ref, vc_ref, kn_ref, vn_ref, m_ref, l_ref, o_ref = refs
+        scalars = (req_ref, base_ref, limit_ref, len_ref, slot_ref)
         step = pl.program_id(0)
 
         @pl.when(step == 0)
         def _():
-            if carry_in:
-                m_ref[...] = m0_ref[...]
-                l_ref[...] = l0_ref[...]
-                o_ref[...] = o0_ref[...]
-            else:
-                m_ref[...] = jnp.full(m_ref.shape, negative, jnp.float32)
-                l_ref[...] = jnp.zeros(l_ref.shape, jnp.float32)
-                o_ref[...] = jnp.zeros(o_ref.shape, jnp.float32)
-
-        req = req_ref[step]
-        base = base_ref[step]
-        limit = limit_ref[step]
-        qlen = len_ref[req]
-        per_request = slot_ref.shape[0] // len_ref.shape[0]
-        queries = jnp.concatenate(
-            [q_ref[:, slot_ref[req * per_request + i]] for i in range(per_request)], axis=1
-        )
-        keys = k_ref[0]
-        vals = v_ref[0]
-        blk_len = keys.shape[1]
-        q_len = queries.shape[1]
-        scale = keys.shape[-1] ** (-0.5)
-        scores = (
-            jnp.einsum("hkd,hqd->hkq", keys, queries, preferred_element_type=jnp.float32)
-            * scale
-        )
-        key_pos = base + lax.broadcasted_iota(jnp.int32, (blk_len, q_len), 0)
-        query_pos = qlen + lax.broadcasted_iota(jnp.int32, (blk_len, q_len), 1)
-        allowed = ((key_pos < limit) & (key_pos <= query_pos))[None]
-        masked = jnp.where(allowed, scores, negative)
-        m_old = m_ref[req]
-        m_new = jnp.maximum(m_old, jnp.max(masked, axis=1, keepdims=True))
-        exp_terms = jnp.where(allowed, jnp.exp(masked - m_new), 0.0)
-        alpha = jnp.exp(m_old - m_new)
-        l_ref[req] = alpha * l_ref[req] + jnp.sum(exp_terms, axis=1, keepdims=True)
-        weighted = jnp.einsum(
-            "hdk,hkq->hdq", vals, exp_terms.astype(jnp.bfloat16),
-            preferred_element_type=jnp.float32,
-        )
-        o_ref[req] = alpha * o_ref[req] + weighted
-        m_ref[req] = m_new
+            m_ref[...] = jnp.full(m_ref.shape, negative, jnp.float32)
+            l_ref[...] = jnp.zeros(l_ref.shape, jnp.float32)
+            o_ref[...] = jnp.zeros(o_ref.shape, jnp.float32)
+
+        @pl.when(step < cache_count)
+        def _():
+            block_step(step, scalars, q_ref, kc_ref, vc_ref, m_ref, l_ref, o_ref)
+
+        @pl.when(step >= cache_count)
+        def _():
+            block_step(step, scalars, q_ref, kn_ref, vn_ref, m_ref, l_ref, o_ref)
 
     return kernel
 
 
 def attend_blocks(
-    queries, keys, vals_t, blk_req, blk_base, blk_limit, lengths, slot_of, carry=None
+    queries, cache_keys, cache_vals, new_keys, new_vals,
+    blk_req, blk_base, blk_limit, lengths, slot_of,
 ):
     head_count, _, blk_len, head_dim = queries.shape
     req_count = lengths.shape[0]
     q_len = slot_of.shape[0] // req_count * blk_len
-    blk_count = keys.shape[0]
+    cache_count = cache_keys.shape[0]
+    new_count = new_keys.shape[0]
     vmem = pltpu.MemorySpace.VMEM
     whole = pl.BlockSpec(memory_space=vmem)
+
+    def cache_block(j, *_):
+        return (jnp.minimum(j, cache_count - 1), 0, 0, 0)
+
+    def new_block(j, *_):
+        return (jnp.maximum(j - cache_count, 0), 0, 0, 0)
+
+    key_shape = (1, head_count, blk_len, head_dim)
+    val_shape = (1, head_count, head_dim, blk_len)
     in_specs = [
         whole,
-        pl.BlockSpec((1, head_count, blk_len, head_dim), lambda j, *_: (j, 0, 0, 0)),
-        pl.BlockSpec((1, head_count, head_dim, blk_len), lambda j, *_: (j, 0, 0, 0)),
+        pl.BlockSpec(key_shape, cache_block),
+        pl.BlockSpec(val_shape, cache_block),
+        pl.BlockSpec(key_shape, new_block),
+        pl.BlockSpec(val_shape, new_block),
     ]
-    args = [queries, keys, vals_t]
-    if carry is not None:
-        in_specs += [whole, whole, whole]
-        args += list(carry)
     out_shape = (
         jax.ShapeDtypeStruct((req_count, head_count, 1, q_len), jnp.float32),
         jax.ShapeDtypeStruct((req_count, head_count, 1, q_len), jnp.float32),
@@ -114,18 +127,17 @@
     )
     grid_spec = pltpu.PrefetchScalarGridSpec(
         num_scalar_prefetch=5,
-        grid=(blk_count,),
+        grid=(cache_count + new_count,),
         in_specs=in_specs,
         out_specs=(whole, whole, whole),
     )
     return pl.pallas_call(
-        attend_kernel(carry is not None),
+        attend_kernel(cache_count),
         out_shape=out_shape,
         grid_spec=grid_spec,
-        compiler_params=pltpu.CompilerParams(
-            dimension_semantics=("arbitrary",)
-        ),
-    )(blk_req, blk_base, blk_limit, lengths, slot_of, *args)
+        compiler_params=pltpu.CompilerParams(dimension_semantics=("arbitrary",)),
+    )(blk_req, blk_base, blk_limit, lengths, slot_of,
+      queries, cache_keys, cache_vals, new_keys, new_vals)
 
 
 def body(tokens, gain, w_qkv, w_out, cache, lengths, order, pages):
@@ -147,6 +159,11 @@
     normed = (tok_float * inv_rms * gain.astype(jnp.float32)[None, :]).astype(jnp.bfloat16)
 
     w_q = lax.all_gather(w_qkv[:, 0], "wide", axis=0, tiled=True)
+    w_kv_local = w_qkv[:, 1:]
+    w_kv = lax.all_to_all(
+        jnp.broadcast_to(w_kv_local[None], (wide_count,) + w_kv_local.shape),
+        "wide", split_axis=0, concat_axis=0, tiled=True,
+    ).reshape((wide_count * w_kv_local.shape[0],) + w_kv_local.shape[1:])
     cache_ids = wide_index * cache_count + jnp.arange(cache_count, dtype=jnp.int32)
     page_ids = jnp.arange(pages.shape[0], dtype=jnp.int32)
     entries = jnp.sum(jnp.where(pages[None, :] == cache_ids[:, None], page_ids[None, :], 0), axis=1)
@@ -175,10 +192,7 @@
     cache_vals = jnp.transpose(
         cache_v[:, :, 1].reshape(cache_count, blk_len, head_count, HD), (0, 2, 3, 1)
     )
-    all_queries, cache_vals, w_kv_local = lax.optimization_barrier(
-        (all_queries, cache_vals, w_qkv[:, 1:])
-    )
-    w_kv = lax.all_gather(w_kv_local, "wide", axis=0, tiled=True)
+    all_queries, cache_vals = lax.optimization_barrier((all_queries, cache_vals))
 
     block_ids = jnp.arange(block_total, dtype=jnp.int32)
     slot_of = jnp.sum(
@@ -186,10 +200,7 @@
     )
     q_heads = all_queries
 
-    carry = attend_blocks(
-        q_heads, cache_keys, cache_vals, cache_req, cache_base, cache_limit, lengths, slot_of
-    )
-    carry, w_out_local = lax.optimization_barrier((carry, w_out))
+    all_queries, w_out_local = lax.optimization_barrier((all_queries, w_out))
     part_out = lax.all_gather(w_out_local, "wide", axis=0, tiled=True)
 
     kv_proj = jnp.einsum("tk,kcj->tcj", normed, w_kv, preferred_element_type=jnp.float32)
@@ -202,14 +213,15 @@
     new_limit = jnp.full((slot_count,), beyond, jnp.int32)
     head_max, head_den, head_num = attend_blocks(
         q_heads,
+        cache_keys,
+        cache_vals,
         jnp.transpose(keys_new, (0, 2, 1, 3)),
         jnp.transpose(vals_new, (0, 2, 3, 1)),
-        slot_req,
-        slot_start,
-        new_limit,
+        jnp.concatenate([cache_req, slot_req]),
+        jnp.concatenate([cache_base, slot_start]),
+        jnp.concatenate([cache_limit, new_limit]),
         lengths,
         slot_of,
-        carry=carry,
     )
 
     split = fresh_len // tok_rows

time: 280 us -> 353 us (1.26)
  waiting for transfers between devices: 116 us -> 178 us
  local copies, waits for them, and re-layouts: 61.9 us -> 75.9 us
  Pallas kernels: 49.9 us -> 42.6 us
  starting transfers between devices: 7.37 us -> 13.2 us
    all_to_all x0 -> x1, waiting for transfers between devices: none -> 93.3 us  [body(): lax.all_to_all(jnp.broadcast_to(w_kv_local[None], (wide_count,) + w_kv_lo...]
    all_gather x1 -> x0, waiting for transfers between devices: 20.5 us -> none  [body(): w_kv = lax.all_gather(w_kv_local, 'wide', axis=0, tiled=True)]
    all_gather x1, waiting for transfers between devices: 10.3 us -> 0.02 us  [body(): w_q = lax.all_gather(w_qkv[:, 0], 'wide', axis=0, tiled=True)]
    all_to_all x0 -> x1, local copies, waits for them, and re-layouts: none -> 8.16 us  [body(): lax.all_to_all(jnp.broadcast_to(w_kv_local[None], (wide_count,) + w_kv_lo...]
    pallas_call x2 -> x1, Pallas kernels: 49.9 us -> 42.6 us  [attend_blocks(): pl.pallas_call(attend_kernel(cache_count), out_shape=out_shape, grid_spec...]
    all_to_all x0 -> x1, starting transfers between devices: none -> 5.31 us  [body(): lax.all_to_all(jnp.broadcast_to(w_kv_local[None], (wide_count,) + w_kv_lo...]
    broadcast_in_dim x0 -> x1, local copies, waits for them, and re-layouts: none -> 4.56 us  [body(): jnp.broadcast_to(w_kv_local[None], (wide_count,) + w_kv_local.shape)]
  transfers between devices with their start and end apart: 7 -> 7, of which waited for: 6 -> 4; matrix products, arithmetic and copies ran while one was open for 28% -> 24% of each run, Pallas kernels for 18% -> 12%
where the time goes in v5:
time: 353 us; the launch traced here: 351 us
  waiting for transfers between devices  178 us (50%)
  local copies, waits for them, and re-layouts  75.9 us (22%)
  Pallas kernels  42.6 us (12%)
  matrix products  14.7 us (4%)
  other arithmetic  13.6 us (4%)
  between operations  13.4 us (4%)
  starting transfers between devices  13.2 us (4%)
    all_to_all x1, waiting for transfers between devices, body(): lax.all_to_all(jnp.broadcast_to(w_kv_local[None], (wide_count,) + w_kv_lo...  93.3 us
    pallas_call x1, Pallas kernels, attend_blocks(): pl.pallas_call(attend_kernel(cache_count), out_shape=out_shape, grid_spec...  42.6 us
    all_to_all x1, waiting for transfers between devices, body(): lax.all_to_all(sent_num, 'wide', split_axis=0, concat_axis=0, tiled=True)  37.6 us
    reduce_scatter x1, waiting for transfers between devices, body(): lax.psum_scatter(out_part.astype(jnp.bfloat16), 'narrow', scatter_dimensi...  34.6 us
    slice x2, local copies, waits for them, and re-layouts, body(): cache_v[:, :, 1].reshape(cache_count, blk_len, head_count, HD)  24.4 us
    slice x1, local copies, waits for them, and re-layouts, body(): cache[:, :, 0].reshape(cache_count, blk_len, head_count, HD)  18.4 us
    all_gather x1, waiting for transfers between devices, body(): all_queries = lax.all_gather(queries, 'wide', axis=1, tiled=True)  12.3 us
    another operation x2, local copies, waits for them, and re-layouts, body(): cache[:, :, 0].reshape(cache_count, blk_len, head_count, HD)  11 us
  transfers between devices with their start and end apart: 7, of which 4 were waited for; matrix products, arithmetic and copies ran while one was open for 24% of the time, Pallas kernels for 12%

profile of v5, /device:TPU:0, one launch (start us, length us, event | category | flops | bytes accessed | tf_op | source)
XLA Modules:
  0.0 351.3 jit_solution(2257389919570711696)
XLA Ops:
  6.5 1.3 slice-done
  7.8 4.6 %broadcast_in_dim.50 = bf16[8,384,2,768]{3,1,2,0:T(8,128)(2,1)} broadcast(bf16[384,2,768]{2,0,1:T(8,128)(2,1)S(1)} %slice-done), dimensions={1,2,3} | broadcast | bytes 10616832 | tf_op jit(solution)/shard_map/broadcast_in_dim | solution.py:164
  12.4 5.3 %all-to-all-start = ((bf16[8,384,2,768]{3,1,2,0:T(8,128)(2,1)}), bf16[8,384,2,768]{3,1,2,0:T(8,128)(2,1)}, u32[]{:S(2)}, u32[]{:S(2)}) async-start(bf16[8,384,2,768]{3,1,2,0:T(8,128)(2,1)} %broadcast_in_dim.50), calls=%async_computation | async-start | bytes 18874368 | tf_op jit(solution)/shard_map/all_to_all | solution.py:163
  17.7 0.9 slice.51
  19.1 18.4 %slice_reduce_fusion = bf16[32,64,768]{2,1,0:T(8,128)(2,1)S(1)} fusion(bf16[32,64,2,768]{3,2,1,0:T(2,128)(2,1)} %param.12), kind=kLoop, calls=%fused_computation.1 | loop fusion | bytes 6291456 | tf_op jit(solution)/shard_map/slice | solution.py:174
  37.6 5.4 %reshape_squeeze.9 = bf16[32,64,8,96]{3,2,1,0:T(8,128)(2,1)} reshape(bf16[32,64,768]{2,1,0:T(8,128)(2,1)S(1)} %slice_reduce_fusion) | data formatting | bytes 6291456 | tf_op jit(solution)/shard_map/reshape;squeeze | solution.py:174
  43.0 5.6 %copy.47 = bf16[32,64,8,96]{3,1,2,0:T(8,128)(2,1)} copy(bf16[32,64,8,96]{3,2,1,0:T(8,128)(2,1)} %reshape_squeeze.9) | data formatting | bytes 6291456 | tf_op jit(solution)/shard_map/reshape;squeeze | solution.py:174
  49.3 93.3 %all-to-all-done = bf16[8,384,2,768]{3,1,2,0:T(8,128)(2,1)} async-done(((bf16[8,384,2,768]{3,1,2,0:T(8,128)(2,1)}), bf16[8,384,2,768]{3,1,2,0:T(8,128)(2,1)}, u32[]{:S(2)}, u32[]{:S(2)}) %all-to-all-start) | async-done | bytes 9437216 | tf_op jit(solution)/shard_map/all_to_all | solution.py:163
  142.6 8.2 %copy.38 = bf16[8,384,2,768]{3,1,0,2:T(8,128)(2,1)} copy(bf16[8,384,2,768]{3,1,2,0:T(8,128)(2,1)} %all-to-all-done) | data formatting | bytes 18874368 | tf_op jit(solution)/shard_map/all_to_all | solution.py:163
  150.7 5.4 %fusion.3 = f32[256,2,768]{2,0,1:T(8,128)S(1)} fusion(bf16[3072,2,768]{2,0,1:T(8,128)(2,1)} %bitcast.43, bf16[256,3072]{1,0:T(8,128)(2,1)S(1)} %copy-done.1, f32[3072]{0:T(1024)S(1)} %convert_element_type.46, f32[256]{0:T(256)S(1)} %add_rsqrt_fusion), kind=kOutput, calls=%fused_computation.10 | convolution fusion | flops 2419064832 | bytes 12596224 | tf_op jit(solution)/shard_map/tk,kcj->tcj/dot_general | solution.py:206
  156.1 1.2 copy-done.2
  157.6 4.4 %fusion.7 = f32[256,768]{0,1:T(8,128)S(1)} fusion(bf16[3072,768]{1,0:T(8,128)(2,1)} %bitcast.52, bf16[256,3072]{1,0:T(8,128)(2,1)S(1)} %copy-done.1, f32[3072]{0:T(1024)S(1)} %convert_element_type.46, f32[256]{0:T(256)S(1)} %add_rsqrt_fusion), kind=kOutput, calls=%fused_computation.17 | convolution fusion | flops 1211105280 | bytes 7091200 | tf_op jit(solution)/shard_map/dot_general | solution.py:183
  162.8 1.1 maximum_bitcast_fusion
  164.2 8.9 %slice.55 = bf16[32,64,1,768]{3,2,1,0:T(2,128)(2,1)} slice(bf16[32,64,2,768]{3,2,1,0:T(2,128)(2,1)} %param.12), slice={[0:32], [0:64], [1:2], [0:768]} | slice | bytes 6291456 | tf_op jit(solution)/shard_map/slice | solution.py:193
  173.0 15.5 %copy.37 = bf16[32,64,1,768]{1,3,0,2:T(8,128)(2,1)} copy(bf16[32,64,1,768]{3,2,1,0:T(2,128)(2,1)} %slice.55) | data formatting | bytes 6291456 | tf_op jit(solution)/shard_map/slice | solution.py:193
  188.6 12.3 %all-gather.5.cloned.1.call-done.refs_0_ = bf16[8,32,64,96]{3,2,1,0:T(8,128)(2,1)} async-done(((bf16[8,4,64,96]{3,2,1,0:T(8,128)(2,1)}), bf16[8,32,64,96]{3,2,1,0:T(8,128)(2,1)}) %all-gather.5.cloned.1.call-update) | async-done | bytes 3145744 | tf_op jit(solution)/shard_map/all_gather | solution.py:190
  201.8 0.6 pad_add_fusion
  202.4 0.7 select_reduce_fusion.1.slot_ref
  203.0 1.2 slice.100
  205.9 1.3 copy.42
  207.2 1.1 maximum_bitcast_fusion.1.refs_3_
  208.3 42.6 %shard_map.82 = (f32[4,8,1,512]{3,2,1,0:T(1,128)}, f32[4,8,1,512]{3,2,1,0:T(1,128)}, f32[4,8,96,512]{3,2,1,0:T(8,128)}) custom-call(s32[36]{0:T(128)} %get-tuple-element.39.req_ref, s32[36]{0:T(128)} %get-tuple-element.40.base_ref, s32[36]{0:T(128)} %concatenate.37.limit_ref, s32[4]{0:T(128)} %len_ref.1, s32[32]{0:T(128)} %select_reduce_fusion.1.slot_ref, ...), custom_call_target="tpu_custom_call" | custom-call | tf_op jit(solution)/shard_map/pallas_call | solution.py:134
  250.9 0.8 fusion.10
  251.8 1.5 fusion.9
  253.3 3.4 all-to-all-start.2
  256.7 3.3 convert.30
  260.4 1.9 pad_maximum_fusion
  262.3 4.1 %all-to-all-start.1 = ((bf16[8,8,96,256]{3,2,1,0:T(8,128)(2,1)}), bf16[8,8,96,256]{3,2,1,0:T(8,128)(2,1)S(1)}, u32[]{:S(2)}, u32[]{:S(2)}) async-start(bf16[8,8,96,256]{3,2,1,0:T(8,128)(2,1)} %bitcast.13), calls=%async_computation.1 | async-start | bytes 6291456 | tf_op jit(solution)/shard_map/all_to_all | solution.py:240
  266.7 37.6 %all-to-all-done.1 = bf16[8,8,96,256]{3,2,1,0:T(8,128)(2,1)S(1)} async-done(((bf16[8,8,96,256]{3,2,1,0:T(8,128)(2,1)}), bf16[8,8,96,256]{3,2,1,0:T(8,128)(2,1)S(1)}, u32[]{:S(2)}, u32[]{:S(2)}) %all-to-all-start.1) | async-done | bytes 3145760 | tf_op jit(solution)/shard_map/all_to_all | solution.py:240
  304.3 0.7 multiply_reduce_fusion
  305.2 4.9 %convolution_convert_fusion = bf16[256,3072]{1,0:T(8,128)(2,1)} fusion(bf16[256,768]{0,1:T(8,128)(2,1)S(1)} %bitcast.49, bf16[3072,768]{1,0:T(8,128)(2,1)} %all-gather.7.cloned.1.call-done), kind=kOutput, calls=%fused_computation.5 | convolution fusion | flops 1208745984 | bytes 6684672 | tf_op jit(solution)/shard_map/dot_general | solution.py:252
  310.1 34.6 %reduce-scatter.2.cloned.1.call-done = bf16[256,768]{1,0:T(8,128)(2,1)} async-done(((bf16[256,3072]{1,0:T(8,128)(2,1)}), bf16[256,768]{1,0:T(8,128)(2,1)}) %reduce-scatter.2.cloned.1.call-update) | async-done | bytes 393232 | tf_op jit(solution)/shard_map/reduce_scatter | solution.py:255
  (55 shorter events, 5.9 us)
Async XLA Ops:
  6.5 1.3 slice-start
  12.4 5.4 %copy-start = (bf16[384,3,768]{2,0,1:T(8,128)(2,1)S(1)}, bf16[384,3,768]{2,0,1:T(8,128)(2,1)}, u32[]{:S(2)}) copy-start(bf16[384,3,768]{2,0,1:T(8,128)(2,1)} %param.10) | copy-start | bytes 5308420
  12.4 6.3 %copy-start.6 = (s32[32]{0:T(128)S(1)}, s32[32]{0:T(128)}, u32[]{:S(2)}) copy-start(s32[32]{0:T(128)} %param.14) | copy-start | bytes 388
  12.4 6.4 %copy-start.5 = (s32[4]{0:T(128)S(1)}, s32[4]{0:T(128)}, u32[]{:S(2)}) copy-start(s32[4]{0:T(128)} %len_ref.1) | copy-start | bytes 52
  12.4 6.8 %copy-start.3 = (bf16[3072]{0:T(1024)(128)(2,1)S(1)}, bf16[3072]{0:T(1024)(128)(2,1)}, u32[]{:S(2)}) copy-start(bf16[3072]{0:T(1024)(128)(2,1)} %param.9) | copy-start | bytes 18436
  12.4 130.2 %all-to-all-start = ((bf16[8,384,2,768]{3,1,2,0:T(8,128)(2,1)}), bf16[8,384,2,768]{3,1,2,0:T(8,128)(2,1)}, u32[]{:S(2)}, u32[]{:S(2)}) async-start(bf16[8,384,2,768]{3,1,2,0:T(8,128)(2,1)} %broadcast_in_dim.50), calls=%async_computation | async-start | bytes 18874368 | tf_op jit(solution)/shard_map/all_to_all | solution.py:163
  17.7 139.9 %all-gather.9.cloned.1.call-start = ((), (), s32[]{:S(2)}) async-start(), calls=%async_computation.7 | async-start | bytes 5308416 | tf_op jit(solution)/shard_map/all_gather | solution.py:161
  18.6 182.2 %all-gather.5.cloned.1.call-start = ((), (), s32[]{:S(2)}) async-start(), calls=%async_computation.4 | async-start | bytes 4718592 | tf_op jit(solution)/shard_map/all_gather | solution.py:190
  43.0 5.6 %copy-start.1 = (bf16[256,3072]{1,0:T(8,128)(2,1)S(1)}, bf16[256,3072]{1,0:T(8,128)(2,1)}, u32[]{:S(2)}) copy-start(bf16[256,3072]{1,0:T(8,128)(2,1)} %param.8) | copy-start | bytes 4718596
  156.1 1.2 copy-start.2
  163.9 141.2 %all-gather.7.cloned.1.call-start = ((), (), s32[]{:S(2)}) async-start(), calls=%async_computation.5 | async-start | bytes 5308416 | tf_op jit(solution)/shard_map/all_gather | solution.py:204
  173.0 27.9 %copy-start.4 = (s32[256]{0:T(256)S(1)}, s32[256]{0:T(256)}, u32[]{:S(2)}) copy-start(s32[256]{0:T(256)} %param.15) | copy-start | bytes 3076
  253.3 9.0 %all-to-all-start.2 = ((f32[8,8,2,256]{3,2,1,0:T(2,128)}), f32[8,8,2,256]{3,2,1,0:T(2,128)S(1)}, u32[]{:S(2)}, u32[]{:S(2)}) async-start(f32[8,8,2,256]{3,2,1,0:T(2,128)} %bitcast.14), calls=%async_computation.2 | async-start | bytes 262144 | tf_op jit(solution)/shard_map/all_to_all | solution.py:241
  262.3 42.0 %all-to-all-start.1 = ((bf16[8,8,96,256]{3,2,1,0:T(8,128)(2,1)}), bf16[8,8,96,256]{3,2,1,0:T(8,128)(2,1)S(1)}, u32[]{:S(2)}, u32[]{:S(2)}) async-start(bf16[8,8,96,256]{3,2,1,0:T(8,128)(2,1)} %bitcast.13), calls=%async_computation.1 | async-start | bytes 6291456 | tf_op jit(solution)/shard_map/all_to_all | solution.py:240
  266.4 78.3 %reduce-scatter.2.cloned.1.call-start = ((), (), s32[]{:S(2)}) async-start(), calls=%async_computation.6 | async-start | bytes 1966080 | tf_op jit(solution)/shard_map/reduce_scatter | solution.py:255
Sparse Core Ops, SparseCore 0:
  20.4 86.0 all-gather.8
  164.1 36.7 all-gather.4
  202.8 38.9 all-gather.6
  310.3 34.4 reduce-scatter.1

commit v6 on v5

--- a/solution.py
+++ b/solution.py
@@ -158,12 +158,9 @@
     inv_rms = lax.rsqrt(jnp.mean(tok_float * tok_float, axis=1, keepdims=True) + 1e-05)
     normed = (tok_float * inv_rms * gain.astype(jnp.float32)[None, :]).astype(jnp.bfloat16)
 
-    w_q = lax.all_gather(w_qkv[:, 0], "wide", axis=0, tiled=True)
-    w_kv_local = w_qkv[:, 1:]
-    w_kv = lax.all_to_all(
-        jnp.broadcast_to(w_kv_local[None], (wide_count,) + w_kv_local.shape),
-        "wide", split_axis=0, concat_axis=0, tiled=True,
-    ).reshape((wide_count * w_kv_local.shape[0],) + w_kv_local.shape[1:])
+    w_all = lax.all_gather(w_qkv, "wide", axis=0, tiled=True)
+    w_q = w_all[:, 0]
+    w_kv = w_all[:, 1:]
     cache_ids = wide_index * cache_count + jnp.arange(cache_count, dtype=jnp.int32)
     page_ids = jnp.arange(pages.shape[0], dtype=jnp.int32)
     entries = jnp.sum(jnp.where(pages[None, :] == cache_ids[:, None], page_ids[None, :], 0), axis=1)
@@ -173,7 +170,12 @@
     cache_keys = jnp.transpose(
         cache[:, :, 0].reshape(cache_count, blk_len, head_count, HD), (0, 2, 1, 3)
     )
-    w_q, cache_keys = lax.optimization_barrier((w_q, cache_keys))
+    cache_vals = jnp.transpose(
+        cache[:, :, 1].reshape(cache_count, blk_len, head_count, HD), (0, 2, 3, 1)
+    )
+    w_q, w_kv, cache_keys, cache_vals = lax.optimization_barrier(
+        (w_q, w_kv, cache_keys, cache_vals)
+    )
     blk_idx = jnp.arange(blk_len, dtype=jnp.int32)
     slot_blocks = lax.dynamic_slice_in_dim(order, wide_index * slot_count, slot_count)
     slot_req = slot_blocks // per_request
@@ -188,11 +190,6 @@
         (2, 0, 1, 3),
     )
     all_queries = lax.all_gather(queries, "wide", axis=1, tiled=True)
-    queries, cache_v = lax.optimization_barrier((queries, cache))
-    cache_vals = jnp.transpose(
-        cache_v[:, :, 1].reshape(cache_count, blk_len, head_count, HD), (0, 2, 3, 1)
-    )
-    all_queries, cache_vals = lax.optimization_barrier((all_queries, cache_vals))
 
     block_ids = jnp.arange(block_total, dtype=jnp.int32)
     slot_of = jnp.sum(
@@ -203,7 +200,8 @@
     all_queries, w_out_local = lax.optimization_barrier((all_queries, w_out))
     part_out = lax.all_gather(w_out_local, "wide", axis=0, tiled=True)
 
-    kv_proj = jnp.einsum("tk,kcj->tcj", normed, w_kv, preferred_element_type=jnp.float32)
+    queries, normed_kv, w_kv = lax.optimization_barrier((queries, normed, w_kv))
+    kv_proj = jnp.einsum("tk,kcj->tcj", normed_kv, w_kv, preferred_element_type=jnp.float32)
     keys_new = (
         rotate(kv_proj[:, 0].reshape(tok_rows, head_count, HD), positions)
         .astype(jnp.bfloat16)
@@ -211,12 +209,15 @@
     )
     vals_new = kv_proj[:, 1].astype(jnp.bfloat16).reshape(slot_count, blk_len, head_count, HD)
     new_limit = jnp.full((slot_count,), beyond, jnp.int32)
+    new_keys = jnp.transpose(keys_new, (0, 2, 1, 3))
+    new_vals = jnp.transpose(vals_new, (0, 2, 3, 1))
+    q_heads, new_keys, new_vals = lax.optimization_barrier((q_heads, new_keys, new_vals))
     head_max, head_den, head_num = attend_blocks(
         q_heads,
         cache_keys,
         cache_vals,
-        jnp.transpose(keys_new, (0, 2, 1, 3)),
-        jnp.transpose(vals_new, (0, 2, 3, 1)),
+        new_keys,
+        new_vals,
         jnp.concatenate([cache_req, slot_req]),
         jnp.concatenate([cache_base, slot_start]),
         jnp.concatenate([cache_limit, new_limit]),

time: 353 us -> 303 us (0.86)
  waiting for transfers between devices: 178 us -> 140 us
  local copies, waits for them, and re-layouts: 75.9 us -> 69.9 us
  starting transfers between devices: 13.2 us -> 7.33 us
    all_to_all x1 -> x0, waiting for transfers between devices: 93.3 us -> none  [body(): lax.all_to_all(jnp.broadcast_to(w_kv_local[None], (wide_count,) + w_kv_lo...]
    all_gather x1, waiting for transfers between devices: 0.02 us -> 27.5 us  [body(): w_all = lax.all_gather(w_qkv, 'wide', axis=0, tiled=True)]
    all_gather x1, waiting for transfers between devices: 12.3 us -> 36.6 us  [body(): all_queries = lax.all_gather(queries, 'wide', axis=1, tiled=True)]
    all_to_all x1 -> x0, local copies, waits for them, and re-layouts: 8.16 us -> none  [body(): lax.all_to_all(jnp.broadcast_to(w_kv_local[None], (wide_count,) + w_kv_lo...]
    all_to_all x1 -> x0, starting transfers between devices: 5.31 us -> none  [body(): lax.all_to_all(jnp.broadcast_to(w_kv_local[None], (wide_count,) + w_kv_lo...]
    squeeze x0 -> x1, local copies, waits for them, and re-layouts: none -> 4.77 us  [body(): w_q = w_all[:, 0]]
    broadcast_in_dim x1 -> x0, local copies, waits for them, and re-layouts: 4.56 us -> none  [body(): jnp.broadcast_to(w_kv_local[None], (wide_count,) + w_kv_local.shape)]
    slice x6 -> x3, local copies, waits for them, and re-layouts: 45 us -> 49.2 us  [the longest x2 41.4 us: body(): cache[:, :, 1].reshape(cache_count, blk_len, head_count, HD)]
  transfers between devices with their start and end apart: 7 -> 6, of which waited for: 4 -> 5; matrix products, arithmetic and copies ran while one was open for 24% -> 25% of each run, Pallas kernels for 12% -> 14%
where the time goes in v6:
time: 303 us; the launch traced here: 302 us
  waiting for transfers between devices  140 us (46%)
  local copies, waits for them, and re-layouts  69.9 us (23%)
  Pallas kernels  42.3 us (14%)
  other arithmetic  14.6 us (5%)
  matrix products  14.4 us (5%)
  between operations  13.4 us (4%)
  starting transfers between devices  7.33 us (2%)
    pallas_call x1, Pallas kernels, attend_blocks(): pl.pallas_call(attend_kernel(cache_count), out_shape=out_shape, grid_spec...  42.3 us
    slice x2, local copies, waits for them, and re-layouts, body(): cache[:, :, 1].reshape(cache_count, blk_len, head_count, HD)  41.4 us
    all_to_all x1, waiting for transfers between devices, body(): lax.all_to_all(sent_num, 'wide', split_axis=0, concat_axis=0, tiled=True)  37.5 us
    all_gather x1, waiting for transfers between devices, body(): all_queries = lax.all_gather(queries, 'wide', axis=1, tiled=True)  36.6 us
    reduce_scatter x1, waiting for transfers between devices, body(): lax.psum_scatter(out_part.astype(jnp.bfloat16), 'narrow', scatter_dimensi...  34.6 us
    all_gather x1, waiting for transfers between devices, body(): w_all = lax.all_gather(w_qkv, 'wide', axis=0, tiled=True)  27.5 us
    another operation x2, local copies, waits for them, and re-layouts, body(): cache[:, :, 0].reshape(cache_count, blk_len, head_count, HD)  11 us
    slice x1, local copies, waits for them, and re-layouts, body(): w_kv = w_all[:, 1:]  7.85 us
  transfers between devices with their start and end apart: 6, of which 5 were waited for; matrix products, arithmetic and copies ran while one was open for 25% of the time, Pallas kernels for 14%

profile of v6, /device:TPU:0, one launch (start us, length us, event | category | flops | bytes accessed | tf_op | source)
XLA Modules:
  0.0 302.0 jit_solution(16692444877487654858)
XLA Ops:
  6.5 0.7 all-gather.4.cloned.1.call-update
  7.3 0.7 and_select_fusion.2
  8.0 0.8 select_reduce_fusion.3
  9.1 0.7 convert_element_type.46
  9.8 25.8 %fusion.12 = (bf16[32,64,1,768]{3,2,1,0:T(2,128)(2,1)}, bf16[32,64,768]{2,1,0:T(8,128)(2,1)S(1)}) fusion(bf16[32,64,2,768]{3,2,1,0:T(2,128)(2,1)} %param.12), kind=kLoop, calls=%fused_computation.60 | loop fusion | bytes 12582912 | tf_op jit(solution)/shard_map/slice | solution.py:174
  35.5 15.6 %copy.24 = bf16[32,64,1,768]{1,3,0,2:T(8,128)(2,1)} copy(bf16[32,64,1,768]{3,2,1,0:T(2,128)(2,1)} %get-tuple-element.35) | data formatting | bytes 6291456 | tf_op jit(solution)/shard_map/slice | solution.py:174
  51.1 5.4 %reshape_squeeze.9 = bf16[32,64,8,96]{3,2,1,0:T(8,128)(2,1)} reshape(bf16[32,64,768]{2,1,0:T(8,128)(2,1)S(1)} %get-tuple-element.36) | data formatting | bytes 6291456 | tf_op jit(solution)/shard_map/reshape;squeeze | solution.py:171
  56.5 5.6 %copy.36 = bf16[32,64,8,96]{3,1,2,0:T(8,128)(2,1)} copy(bf16[32,64,8,96]{3,2,1,0:T(8,128)(2,1)} %reshape_squeeze.9) | data formatting | bytes 6291456 | tf_op jit(solution)/shard_map/reshape;squeeze | solution.py:171
  63.3 27.5 %all-gather.4.cloned.1.call-done = bf16[3072,3,768]{2,0,1:T(8,128)(2,1)} async-done(((bf16[384,3,768]{2,0,1:T(8,128)(2,1)}), bf16[3072,3,768]{2,0,1:T(8,128)(2,1)}) %all-gather.4.cloned.1.call-update) | async-done | bytes 14155792 | tf_op jit(solution)/shard_map/all_gather | solution.py:161
  90.8 4.8 %slice_bitcast_fusion = bf16[3072,768]{1,0:T(8,128)(2,1)} fusion(bf16[3072,3,768]{2,0,1:T(8,128)(2,1)} %all-gather.4.cloned.1.call-done), kind=kLoop, calls=%fused_computation.2 | loop fusion | bytes 9437184 | tf_op jit(solution)/shard_map/squeeze | solution.py:162
  95.5 7.9 %slice.68 = bf16[3072,2,768]{2,0,1:T(8,128)(2,1)} slice(bf16[3072,3,768]{2,0,1:T(8,128)(2,1)} %all-gather.4.cloned.1.call-done), slice={[0:3072], [1:3], [0:768]} | slice | bytes 18874368 | tf_op jit(solution)/shard_map/slice | solution.py:163
  103.4 4.3 %fusion.14 = f32[256,768]{0,1:T(8,128)S(1)} fusion(bf16[256,3072]{1,0:T(8,128)(2,1)S(1)} %fusion.2, bf16[3072,768]{1,0:T(8,128)(2,1)} %slice_bitcast_fusion), kind=kOutput, calls=%fused_computation.62 | convolution fusion | flops 1207959552 | bytes 7077888 | tf_op jit(solution)/shard_map/dot_general | solution.py:185
  108.4 1.1 maximum_bitcast_fusion
  109.8 36.6 %all-gather.6.cloned.1.call-done.refs_0_ = bf16[8,32,64,96]{3,2,1,0:T(8,128)(2,1)} async-done(((bf16[8,4,64,96]{3,2,1,0:T(8,128)(2,1)}), bf16[8,32,64,96]{3,2,1,0:T(8,128)(2,1)}) %all-gather.6.cloned.1.call-update) | async-done | bytes 3145744 | tf_op jit(solution)/shard_map/all_gather | solution.py:192
  146.7 0.5 concatenate.37.limit_ref
  147.3 0.6 pad_add_fusion
  147.9 0.7 select_reduce_fusion.1.slot_ref
  148.6 5.2 %fusion.3 = f32[256,2,768]{2,0,1:T(8,128)S(1)} fusion(bf16[3072,2,768]{2,0,1:T(8,128)(2,1)} %slice.68, bf16[256,3072]{1,0:T(8,128)(2,1)S(1)} %fusion.2), kind=kOutput, calls=%fused_computation.11 | convolution fusion | flops 2415919104 | bytes 12582912 | tf_op jit(solution)/shard_map/tk,kcj->tcj/dot_general | solution.py:204
  154.2 0.6 convert_element_type.50
  155.4 1.3 copy.31
  157.2 1.1 maximum_bitcast_fusion.1.refs_3_
  158.3 42.3 %shard_map.82 = (f32[4,8,1,512]{3,2,1,0:T(1,128)}, f32[4,8,1,512]{3,2,1,0:T(1,128)}, f32[4,8,96,512]{3,2,1,0:T(8,128)}) custom-call(s32[36]{0:T(128)} %get-tuple-element.47.req_ref, s32[36]{0:T(128)} %get-tuple-element.48.base_ref, s32[36]{0:T(128)} %concatenate.37.limit_ref, s32[4]{0:T(128)} %len_ref.1, s32[32]{0:T(128)} %select_reduce_fusion.1.slot_ref, ...), custom_call_target="tpu_custom_call" | custom-call | tf_op jit(solution)/shard_map/pallas_call | solution.py:134
  200.6 3.3 %convert.30 = bf16[4,8,96,512]{3,2,1,0:T(8,128)(2,1)S(1)} convert(f32[4,8,96,512]{3,2,1,0:T(8,128)} %get-tuple-element.27) | non-fusion elementwise | flops 1572864 | bytes 9437184 | tf_op jit(solution)/shard_map/convert.3
  204.0 0.7 fusion.6
  204.8 3.4 %all-to-all-start.1 = ((f32[8,8,2,256]{3,2,1,0:T(2,128)}), f32[8,8,2,256]{3,2,1,0:T(2,128)S(1)}, u32[]{:S(2)}, u32[]{:S(2)}) async-start(f32[8,8,2,256]{3,2,1,0:T(2,128)} %bitcast.13), calls=%async_computation.1 | async-start | bytes 262144 | tf_op jit(solution)/shard_map/all_to_all | solution.py:242
  208.6 1.9 pad_maximum_fusion
  210.5 3.1 %all-to-all-done.1 = f32[8,8,2,256]{3,2,1,0:T(2,128)S(1)} async-done(((f32[8,8,2,256]{3,2,1,0:T(2,128)}), f32[8,8,2,256]{3,2,1,0:T(2,128)S(1)}, u32[]{:S(2)}, u32[]{:S(2)}) %all-to-all-start.1) | async-done | bytes 131104 | tf_op jit(solution)/shard_map/all_to_all | solution.py:242
  213.6 3.6 %all-to-all-start = ((bf16[8,8,96,256]{3,2,1,0:T(8,128)(2,1)}), bf16[8,8,96,256]{3,2,1,0:T(8,128)(2,1)S(1)}, u32[]{:S(2)}, u32[]{:S(2)}) async-start(bf16[8,8,96,256]{3,2,1,0:T(8,128)(2,1)} %bitcast.12), calls=%async_computation | async-start | bytes 6291456 | tf_op jit(solution)/shard_map/all_to_all | solution.py:241
  217.5 37.5 %all-to-all-done = bf16[8,8,96,256]{3,2,1,0:T(8,128)(2,1)S(1)} async-done(((bf16[8,8,96,256]{3,2,1,0:T(8,128)(2,1)}), bf16[8,8,96,256]{3,2,1,0:T(8,128)(2,1)S(1)}, u32[]{:S(2)}, u32[]{:S(2)}) %all-to-all-start) | async-done | bytes 3145760 | tf_op jit(solution)/shard_map/all_to_all | solution.py:241
  255.1 0.7 multiply_reduce_fusion
  255.9 5.0 %convolution_convert_fusion = bf16[256,3072]{1,0:T(8,128)(2,1)} fusion(bf16[256,768]{0,1:T(8,128)(2,1)S(1)} %bitcast.49, bf16[3072,768]{1,0:T(8,128)(2,1)} %all-gather.8.cloned.1.call-done), kind=kOutput, calls=%fused_computation.6 | convolution fusion | flops 1208745984 | bytes 6684672 | tf_op jit(solution)/shard_map/dot_general | solution.py:253
  260.9 34.6 %reduce-scatter.2.cloned.1.call-done = bf16[256,768]{1,0:T(8,128)(2,1)} async-done(((bf16[256,3072]{1,0:T(8,128)(2,1)}), bf16[256,768]{1,0:T(8,128)(2,1)}) %reduce-scatter.2.cloned.1.call-update) | async-done | bytes 393232 | tf_op jit(solution)/shard_map/reduce_scatter | solution.py:256
  (49 shorter events, 5.0 us)
Async XLA Ops:
  6.5 84.2 %all-gather.4.cloned.1.call-start = ((), (), s32[]{:S(2)}) async-start(), calls=%async_computation.3 | async-start | bytes 15925248 | tf_op jit(solution)/shard_map/all_gather | solution.py:161
  7.3 139.1 %all-gather.6.cloned.1.call-start = ((), (), s32[]{:S(2)}) async-start(), calls=%async_computation.4 | async-start | bytes 4718592 | tf_op jit(solution)/shard_map/all_gather | solution.py:192
  56.5 5.6 %copy-start = (bf16[256,3072]{1,0:T(8,128)(2,1)S(1)}, bf16[256,3072]{1,0:T(8,128)(2,1)}, u32[]{:S(2)}) copy-start(bf16[256,3072]{1,0:T(8,128)(2,1)} %param.8) | copy-start | bytes 4718596
  107.7 38.8 %copy-start.3 = (s32[256]{0:T(256)S(1)}, s32[256]{0:T(256)}, u32[]{:S(2)}) copy-start(s32[256]{0:T(256)} %param.15) | copy-start | bytes 3076
  107.7 39.0 %copy-start.4 = (s32[4]{0:T(128)S(1)}, s32[4]{0:T(128)}, u32[]{:S(2)}) copy-start(s32[4]{0:T(128)} %len_ref.1) | copy-start | bytes 52
  107.7 40.2 %copy-start.5 = (s32[32]{0:T(128)S(1)}, s32[32]{0:T(128)}, u32[]{:S(2)}) copy-start(s32[32]{0:T(128)} %param.14) | copy-start | bytes 388
  109.5 146.4 %all-gather.8.cloned.1.call-start = ((), (), s32[]{:S(2)}) async-start(), calls=%async_computation.5 | async-start | bytes 5308416 | tf_op jit(solution)/shard_map/all_gather | solution.py:201
  200.6 3.3 %copy-start.1 = (f32[4,8,1,512]{3,2,1,0:T(1,128)S(1)}, f32[4,8,1,512]{3,2,1,0:T(1,128)}, u32[]{:S(2)}) copy-start(f32[4,8,1,512]{3,2,1,0:T(1,128)} %get-tuple-element.28) | copy-start | bytes 196612
  200.6 3.3 %copy-start.2 = (f32[4,8,1,512]{3,2,1,0:T(1,128)S(1)}, f32[4,8,1,512]{3,2,1,0:T(1,128)}, u32[]{:S(2)}) copy-start(f32[4,8,1,512]{3,2,1,0:T(1,128)} %get-tuple-element.29) | copy-start | bytes 196612
  204.8 8.8 %all-to-all-start.1 = ((f32[8,8,2,256]{3,2,1,0:T(2,128)}), f32[8,8,2,256]{3,2,1,0:T(2,128)S(1)}, u32[]{:S(2)}, u32[]{:S(2)}) async-start(f32[8,8,2,256]{3,2,1,0:T(2,128)} %bitcast.13), calls=%async_computation.1 | async-start | bytes 262144 | tf_op jit(solution)/shard_map/all_to_all | solution.py:242
  213.6 41.5 %all-to-all-start = ((bf16[8,8,96,256]{3,2,1,0:T(8,128)(2,1)}), bf16[8,8,96,256]{3,2,1,0:T(8,128)(2,1)S(1)}, u32[]{:S(2)}, u32[]{:S(2)}) async-start(bf16[8,8,96,256]{3,2,1,0:T(8,128)(2,1)} %bitcast.12), calls=%async_computation | async-start | bytes 6291456 | tf_op jit(solution)/shard_map/all_to_all | solution.py:241
  217.3 78.2 %reduce-scatter.2.cloned.1.call-start = ((), (), s32[]{:S(2)}) async-start(), calls=%async_computation.6 | async-start | bytes 1966080 | tf_op jit(solution)/shard_map/reduce_scatter | solution.py:256
Sparse Core Ops, SparseCore 0:
  9.3 81.4 all-gather.3
  109.7 36.7 all-gather.5
  148.3 38.9 all-gather.7
  261.0 34.4 reduce-scatter.1

commit v7 on v4

--- a/solution.py
+++ b/solution.py
@@ -170,7 +170,13 @@
         .reshape(slot_count, blk_len, head_count, HD),
         (2, 0, 1, 3),
     )
-    all_queries = lax.all_gather(queries, "wide", axis=1, tiled=True)
+    received = [queries] + [
+        lax.ppermute(
+            queries, "wide", [(src, (src + shift) % wide_count) for src in range(wide_count)]
+        )
+        for shift in range(1, wide_count)
+    ]
+    all_queries = jnp.concatenate(received, axis=1)
     queries, cache_v = lax.optimization_barrier((queries, cache))
     cache_vals = jnp.transpose(
         cache_v[:, :, 1].reshape(cache_count, blk_len, head_count, HD), (0, 2, 3, 1)
@@ -184,6 +190,8 @@
     slot_of = jnp.sum(
         jnp.where(order[None, :] == block_ids[:, None], block_ids[None, :], 0), axis=1
     )
+    slot_src = slot_of // slot_count
+    slot_of = (wide_index - slot_src) % wide_count * slot_count + slot_of % slot_count
     q_heads = all_queries
 
     carry = attend_blocks(

time: 280 us -> 294 us (1.050)
  local copies, waits for them, and re-layouts: 61.9 us -> 70.4 us
  starting transfers between devices: 7.37 us -> 15.4 us
  waiting for transfers between devices: 116 us -> 113 us
    all_gather x1 -> x0, waiting for transfers between devices: 11.3 us -> none  [body(): all_queries = lax.all_gather(queries, 'wide', axis=1, tiled=True)]
    ppermute x0 -> x7, waiting for transfers between devices: none -> 8.72 us  [body(): lax.ppermute(queries, 'wide', [(src, (src + shift) % wide_count) for src...]
    ppermute x0 -> x7, starting transfers between devices: none -> 8.05 us  [body(): lax.ppermute(queries, 'wide', [(src, (src + shift) % wide_count) for src...]
    unnamed x21 -> x27, local copies, waits for them, and re-layouts: 0.05 us -> 7.73 us
  transfers between devices with their start and end apart: 7 -> 13, of which waited for: 6 -> 7; matrix products, arithmetic and copies ran while one was open for 28% -> 29% of each run, Pallas kernels for 18% -> 17%
where the time goes in v7:
time: 294 us; the launch traced here: 292 us
  waiting for transfers between devices  113 us (38%)
  local copies, waits for them, and re-layouts  70.4 us (24%)
  Pallas kernels  49.7 us (17%)
  starting transfers between devices  15.4 us (5%)
  other arithmetic  15.2 us (5%)
  matrix products  14.7 us (5%)
  between operations  13.4 us (5%)
    pallas_call x2, Pallas kernels, attend_blocks(): pl.pallas_call(attend_kernel(carry is not None), out_shape=out_shape, gri...  49.7 us
    all_to_all x1, waiting for transfers between devices, body(): lax.all_to_all(sent_num, 'wide', split_axis=0, concat_axis=0, tiled=True)  37.5 us
    reduce_scatter x1, waiting for transfers between devices, body(): lax.psum_scatter(out_part.astype(jnp.bfloat16), 'narrow', scatter_dimensi...  34.5 us
    slice x2, local copies, waits for them, and re-layouts, body(): cache_v[:, :, 1].reshape(cache_count, blk_len, head_count, HD)  24.3 us
    all_gather x1, waiting for transfers between devices, body(): w_kv = lax.all_gather(w_kv_local, 'wide', axis=0, tiled=True)  20.5 us
    slice x1, local copies, waits for them, and re-layouts, body(): cache[:, :, 0].reshape(cache_count, blk_len, head_count, HD)  18.4 us
    another operation x2, local copies, waits for them, and re-layouts, body(): cache[:, :, 0].reshape(cache_count, blk_len, head_count, HD)  11.1 us
    all_gather x1, waiting for transfers between devices, body(): w_q = lax.all_gather(w_qkv[:, 0], 'wide', axis=0, tiled=True)  10.3 us
  transfers between devices with their start and end apart: 13, of which 7 were waited for; matrix products, arithmetic and copies ran while one was open for 29% of the time, Pallas kernels for 17%

profile of v7, /device:TPU:0, one launch (start us, length us, event | category | flops | bytes accessed | tf_op | source)
XLA Modules:
  0.0 292.1 jit_solution(10043483166981917500)
XLA Ops:
  6.5 1.9 slice.51
  10.3 18.4 %slice_reduce_fusion = bf16[32,64,768]{2,1,0:T(8,128)(2,1)S(1)} fusion(bf16[32,64,2,768]{3,2,1,0:T(2,128)(2,1)} %param.12), kind=kLoop, calls=%fused_computation.1 | loop fusion | bytes 6291456 | tf_op jit(solution)/shard_map/slice | solution.py:157
  28.8 5.5 %reshape_squeeze.9 = bf16[32,64,8,96]{3,2,1,0:T(8,128)(2,1)} reshape(bf16[32,64,768]{2,1,0:T(8,128)(2,1)S(1)} %slice_reduce_fusion) | data formatting | bytes 6291456 | tf_op jit(solution)/shard_map/reshape;squeeze | solution.py:157
  34.3 5.6 %copy.36 = bf16[32,64,8,96]{3,1,2,0:T(8,128)(2,1)} copy(bf16[32,64,8,96]{3,2,1,0:T(8,128)(2,1)} %reshape_squeeze.9) | data formatting | bytes 6291456 | tf_op jit(solution)/shard_map/reshape;squeeze | solution.py:157
  40.6 10.3 %all-gather.9.cloned.1.call-done = bf16[3072,1,768]{2,0,1:T(8,128)(2,1)} async-done(((bf16[384,1,768]{2,0,1:T(8,128)(2,1)}), bf16[3072,1,768]{2,0,1:T(8,128)(2,1)}) %all-gather.9.cloned.1.call-update) | async-done | bytes 4718608 | tf_op jit(solution)/shard_map/all_gather | solution.py:149
  50.9 4.4 %fusion.7 = f32[256,768]{0,1:T(8,128)S(1)} fusion(bf16[3072,768]{1,0:T(8,128)(2,1)} %bitcast.51, bf16[256,3072]{1,0:T(8,128)(2,1)S(1)} %copy-done.1, f32[3072]{0:T(1024)S(1)} %convert_element_type.46, f32[256]{0:T(256)S(1)} %add_rsqrt_fusion), kind=kOutput, calls=%fused_computation.17 | convolution fusion | flops 1211105280 | bytes 7091200 | tf_op jit(solution)/shard_map/dot_general | solution.py:166
  56.0 1.4 constant_dynamic-update-slice_fusion.7
  57.6 1.5 collective-permute-start.1
  59.1 1.2 collective-permute-start.2
  60.3 1.5 collective-permute-start.3
  61.7 1.1 slice.56
  62.9 8.9 %slice.55 = bf16[32,64,1,768]{3,2,1,0:T(2,128)(2,1)} slice(bf16[32,64,2,768]{3,2,1,0:T(2,128)(2,1)} %param.12), slice={[0:32], [0:64], [1:2], [0:768]} | slice | bytes 6291456 | tf_op jit(solution)/shard_map/slice | solution.py:182
  71.7 15.4 %copy.27 = bf16[32,64,1,768]{1,3,0,2:T(8,128)(2,1)} copy(bf16[32,64,1,768]{3,2,1,0:T(2,128)(2,1)} %slice.55) | data formatting | bytes 6291456 | tf_op jit(solution)/shard_map/slice | solution.py:182
  87.1 1.5 collective-permute-start.5
  88.7 2.0 constant_dynamic-update-slice_fusion.6
  90.6 2.1 collective-permute-start.6
  92.8 1.9 constant_dynamic-update-slice_fusion.5
  96.9 8.4 %collective-permute-done.4 = bf16[8,4,64,96]{3,2,1,0:T(8,128)(2,1)S(1)} collective-permute-done((bf16[8,4,64,96]{3,2,1,0:T(8,128)(2,1)}, bf16[8,4,64,96]{3,2,1,0:T(8,128)(2,1)S(1)}, u32[]{:S(2)}, u32[]{:S(2)}) %collective-permute-start.4) | collective-permute-done | bytes 393248 | tf_op jit(solution)/shard_map/ppermute | solution.py:174
  110.0 37.9 %shard_map.82 = (f32[4,8,1,512]{3,2,1,0:T(1,128)}, f32[4,8,1,512]{3,2,1,0:T(1,128)}, f32[4,8,96,512]{3,2,1,0:T(8,128)}) custom-call(s32[32]{0:T(128)} %copy-done.5, s32[32]{0:T(128)} %get-tuple-element.51.base_ref, s32[32]{0:T(128)} %select_reduce_fusion.2.limit_ref, s32[4]{0:T(128)} %len_ref.3, s32[32]{0:T(128)} %get-tuple-element.53.slot_ref, ...), custom_call_target="tpu_custom_call" | custom-call | tf_op jit(solution)/shard_map/pallas_call | solution.py:121
  147.9 20.5 %all-gather.5.cloned.1.call-done = bf16[3072,2,768]{2,0,1:T(8,128)(2,1)} async-done(((bf16[384,2,768]{2,0,1:T(8,128)(2,1)}), bf16[3072,2,768]{2,0,1:T(8,128)(2,1)}) %all-gather.5.cloned.1.call-update) | async-done | bytes 9437200 | tf_op jit(solution)/shard_map/all_gather | solution.py:187
  168.4 5.4 %fusion.3 = f32[256,2,768]{2,0,1:T(8,128)S(1)} fusion(bf16[3072,2,768]{2,0,1:T(8,128)(2,1)} %all-gather.5.cloned.1.call-done, bf16[256,3072]{1,0:T(8,128)(2,1)S(1)} %copy-done.2, f32[3072]{0:T(1024)S(1)} %convert_element_type.46, f32[256]{0:T(256)S(1)} %add_rsqrt_fusion), kind=kOutput, calls=%fused_computation.10 | convolution fusion | flops 2419064832 | bytes 12596224 | tf_op jit(solution)/shard_map/tk,kcj->tcj/dot_general | solution.py:203
  176.0 1.3 copy.31
  178.9 11.9 %shard_map.83 = (f32[4,8,1,512]{3,2,1,0:T(1,128)}, f32[4,8,1,512]{3,2,1,0:T(1,128)}, f32[4,8,96,512]{3,2,1,0:T(8,128)}) custom-call(s32[4]{0:T(128)} %copy-done.7, s32[4]{0:T(128)} %copy-done.6, s32[4]{0:T(128)} %broadcast_13_limit_ref.2.limit_ref, s32[4]{0:T(128)} %len_ref.3, s32[32]{0:T(128)} %get-tuple-element.53.slot_ref, ...), custom_call_target="tpu_custom_call" | custom-call | tf_op jit(solution)/shard_map/pallas_call | solution.py:121
  191.6 1.5 fusion.9
  193.2 3.4 %all-to-all-start.1 = ((f32[8,8,2,256]{3,2,1,0:T(2,128)}), f32[8,8,2,256]{3,2,1,0:T(2,128)S(1)}, u32[]{:S(2)}, u32[]{:S(2)}) async-start(f32[8,8,2,256]{3,2,1,0:T(2,128)} %bitcast.13), calls=%async_computation.1 | async-start | bytes 262144 | tf_op jit(solution)/shard_map/all_to_all | solution.py:237
  196.5 3.3 %convert.30 = bf16[4,8,96,512]{3,2,1,0:T(8,128)(2,1)S(1)} convert(f32[4,8,96,512]{3,2,1,0:T(8,128)} %get-tuple-element.33) | non-fusion elementwise | flops 1572864 | bytes 9437184 | tf_op jit(solution)/shard_map/convert.3
  200.2 1.9 pad_maximum_fusion
  202.2 1.6 all-to-all-done.1
  203.7 3.6 %all-to-all-start = ((bf16[8,8,96,256]{3,2,1,0:T(8,128)(2,1)}), bf16[8,8,96,256]{3,2,1,0:T(8,128)(2,1)S(1)}, u32[]{:S(2)}, u32[]{:S(2)}) async-start(bf16[8,8,96,256]{3,2,1,0:T(8,128)(2,1)} %bitcast.12), calls=%async_computation | async-start | bytes 6291456 | tf_op jit(solution)/shard_map/all_to_all | solution.py:236
  207.7 37.5 %all-to-all-done = bf16[8,8,96,256]{3,2,1,0:T(8,128)(2,1)S(1)} async-done(((bf16[8,8,96,256]{3,2,1,0:T(8,128)(2,1)}), bf16[8,8,96,256]{3,2,1,0:T(8,128)(2,1)S(1)}, u32[]{:S(2)}, u32[]{:S(2)}) %all-to-all-start) | async-done | bytes 3145760 | tf_op jit(solution)/shard_map/all_to_all | solution.py:236
  246.0 4.9 %convolution_convert_fusion = bf16[256,3072]{1,0:T(8,128)(2,1)} fusion(bf16[256,768]{0,1:T(8,128)(2,1)S(1)} %bitcast.48, bf16[3072,768]{1,0:T(8,128)(2,1)} %all-gather.7.cloned.1.call-done), kind=kOutput, calls=%fused_computation.5 | convolution fusion | flops 1208745984 | bytes 6684672 | tf_op jit(solution)/shard_map/dot_general | solution.py:248
  251.0 34.5 %reduce-scatter.2.cloned.1.call-done = bf16[256,768]{1,0:T(8,128)(2,1)} async-done(((bf16[256,3072]{1,0:T(8,128)(2,1)}), bf16[256,768]{1,0:T(8,128)(2,1)}) %reduce-scatter.2.cloned.1.call-update) | async-done | bytes 393232 | tf_op jit(solution)/shard_map/reduce_scatter | solution.py:251
  (78 shorter events, 16.5 us)
Async XLA Ops:
  6.5 44.4 %all-gather.9.cloned.1.call-start = ((), (), s32[]{:S(2)}) async-start(), calls=%async_computation.6 | async-start | bytes 5308416 | tf_op jit(solution)/shard_map/all_gather | solution.py:149
  8.5 159.9 %all-gather.5.cloned.1.call-start = ((), (), s32[]{:S(2)}) async-start(), calls=%async_computation.3 | async-start | bytes 10616832 | tf_op jit(solution)/shard_map/all_gather | solution.py:187
  9.3 19.5 %copy-start.7 = (s32[4]{0:T(128)}, s32[4]{0:T(128)S(1)}, u32[]{:S(2)}) copy-start(s32[4]{0:T(128)S(1)} %get-tuple-element.41.req_ref) | copy-start | bytes 52
  10.1 18.6 %copy-start.6 = (s32[4]{0:T(128)}, s32[4]{0:T(128)S(1)}, u32[]{:S(2)}) copy-start(s32[4]{0:T(128)S(1)} %fusion.14.base_ref) | copy-start | bytes 52
  34.3 5.6 %copy-start.3 = (bf16[3072]{0:T(1024)(128)(2,1)S(1)}, bf16[3072]{0:T(1024)(128)(2,1)}, u32[]{:S(2)}) copy-start(bf16[3072]{0:T(1024)(128)(2,1)} %param.9) | copy-start | bytes 18436
  34.3 5.6 %copy-start.1 = (bf16[256,3072]{1,0:T(8,128)(2,1)S(1)}, bf16[256,3072]{1,0:T(8,128)(2,1)}, u32[]{:S(2)}) copy-start(bf16[256,3072]{1,0:T(8,128)(2,1)} %param.8) | copy-start | bytes 4718596
  55.3 6.5 %copy-start = (bf16[384,3,768]{2,0,1:T(8,128)(2,1)S(1)}, bf16[384,3,768]{2,0,1:T(8,128)(2,1)}, u32[]{:S(2)}) copy-start(bf16[384,3,768]{2,0,1:T(8,128)(2,1)} %param.10) | copy-start | bytes 5308420
  57.3 29.8 %collective-permute-start = (bf16[8,4,64,96]{3,2,1,0:T(8,128)(2,1)}, bf16[8,4,64,96]{3,2,1,0:T(8,128)(2,1)}, u32[]{:S(2)}, u32[]{:S(2)}) collective-permute-start(bf16[8,4,64,96]{3,2,1,0:T(8,128)(2,1)} %get-tuple-element.40), channel_id=1, source_target_pairs={{0,4},{4,8},{8,12},{12,16},{16,20},{20,24},{24,28},{28,0},{1,5},{5... | collective-permute-start | bytes 1179656 | tf_op jit(solution)/shard_map/ppermute | solution.py:174
  57.6 33.0 %collective-permute-start.1 = (bf16[8,4,64,96]{3,2,1,0:T(8,128)(2,1)}, bf16[8,4,64,96]{3,2,1,0:T(8,128)(2,1)}, u32[]{:S(2)}, u32[]{:S(2)}) collective-permute-start(bf16[8,4,64,96]{3,2,1,0:T(8,128)(2,1)} %get-tuple-element.40), channel_id=1, source_target_pairs={{0,8},{4,12},{8,16},{12,20},{16,24},{20,28},{24,0},{28,4},{1,9},{5... | collective-permute-start | bytes 1179656 | tf_op jit(solution)/shard_map/ppermute | solution.py:174
  59.1 36.0 %collective-permute-start.2 = (bf16[8,4,64,96]{3,2,1,0:T(8,128)(2,1)}, bf16[8,4,64,96]{3,2,1,0:T(8,128)(2,1)S(1)}, u32[]{:S(2)}, u32[]{:S(2)}) collective-permute-start(bf16[8,4,64,96]{3,2,1,0:T(8,128)(2,1)} %get-tuple-element.40), channel_id=1, source_target_pairs={{0,12},{4,16},{8,20},{12,24},{16,28},{20,0},{24,4},{28,8},{1,13},{... | collective-permute-start | bytes 1179656 | tf_op jit(solution)/shard_map/ppermute | solution.py:174
  60.3 35.7 %collective-permute-start.3 = (bf16[8,4,64,96]{3,2,1,0:T(8,128)(2,1)}, bf16[8,4,64,96]{3,2,1,0:T(8,128)(2,1)S(1)}, u32[]{:S(2)}, u32[]{:S(2)}) collective-permute-start(bf16[8,4,64,96]{3,2,1,0:T(8,128)(2,1)} %get-tuple-element.40), channel_id=1, source_target_pairs={{0,16},{4,20},{8,24},{12,28},{16,0},{20,4},{24,8},{28,12},{1,17},{... | collective-permute-start | bytes 1179656 | tf_op jit(solution)/shard_map/ppermute | solution.py:174
  62.8 42.5 %collective-permute-start.4 = (bf16[8,4,64,96]{3,2,1,0:T(8,128)(2,1)}, bf16[8,4,64,96]{3,2,1,0:T(8,128)(2,1)S(1)}, u32[]{:S(2)}, u32[]{:S(2)}) collective-permute-start(bf16[8,4,64,96]{3,2,1,0:T(8,128)(2,1)} %get-tuple-element.40), channel_id=1, source_target_pairs={{0,20},{4,24},{8,28},{12,0},{16,4},{20,8},{24,12},{28,16},{1,21},{... | collective-permute-start | bytes 1179656 | tf_op jit(solution)/shard_map/ppermute | solution.py:174
  87.1 19.1 %collective-permute-start.5 = (bf16[8,4,64,96]{3,2,1,0:T(8,128)(2,1)}, bf16[8,4,64,96]{3,2,1,0:T(8,128)(2,1)S(1)}, u32[]{:S(2)}, u32[]{:S(2)}) collective-permute-start(bf16[8,4,64,96]{3,2,1,0:T(8,128)(2,1)} %get-tuple-element.40), channel_id=1, source_target_pairs={{0,24},{4,28},{8,0},{12,4},{16,8},{20,12},{24,16},{28,20},{1,25},{... | collective-permute-start | bytes 1179656 | tf_op jit(solution)/shard_map/ppermute | solution.py:174
  88.7 19.8 %copy-start.9 = (s32[32]{0:T(128)S(1)}, s32[32]{0:T(128)}, u32[]{:S(2)}) copy-start(s32[32]{0:T(128)} %param.14) | copy-start | bytes 388
  88.7 19.9 %copy-start.8 = (s32[256]{0:T(256)S(1)}, s32[256]{0:T(256)}, u32[]{:S(2)}) copy-start(s32[256]{0:T(256)} %param.15) | copy-start | bytes 3076
  88.7 20.7 %copy-start.4 = (s32[4]{0:T(128)S(1)}, s32[4]{0:T(128)}, u32[]{:S(2)}) copy-start(s32[4]{0:T(128)} %len_ref.3) | copy-start | bytes 52
  90.6 16.6 %collective-permute-start.6 = (bf16[8,4,64,96]{3,2,1,0:T(8,128)(2,1)}, bf16[8,4,64,96]{3,2,1,0:T(8,128)(2,1)S(1)}, u32[]{:S(2)}, u32[]{:S(2)}) collective-permute-start(bf16[8,4,64,96]{3,2,1,0:T(8,128)(2,1)} %get-tuple-element.40), channel_id=1, source_target_pairs={{0,28},{4,0},{8,4},{12,8},{16,12},{20,16},{24,20},{28,24},{1,29},{... | collective-permute-start | bytes 1179656 | tf_op jit(solution)/shard_map/ppermute | solution.py:174
  108.2 137.9 %all-gather.7.cloned.1.call-start = ((), (), s32[]{:S(2)}) async-start(), calls=%async_computation.4 | async-start | bytes 5308416 | tf_op jit(solution)/shard_map/all_gather | solution.py:201
  109.3 0.7 copy-start.5
  110.0 58.4 %copy-start.2 = (bf16[256,3072]{1,0:T(8,128)(2,1)S(1)}, bf16[256,3072]{1,0:T(8,128)(2,1)}, u32[]{:S(2)}) copy-start(bf16[256,3072]{1,0:T(8,128)(2,1)} %param.8) | copy-start | bytes 4718596
  193.2 10.6 %all-to-all-start.1 = ((f32[8,8,2,256]{3,2,1,0:T(2,128)}), f32[8,8,2,256]{3,2,1,0:T(2,128)S(1)}, u32[]{:S(2)}, u32[]{:S(2)}) async-start(f32[8,8,2,256]{3,2,1,0:T(2,128)} %bitcast.13), calls=%async_computation.1 | async-start | bytes 262144 | tf_op jit(solution)/shard_map/all_to_all | solution.py:237
  203.7 41.5 %all-to-all-start = ((bf16[8,8,96,256]{3,2,1,0:T(8,128)(2,1)}), bf16[8,8,96,256]{3,2,1,0:T(8,128)(2,1)S(1)}, u32[]{:S(2)}, u32[]{:S(2)}) async-start(bf16[8,8,96,256]{3,2,1,0:T(8,128)(2,1)} %bitcast.12), calls=%async_computation | async-start | bytes 6291456 | tf_op jit(solution)/shard_map/all_to_all | solution.py:236
  207.4 78.2 %reduce-scatter.2.cloned.1.call-start = ((), (), s32[]{:S(2)}) async-start(), calls=%async_computation.5 | async-start | bytes 1966080 | tf_op jit(solution)/shard_map/reduce_scatter | solution.py:251
Sparse Core Ops, SparseCore 0:
  9.2 41.6 all-gather.8
  108.3 60.0 all-gather.4
  170.3 40.3 all-gather.6
  251.1 34.3 reduce-scatter.1

commit v8 on v4

--- a/solution.py
+++ b/solution.py
@@ -34,10 +34,11 @@
     return jnp.sum(jnp.where(matches, small_table, 0), axis=-1)
 
 
-def attend_kernel(carry_in):
+def attend_kernel(carry_in, out_rows):
     def kernel(req_ref, base_ref, limit_ref, len_ref, slot_ref, *refs):
         if carry_in:
-            q_ref, k_ref, v_ref, m0_ref, l0_ref, o0_ref, m_ref, l_ref, o_ref = refs
+            (q_ref, k_ref, v_ref, m0_ref, l0_ref, o0_ref,
+             num_ref, stats_ref, m_ref, l_ref, o_ref) = refs
         else:
             q_ref, k_ref, v_ref, m_ref, l_ref, o_ref = refs
         step = pl.program_id(0)
@@ -76,7 +77,8 @@
         masked = jnp.where(allowed, scores, negative)
         m_old = m_ref[req]
         m_new = jnp.maximum(m_old, jnp.max(masked, axis=1, keepdims=True))
-        exp_terms = jnp.where(allowed, jnp.exp(masked - m_new), 0.0)
+        shift = jnp.where(m_new == negative, 0.0, m_new)
+        exp_terms = jnp.exp(masked - shift)
         alpha = jnp.exp(m_old - m_new)
         l_ref[req] = alpha * l_ref[req] + jnp.sum(exp_terms, axis=1, keepdims=True)
         weighted = jnp.einsum(
@@ -86,11 +88,23 @@
         o_ref[req] = alpha * o_ref[req] + weighted
         m_ref[req] = m_new
 
+        if carry_in:
+            @pl.when(step == pl.num_programs(0) - 1)
+            def _():
+                split = q_len // out_rows
+                for r in range(len_ref.shape[0]):
+                    for c in range(split):
+                        cols = pl.ds(c * out_rows, out_rows)
+                        num_ref[r * split + c] = o_ref[r, :, :, cols].astype(jnp.bfloat16)
+                        stats_ref[r * split + c, :, 0:1] = m_ref[r, :, :, cols]
+                        stats_ref[r * split + c, :, 1:2] = l_ref[r, :, :, cols]
+
     return kernel
 
 
 def attend_blocks(
-    queries, keys, vals_t, blk_req, blk_base, blk_limit, lengths, slot_of, carry=None
+    queries, keys, vals_t, blk_req, blk_base, blk_limit, lengths, slot_of,
+    carry=None, out_rows=None,
 ):
     head_count, _, blk_len, head_dim = queries.shape
     req_count = lengths.shape[0]
@@ -104,27 +118,37 @@
         pl.BlockSpec((1, head_count, head_dim, blk_len), lambda j, *_: (j, 0, 0, 0)),
     ]
     args = [queries, keys, vals_t]
-    if carry is not None:
+    acc_shapes = (
+        ((req_count, head_count, 1, q_len), jnp.float32),
+        ((req_count, head_count, 1, q_len), jnp.float32),
+        ((req_count, head_count, head_dim, q_len), jnp.float32),
+    )
+    if carry is None:
+        out_shape = tuple(jax.ShapeDtypeStruct(*a) for a in acc_shapes)
+        out_specs = (whole, whole, whole)
+        scratch = ()
+    else:
         in_specs += [whole, whole, whole]
         args += list(carry)
-    out_shape = (
-        jax.ShapeDtypeStruct((req_count, head_count, 1, q_len), jnp.float32),
-        jax.ShapeDtypeStruct((req_count, head_count, 1, q_len), jnp.float32),
-        jax.ShapeDtypeStruct((req_count, head_count, head_dim, q_len), jnp.float32),
-    )
+        groups = req_count * q_len // out_rows
+        out_shape = (
+            jax.ShapeDtypeStruct((groups, head_count, head_dim, out_rows), jnp.bfloat16),
+            jax.ShapeDtypeStruct((groups, head_count, 2, out_rows), jnp.float32),
+        )
+        out_specs = (whole, whole)
+        scratch = tuple(pltpu.VMEM(*a) for a in acc_shapes)
     grid_spec = pltpu.PrefetchScalarGridSpec(
         num_scalar_prefetch=5,
         grid=(blk_count,),
         in_specs=in_specs,
-        out_specs=(whole, whole, whole),
+        out_specs=out_specs,
+        scratch_shapes=scratch,
     )
     return pl.pallas_call(
-        attend_kernel(carry is not None),
+        attend_kernel(carry is not None, out_rows),
         out_shape=out_shape,
         grid_spec=grid_spec,
-        compiler_params=pltpu.CompilerParams(
-            dimension_semantics=("arbitrary",)
-        ),
+        compiler_params=pltpu.CompilerParams(dimension_semantics=("arbitrary",)),
     )(blk_req, blk_base, blk_limit, lengths, slot_of, *args)
 
 
@@ -200,7 +224,7 @@
     )
     vals_new = kv_proj[:, 1].astype(jnp.bfloat16).reshape(slot_count, blk_len, head_count, HD)
     new_limit = jnp.full((slot_count,), beyond, jnp.int32)
-    head_max, head_den, head_num = attend_blocks(
+    sent_num, sent_stats = attend_blocks(
         q_heads,
         jnp.transpose(keys_new, (0, 2, 1, 3)),
         jnp.transpose(vals_new, (0, 2, 3, 1)),
@@ -210,21 +234,9 @@
         lengths,
         slot_of,
         carry=carry,
-    )
-
-    split = fresh_len // tok_rows
-    sent_num = (
-        head_num.reshape(req_count, head_count, HD, split, tok_rows)
-        .transpose(0, 3, 1, 2, 4)
-        .reshape(wide_count, head_count, HD, tok_rows)
-        .astype(jnp.bfloat16)
-    )
-    stats = jnp.concatenate([head_max, head_den], axis=2)
-    sent_stats = (
-        stats.reshape(req_count, head_count, 2, split, tok_rows)
-        .transpose(0, 3, 1, 2, 4)
-        .reshape(wide_count, head_count, 2, tok_rows)
-    )
+        out_rows=tok_rows,
+    )
+
     got_num = lax.all_to_all(sent_num, "wide", split_axis=0, concat_axis=0, tiled=True)
     got_stats = lax.all_to_all(sent_stats, "wide", split_axis=0, concat_axis=0, tiled=True)
     got_max = got_stats[:, :, 0:1]

time: 280 us -> 278 us (level)
  blocking collectives: 0 us -> 10.5 us
  other arithmetic: 15.4 us -> 7.8 us
  starting transfers between devices: 7.37 us -> 4 us
    all_to_all x0 -> x1, blocking collectives: none -> 10.5 us  [body(): lax.all_to_all(sent_stats, 'wide', split_axis=0, concat_axis=0, tiled=True)]
    another operation x4 -> x2, other arithmetic: 5.03 us -> 0.23 us
    all_to_all x1 -> x0, starting transfers between devices: 3.37 us -> none  [body(): lax.all_to_all(sent_stats, 'wide', split_axis=0, concat_axis=0, tiled=True)]
  transfers between devices with their start and end apart: 7 -> 6, of which waited for: 6 -> 5; matrix products, arithmetic and copies ran while one was open for 28% -> 26% of each run, Pallas kernels for 18% -> 17%
where the time goes in v8:
time: 278 us; the launch traced here: 277 us
  waiting for transfers between devices  117 us (42%)
  local copies, waits for them, and re-layouts  61.5 us (22%)
  Pallas kernels  47.4 us (17%)
  matrix products  14.7 us (5%)
  between operations  13.4 us (5%)
  blocking collectives  10.5 us (4%)
  other arithmetic  7.8 us (3%)
  starting transfers between devices  4 us (1%)
    pallas_call x2, Pallas kernels, attend_blocks(): pl.pallas_call(attend_kernel(carry is not None, out_rows), out_shape=out_...  47.4 us
    all_to_all x1, waiting for transfers between devices, body(): lax.all_to_all(sent_num, 'wide', split_axis=0, concat_axis=0, tiled=True)  39 us
    reduce_scatter x1, waiting for transfers between devices, body(): lax.psum_scatter(out_part.astype(jnp.bfloat16), 'narrow', scatter_dimensi...  34.5 us
    slice x2, local copies, waits for them, and re-layouts, body(): cache_v[:, :, 1].reshape(cache_count, blk_len, head_count, HD)  24.4 us
    all_gather x1, waiting for transfers between devices, body(): w_kv = lax.all_gather(w_kv_local, 'wide', axis=0, tiled=True)  22.1 us
    slice x1, local copies, waits for them, and re-layouts, body(): cache[:, :, 0].reshape(cache_count, blk_len, head_count, HD)  18.4 us
    all_gather x1, waiting for transfers between devices, body(): all_queries = lax.all_gather(queries, 'wide', axis=1, tiled=True)  11.3 us
    another operation x2, local copies, waits for them, and re-layouts, body(): cache[:, :, 0].reshape(cache_count, blk_len, head_count, HD)  11.1 us
  transfers between devices with their start and end apart: 6, of which 5 were waited for; matrix products, arithmetic and copies ran while one was open for 26% of the time, Pallas kernels for 17%

profile of v8, /device:TPU:0, one launch (start us, length us, event | category | flops | bytes accessed | tf_op | source)
XLA Modules:
  0.0 276.7 jit_solution(17741986275805867280)
XLA Ops:
  6.5 2.0 slice.37
  8.6 0.7 and_select_fusion.3
  9.3 0.8 select_reduce_fusion.3
  10.3 18.4 %slice_reduce_fusion = bf16[32,64,768]{2,1,0:T(8,128)(2,1)S(1)} fusion(bf16[32,64,2,768]{3,2,1,0:T(2,128)(2,1)} %param.12), kind=kLoop, calls=%fused_computation.1 | loop fusion | bytes 6291456 | tf_op jit(solution)/shard_map/slice | solution.py:181
  28.8 5.5 %reshape_squeeze.9 = bf16[32,64,8,96]{3,2,1,0:T(8,128)(2,1)} reshape(bf16[32,64,768]{2,1,0:T(8,128)(2,1)S(1)} %slice_reduce_fusion) | data formatting | bytes 6291456 | tf_op jit(solution)/shard_map/reshape;squeeze | solution.py:181
  34.3 5.6 %copy.36 = bf16[32,64,8,96]{3,1,2,0:T(8,128)(2,1)} copy(bf16[32,64,8,96]{3,2,1,0:T(8,128)(2,1)} %reshape_squeeze.9) | data formatting | bytes 6291456 | tf_op jit(solution)/shard_map/reshape;squeeze | solution.py:181
  39.9 0.4 fusion
  40.6 10.3 %all-gather.12.cloned.1.call-done = bf16[3072,1,768]{2,0,1:T(8,128)(2,1)} async-done(((bf16[384,1,768]{2,0,1:T(8,128)(2,1)}), bf16[3072,1,768]{2,0,1:T(8,128)(2,1)}) %all-gather.12.cloned.1.call-update) | async-done | bytes 4718608 | tf_op jit(solution)/shard_map/all_gather | solution.py:173
  50.9 4.4 %fusion.7 = f32[256,768]{0,1:T(8,128)S(1)} fusion(bf16[3072,768]{1,0:T(8,128)(2,1)} %bitcast.48, bf16[256,3072]{1,0:T(8,128)(2,1)S(1)} %copy-done.1, f32[3072]{0:T(1024)S(1)} %convert_element_type.40, f32[256]{0:T(256)S(1)} %add_rsqrt_fusion), kind=kOutput, calls=%fused_computation.16 | convolution fusion | flops 1211105280 | bytes 7091200 | tf_op jit(solution)/shard_map/dot_general | solution.py:190
  56.0 1.1 maximum_bitcast_fusion
  57.2 1.1 slice.42
  58.3 8.9 %slice.41 = bf16[32,64,1,768]{3,2,1,0:T(2,128)(2,1)} slice(bf16[32,64,2,768]{3,2,1,0:T(2,128)(2,1)} %param.12), slice={[0:32], [0:64], [1:2], [0:768]} | slice | bytes 6291456 | tf_op jit(solution)/shard_map/slice | solution.py:200
  67.2 15.5 %copy.27 = bf16[32,64,1,768]{1,3,0,2:T(8,128)(2,1)} copy(bf16[32,64,1,768]{3,2,1,0:T(2,128)(2,1)} %slice.41) | data formatting | bytes 6291456 | tf_op jit(solution)/shard_map/slice | solution.py:200
  82.7 11.3 %all-gather.6.cloned.1.call-done.refs_0_ = bf16[8,32,64,96]{3,2,1,0:T(8,128)(2,1)} async-done(((bf16[8,4,64,96]{3,2,1,0:T(8,128)(2,1)}), bf16[8,32,64,96]{3,2,1,0:T(8,128)(2,1)}) %all-gather.6.cloned.1.call-update) | async-done | bytes 3145744 | tf_op jit(solution)/shard_map/all_gather | solution.py:197
  94.3 0.7 select_reduce_fusion.1.slot_ref
  95.1 0.5 fusion.12
  95.7 0.6 select_reduce_fusion.2.limit_ref
  96.3 36.3 %shard_map.82 = (f32[4,8,1,512]{3,2,1,0:T(1,128)}, f32[4,8,1,512]{3,2,1,0:T(1,128)}, f32[4,8,96,512]{3,2,1,0:T(8,128)}) custom-call(s32[32]{0:T(128)} %copy-done.8, s32[32]{0:T(128)} %get-tuple-element.45.base_ref, s32[32]{0:T(128)} %select_reduce_fusion.2.limit_ref, s32[4]{0:T(128)} %len_ref.3, s32[32]{0:T(128)} %select_reduce_fusion.1.slot_ref, ...), custom_call_target="tpu_custom_call" | custom-call | tf_op jit(solution)/shard_map/pallas_call | solution.py:147
  132.7 22.1 %all-gather.8.cloned.1.call-done = bf16[3072,2,768]{2,0,1:T(8,128)(2,1)} async-done(((bf16[384,2,768]{2,0,1:T(8,128)(2,1)}), bf16[3072,2,768]{2,0,1:T(8,128)(2,1)}) %all-gather.8.cloned.1.call-update) | async-done | bytes 9437200 | tf_op jit(solution)/shard_map/all_gather | solution.py:205
  154.8 5.4 %fusion.3 = f32[256,2,768]{2,0,1:T(8,128)S(1)} fusion(bf16[3072,2,768]{2,0,1:T(8,128)(2,1)} %all-gather.8.cloned.1.call-done, bf16[256,3072]{1,0:T(8,128)(2,1)S(1)} %copy-done.2, f32[3072]{0:T(1024)S(1)} %convert_element_type.40, f32[256]{0:T(256)S(1)} %add_rsqrt_fusion), kind=kOutput, calls=%fused_computation.9 | convolution fusion | flops 2419064832 | bytes 12596224 | tf_op jit(solution)/shard_map/tk,kcj->tcj/dot_general | solution.py:219
  161.4 0.4 copy.30
  161.8 0.6 convert_element_type.44
  162.3 1.2 copy.31
  163.6 1.1 maximum_bitcast_fusion.1.refs_1_
  164.7 0.5 broadcast_13_limit_ref.2.limit_ref
  165.2 11.1 %shard_map.83 = (bf16[8,8,96,256]{3,2,1,0:T(8,128)(2,1)}, f32[8,8,2,256]{3,2,1,0:T(2,128)}) custom-call(s32[4]{0:T(128)} %copy-done.6, s32[4]{0:T(128)} %copy-done.5, s32[4]{0:T(128)} %broadcast_13_limit_ref.2.limit_ref, s32[4]{0:T(128)} %len_ref.3, s32[32]{0:T(128)} %select_reduce_fusion.1.slot_ref, ...), custom_call_target="tpu_custom_call" | custom-call | tf_op jit(solution)/shard_map/pallas_call | solution.py:147
  176.3 10.5 %all_to_all.10 = f32[8,8,2,256]{3,2,1,0:T(2,128)S(1)} all-to-all(f32[8,8,2,256]{3,2,1,0:T(2,128)} %get-tuple-element.33), channel_id=1, replica_groups=mesh['wide'=8,'narrow'=4] {'wide'}, dimensions={0} | all-to-all | bytes 262144 | tf_op jit(solution)/shard_map/all_to_all | solution.py:241
  186.8 3.6 %all-to-all-start = ((bf16[8,8,96,256]{3,2,1,0:T(8,128)(2,1)}), bf16[8,8,96,256]{3,2,1,0:T(8,128)(2,1)S(1)}, u32[]{:S(2)}, u32[]{:S(2)}) async-start(bf16[8,8,96,256]{3,2,1,0:T(8,128)(2,1)} %get-tuple-element.32), calls=%async_computation | async-start | bytes 6291456 | tf_op jit(solution)/shard_map/all_to_all | solution.py:240
  190.7 39.0 %all-to-all-done = bf16[8,8,96,256]{3,2,1,0:T(8,128)(2,1)S(1)} async-done(((bf16[8,8,96,256]{3,2,1,0:T(8,128)(2,1)}), bf16[8,8,96,256]{3,2,1,0:T(8,128)(2,1)S(1)}, u32[]{:S(2)}, u32[]{:S(2)}) %all-to-all-start) | async-done | bytes 3145760 | tf_op jit(solution)/shard_map/all_to_all | solution.py:240
  229.8 0.7 multiply_reduce_fusion
  230.6 4.9 %convolution_convert_fusion = bf16[256,3072]{1,0:T(8,128)(2,1)} fusion(bf16[256,768]{0,1:T(8,128)(2,1)S(1)} %bitcast.45, bf16[3072,768]{1,0:T(8,128)(2,1)} %all-gather.10.cloned.1.call-done), kind=kOutput, calls=%fused_computation.5 | convolution fusion | flops 1208745984 | bytes 6684672 | tf_op jit(solution)/shard_map/dot_general | solution.py:252
  235.6 34.5 %reduce-scatter.2.cloned.1.call-done = bf16[256,768]{1,0:T(8,128)(2,1)} async-done(((bf16[256,3072]{1,0:T(8,128)(2,1)}), bf16[256,768]{1,0:T(8,128)(2,1)}) %reduce-scatter.2.cloned.1.call-update) | async-done | bytes 393232 | tf_op jit(solution)/shard_map/reduce_scatter | solution.py:255
  (54 shorter events, 3.3 us)
Async XLA Ops:
  6.5 44.4 %all-gather.12.cloned.1.call-start = ((), (), s32[]{:S(2)}) async-start(), calls=%async_computation.7 | async-start | bytes 5308416 | tf_op jit(solution)/shard_map/all_gather | solution.py:173
  8.5 85.5 %all-gather.6.cloned.1.call-start = ((), (), s32[]{:S(2)}) async-start(), calls=%async_computation.3 | async-start | bytes 4718592 | tf_op jit(solution)/shard_map/all_gather | solution.py:197
  9.3 19.5 %copy-start.6 = (s32[4]{0:T(128)}, s32[4]{0:T(128)S(1)}, u32[]{:S(2)}) copy-start(s32[4]{0:T(128)S(1)} %get-tuple-element.37.req_ref) | copy-start | bytes 52
  10.2 18.6 %copy-start.5 = (s32[4]{0:T(128)}, s32[4]{0:T(128)S(1)}, u32[]{:S(2)}) copy-start(s32[4]{0:T(128)S(1)} %fusion.11.base_ref) | copy-start | bytes 52
  34.3 5.6 %copy-start.3 = (bf16[3072]{0:T(1024)(128)(2,1)S(1)}, bf16[3072]{0:T(1024)(128)(2,1)}, u32[]{:S(2)}) copy-start(bf16[3072]{0:T(1024)(128)(2,1)} %param.9) | copy-start | bytes 18436
  34.3 5.6 %copy-start.1 = (bf16[256,3072]{1,0:T(8,128)(2,1)S(1)}, bf16[256,3072]{1,0:T(8,128)(2,1)}, u32[]{:S(2)}) copy-start(bf16[256,3072]{1,0:T(8,128)(2,1)} %param.8) | copy-start | bytes 4718596
  55.3 1.9 copy-start
  57.1 97.6 %all-gather.8.cloned.1.call-start = ((), (), s32[]{:S(2)}) async-start(), calls=%async_computation.4 | async-start | bytes 10616832 | tf_op jit(solution)/shard_map/all_gather | solution.py:205
  67.2 27.1 %copy-start.9 = (s32[32]{0:T(128)S(1)}, s32[32]{0:T(128)}, u32[]{:S(2)}) copy-start(s32[32]{0:T(128)} %param.14) | copy-start | bytes 388
  67.2 27.8 %copy-start.7 = (s32[256]{0:T(256)S(1)}, s32[256]{0:T(256)}, u32[]{:S(2)}) copy-start(s32[256]{0:T(256)} %param.15) | copy-start | bytes 3076
  67.2 28.5 %copy-start.4 = (s32[4]{0:T(128)S(1)}, s32[4]{0:T(128)}, u32[]{:S(2)}) copy-start(s32[4]{0:T(128)} %len_ref.3) | copy-start | bytes 52
  94.0 136.6 %all-gather.10.cloned.1.call-start = ((), (), s32[]{:S(2)}) async-start(), calls=%async_computation.5 | async-start | bytes 5308416 | tf_op jit(solution)/shard_map/all_gather | solution.py:217
  95.7 0.6 copy-start.8
  96.3 58.5 %copy-start.2 = (bf16[256,3072]{1,0:T(8,128)(2,1)S(1)}, bf16[256,3072]{1,0:T(8,128)(2,1)}, u32[]{:S(2)}) copy-start(bf16[256,3072]{1,0:T(8,128)(2,1)} %param.8) | copy-start | bytes 4718596
  186.8 43.0 %all-to-all-start = ((bf16[8,8,96,256]{3,2,1,0:T(8,128)(2,1)}), bf16[8,8,96,256]{3,2,1,0:T(8,128)(2,1)S(1)}, u32[]{:S(2)}, u32[]{:S(2)}) async-start(bf16[8,8,96,256]{3,2,1,0:T(8,128)(2,1)} %get-tuple-element.32), calls=%async_computation | async-start | bytes 6291456 | tf_op jit(solution)/shard_map/all_to_all | solution.py:240
  190.5 79.7 %reduce-scatter.2.cloned.1.call-start = ((), (), s32[]{:S(2)}) async-start(), calls=%async_computation.6 | async-start | bytes 1966080 | tf_op jit(solution)/shard_map/reduce_scatter | solution.py:255
Sparse Core Ops, SparseCore 0:
  9.2 41.6 all-gather.11
  57.2 36.7 all-gather.5
  95.9 58.8 all-gather.7
  156.5 41.8 all-gather.9
  235.7 34.3 reduce-scatter.1

commit v9 on v8

--- a/solution.py
+++ b/solution.py
@@ -237,8 +237,25 @@
         out_rows=tok_rows,
     )
 
-    got_num = lax.all_to_all(sent_num, "wide", split_axis=0, concat_axis=0, tiled=True)
-    got_stats = lax.all_to_all(sent_stats, "wide", split_axis=0, concat_axis=0, tiled=True)
+    parts = []
+    rest = sent_stats
+    for _ in range(3):
+        part = rest.astype(jnp.bfloat16)
+        parts.append(part)
+        rest = rest - part.astype(jnp.float32)
+    pad_rows = (-(HD + 6)) % 8
+    packed = jnp.concatenate(
+        [sent_num] + parts
+        + [jnp.zeros(sent_num.shape[:2] + (pad_rows,) + sent_num.shape[3:], jnp.bfloat16)],
+        axis=2,
+    )
+    got = lax.all_to_all(packed, "wide", split_axis=0, concat_axis=0, tiled=True)
+    got_num = got[:, :, :HD]
+    got_stats = (
+        got[:, :, HD:HD + 2].astype(jnp.float32)
+        + got[:, :, HD + 2:HD + 4].astype(jnp.float32)
+        + got[:, :, HD + 4:HD + 6].astype(jnp.float32)
+    )
     got_max = got_stats[:, :, 0:1]
     got_den = got_stats[:, :, 1:2]
     top_max = jnp.max(got_max, axis=0)

time: 278 us -> 283 us (1.018)
  waiting for transfers between devices: 117 us -> 78.4 us
  blocking collectives: 10.5 us -> 43.2 us
  local copies, waits for them, and re-layouts: 61.5 us -> 74.8 us
  starting transfers between devices: 4 us -> 0.35 us
    all_to_all x1 -> x0, waiting for transfers between devices: 39 us -> none  [body(): lax.all_to_all(sent_num, 'wide', split_axis=0, concat_axis=0, tiled=True)]
    all_to_all x1, blocking collectives: 10.5 us -> 43.2 us  [body(): lax.all_to_all(packed, 'wide', split_axis=0, concat_axis=0, tiled=True)]
    concatenate x0 -> x1, local copies, waits for them, and re-layouts: none -> 12.6 us  [body(): jnp.concatenate([sent_num] + parts + [jnp.zeros(sent_num.shape[:2] + (pad...]
    all_to_all x1 -> x0, starting transfers between devices: 3.65 us -> none  [body(): lax.all_to_all(sent_num, 'wide', split_axis=0, concat_axis=0, tiled=True)]
  transfers between devices with their start and end apart: 6 -> 5, of which waited for: 5 -> 4; matrix products, arithmetic and copies ran while one was open for 26% -> 30% of each run, Pallas kernels for 17% -> 17%
where the time goes in v9:
time: 283 us; the launch traced here: 282 us
  waiting for transfers between devices  78.4 us (28%)
  local copies, waits for them, and re-layouts  74.8 us (26%)
  Pallas kernels  47.4 us (17%)
  blocking collectives  43.2 us (15%)
  matrix products  14.7 us (5%)
  between operations  13.4 us (5%)
  other arithmetic  9.57 us (3%)
    pallas_call x2, Pallas kernels, attend_blocks(): pl.pallas_call(attend_kernel(carry is not None, out_rows), out_shape=out_...  47.4 us
    all_to_all x1, blocking collectives, body(): lax.all_to_all(packed, 'wide', split_axis=0, concat_axis=0, tiled=True)  43.2 us
    reduce_scatter x1, waiting for transfers between devices, body(): lax.psum_scatter(out_part.astype(jnp.bfloat16), 'narrow', scatter_dimensi...  34.5 us
    slice x2, local copies, waits for them, and re-layouts, body(): cache_v[:, :, 1].reshape(cache_count, blk_len, head_count, HD)  24.4 us
    all_gather x1, waiting for transfers between devices, body(): w_kv = lax.all_gather(w_kv_local, 'wide', axis=0, tiled=True)  22.1 us
    slice x1, local copies, waits for them, and re-layouts, body(): cache[:, :, 0].reshape(cache_count, blk_len, head_count, HD)  18.4 us
    concatenate x1, local copies, waits for them, and re-layouts, body(): jnp.concatenate([sent_num] + parts + [jnp.zeros(sent_num.shape[:2] + (pad...  12.6 us
    all_gather x1, waiting for transfers between devices, body(): all_queries = lax.all_gather(queries, 'wide', axis=1, tiled=True)  11.4 us
  transfers between devices with their start and end apart: 5, of which 4 were waited for; matrix products, arithmetic and copies ran while one was open for 30% of the time, Pallas kernels for 17%

profile of v9, /device:TPU:0, one launch (start us, length us, event | category | flops | bytes accessed | tf_op | source)
XLA Modules:
  0.0 281.8 jit_solution(14526560620132004376)
XLA Ops:
  6.5 2.0 slice.49
  8.6 0.7 and_select_fusion.3
  9.3 0.8 select_reduce_fusion.3
  10.3 18.4 %slice_reduce_fusion = bf16[32,64,768]{2,1,0:T(8,128)(2,1)S(1)} fusion(bf16[32,64,2,768]{3,2,1,0:T(2,128)(2,1)} %param.12), kind=kLoop, calls=%fused_computation.1 | loop fusion | bytes 6291456 | tf_op jit(solution)/shard_map/slice | solution.py:181
  28.8 5.5 %reshape_squeeze.9 = bf16[32,64,8,96]{3,2,1,0:T(8,128)(2,1)} reshape(bf16[32,64,768]{2,1,0:T(8,128)(2,1)S(1)} %slice_reduce_fusion) | data formatting | bytes 6291456 | tf_op jit(solution)/shard_map/reshape;squeeze | solution.py:181
  34.3 5.6 %copy.36 = bf16[32,64,8,96]{3,1,2,0:T(8,128)(2,1)} copy(bf16[32,64,8,96]{3,2,1,0:T(8,128)(2,1)} %reshape_squeeze.9) | data formatting | bytes 6291456 | tf_op jit(solution)/shard_map/reshape;squeeze | solution.py:181
  39.9 0.4 fusion
  40.6 10.3 %all-gather.12.cloned.1.call-done = bf16[3072,1,768]{2,0,1:T(8,128)(2,1)} async-done(((bf16[384,1,768]{2,0,1:T(8,128)(2,1)}), bf16[3072,1,768]{2,0,1:T(8,128)(2,1)}) %all-gather.12.cloned.1.call-update) | async-done | bytes 4718608 | tf_op jit(solution)/shard_map/all_gather | solution.py:173
  50.9 4.4 %fusion.7 = f32[256,768]{0,1:T(8,128)S(1)} fusion(bf16[3072,768]{1,0:T(8,128)(2,1)} %bitcast.48, bf16[256,3072]{1,0:T(8,128)(2,1)S(1)} %copy-done.1, f32[3072]{0:T(1024)S(1)} %convert_element_type.64, f32[256]{0:T(256)S(1)} %add_rsqrt_fusion), kind=kOutput, calls=%fused_computation.16 | convolution fusion | flops 1211105280 | bytes 7091200 | tf_op jit(solution)/shard_map/dot_general | solution.py:190
  56.0 1.1 maximum_bitcast_fusion
  57.2 1.1 slice.54
  58.3 8.8 %slice.53 = bf16[32,64,1,768]{3,2,1,0:T(2,128)(2,1)} slice(bf16[32,64,2,768]{3,2,1,0:T(2,128)(2,1)} %param.12), slice={[0:32], [0:64], [1:2], [0:768]} | slice | bytes 6291456 | tf_op jit(solution)/shard_map/slice | solution.py:200
  67.1 15.5 %copy.27 = bf16[32,64,1,768]{1,3,0,2:T(8,128)(2,1)} copy(bf16[32,64,1,768]{3,2,1,0:T(2,128)(2,1)} %slice.53) | data formatting | bytes 6291456 | tf_op jit(solution)/shard_map/slice | solution.py:200
  82.6 11.4 %all-gather.6.cloned.1.call-done.refs_0_ = bf16[8,32,64,96]{3,2,1,0:T(8,128)(2,1)} async-done(((bf16[8,4,64,96]{3,2,1,0:T(8,128)(2,1)}), bf16[8,32,64,96]{3,2,1,0:T(8,128)(2,1)}) %all-gather.6.cloned.1.call-update) | async-done | bytes 3145744 | tf_op jit(solution)/shard_map/all_gather | solution.py:197
  94.1 0.6 select_reduce_fusion.1.slot_ref
  94.9 0.5 fusion.13
  95.5 0.6 select_reduce_fusion.2.limit_ref
  96.1 36.4 %shard_map.82 = (f32[4,8,1,512]{3,2,1,0:T(1,128)}, f32[4,8,1,512]{3,2,1,0:T(1,128)}, f32[4,8,96,512]{3,2,1,0:T(8,128)}) custom-call(s32[32]{0:T(128)} %copy-done.8, s32[32]{0:T(128)} %get-tuple-element.48.base_ref, s32[32]{0:T(128)} %select_reduce_fusion.2.limit_ref, s32[4]{0:T(128)} %len_ref.3, s32[32]{0:T(128)} %select_reduce_fusion.1.slot_ref, ...), custom_call_target="tpu_custom_call" | custom-call | tf_op jit(solution)/shard_map/pallas_call | solution.py:147
  132.7 22.1 %all-gather.8.cloned.1.call-done = bf16[3072,2,768]{2,0,1:T(8,128)(2,1)} async-done(((bf16[384,2,768]{2,0,1:T(8,128)(2,1)}), bf16[3072,2,768]{2,0,1:T(8,128)(2,1)}) %all-gather.8.cloned.1.call-update) | async-done | bytes 9437200 | tf_op jit(solution)/shard_map/all_gather | solution.py:205
  154.8 5.4 %fusion.3 = f32[256,2,768]{2,0,1:T(8,128)S(1)} fusion(bf16[3072,2,768]{2,0,1:T(8,128)(2,1)} %all-gather.8.cloned.1.call-done, bf16[256,3072]{1,0:T(8,128)(2,1)S(1)} %copy-done.2, f32[3072]{0:T(1024)S(1)} %convert_element_type.64, f32[256]{0:T(256)S(1)} %add_rsqrt_fusion), kind=kOutput, calls=%fused_computation.9 | convolution fusion | flops 2419064832 | bytes 12596224 | tf_op jit(solution)/shard_map/tk,kcj->tcj/dot_general | solution.py:219
  161.8 0.6 convert_element_type.68
  162.3 1.2 copy.31
  163.6 1.1 maximum_bitcast_fusion.1.refs_1_
  164.7 0.6 broadcast_13_limit_ref.2.limit_ref
  165.3 11.1 %shard_map.83 = (bf16[8,8,96,256]{3,2,1,0:T(8,128)(2,1)}, f32[8,8,2,256]{3,2,1,0:T(2,128)}) custom-call(s32[4]{0:T(128)} %copy-done.6, s32[4]{0:T(128)} %copy-done.5, s32[4]{0:T(128)} %broadcast_13_limit_ref.2.limit_ref, s32[4]{0:T(128)} %len_ref.3, s32[32]{0:T(128)} %select_reduce_fusion.1.slot_ref, ...), custom_call_target="tpu_custom_call" | custom-call | tf_op jit(solution)/shard_map/pallas_call | solution.py:147
  176.4 1.7 subtract_convert_fusion.2
  178.1 0.7 broadcast_in_dim.74
  178.7 12.6 %concatenate.27 = bf16[8,8,104,256]{3,2,1,0:T(8,128)(2,1)S(1)} concatenate(bf16[8,8,96,256]{3,2,1,0:T(8,128)(2,1)} %get-tuple-element.32, bf16[8,8,2,256]{3,2,1,0:T(2,128)(2,1)} %get-tuple-element.45, bf16[8,8,2,256]{3,2,1,0:T(2,128)(2,1)S(1)} %get-tuple-element.44, bf16[8,8,2,256]{3,2,1,0:T(2,128)(2,1)S(1)} %get-tuple-element.43, bf16[8,8,2,256]{3,2,1,0:T(2,128)(2,1)} %broadcast_in_dim.74), dimensions={2} | concatenate | bytes 6815744 | tf_op jit(solution)/shard_map/concatenate | solution.py:247
  191.4 43.2 %all_to_all.5 = bf16[8,8,104,256]{3,2,1,0:T(8,128)(2,1)S(1)} all-to-all(bf16[8,8,104,256]{3,2,1,0:T(8,128)(2,1)S(1)} %concatenate.27), channel_id=1, replica_groups=mesh['wide'=8,'narrow'=4] {'wide'}, dimensions={0} | all-to-all | bytes 6815744 | tf_op jit(solution)/shard_map/all_to_all | solution.py:252
  235.0 0.7 multiply_reduce_fusion
  235.8 4.9 %convolution_convert_fusion = bf16[256,3072]{1,0:T(8,128)(2,1)} fusion(bf16[256,768]{0,1:T(8,128)(2,1)S(1)} %bitcast.45, bf16[3072,768]{1,0:T(8,128)(2,1)} %all-gather.10.cloned.1.call-done), kind=kOutput, calls=%fused_computation.5 | convolution fusion | flops 1208745984 | bytes 6684672 | tf_op jit(solution)/shard_map/dot_general | solution.py:269
  240.7 34.5 %reduce-scatter.2.cloned.1.call-done = bf16[256,768]{1,0:T(8,128)(2,1)} async-done(((bf16[256,3072]{1,0:T(8,128)(2,1)}), bf16[256,768]{1,0:T(8,128)(2,1)}) %reduce-scatter.2.cloned.1.call-update) | async-done | bytes 393232 | tf_op jit(solution)/shard_map/reduce_scatter | solution.py:272
  (56 shorter events, 3.8 us)
Async XLA Ops:
  6.5 44.4 %all-gather.12.cloned.1.call-start = ((), (), s32[]{:S(2)}) async-start(), calls=%async_computation.6 | async-start | bytes 5308416 | tf_op jit(solution)/shard_map/all_gather | solution.py:173
  8.5 85.5 %all-gather.6.cloned.1.call-start = ((), (), s32[]{:S(2)}) async-start(), calls=%async_computation.2 | async-start | bytes 4718592 | tf_op jit(solution)/shard_map/all_gather | solution.py:197
  9.3 19.5 %copy-start.6 = (s32[4]{0:T(128)}, s32[4]{0:T(128)S(1)}, u32[]{:S(2)}) copy-start(s32[4]{0:T(128)S(1)} %get-tuple-element.37.req_ref) | copy-start | bytes 52
  10.2 18.6 %copy-start.5 = (s32[4]{0:T(128)}, s32[4]{0:T(128)S(1)}, u32[]{:S(2)}) copy-start(s32[4]{0:T(128)S(1)} %fusion.12.base_ref) | copy-start | bytes 52
  34.3 5.6 %copy-start.3 = (bf16[3072]{0:T(1024)(128)(2,1)S(1)}, bf16[3072]{0:T(1024)(128)(2,1)}, u32[]{:S(2)}) copy-start(bf16[3072]{0:T(1024)(128)(2,1)} %param.9) | copy-start | bytes 18436
  34.3 5.6 %copy-start.1 = (bf16[256,3072]{1,0:T(8,128)(2,1)S(1)}, bf16[256,3072]{1,0:T(8,128)(2,1)}, u32[]{:S(2)}) copy-start(bf16[256,3072]{1,0:T(8,128)(2,1)} %param.8) | copy-start | bytes 4718596
  55.3 1.9 copy-start
  57.1 97.6 %all-gather.8.cloned.1.call-start = ((), (), s32[]{:S(2)}) async-start(), calls=%async_computation.3 | async-start | bytes 10616832 | tf_op jit(solution)/shard_map/all_gather | solution.py:205
  67.1 27.0 %copy-start.9 = (s32[32]{0:T(128)S(1)}, s32[32]{0:T(128)}, u32[]{:S(2)}) copy-start(s32[32]{0:T(128)} %param.14) | copy-start | bytes 388
  67.1 27.6 %copy-start.7 = (s32[256]{0:T(256)S(1)}, s32[256]{0:T(256)}, u32[]{:S(2)}) copy-start(s32[256]{0:T(256)} %param.15) | copy-start | bytes 3076
  67.1 28.4 %copy-start.4 = (s32[4]{0:T(128)S(1)}, s32[4]{0:T(128)}, u32[]{:S(2)}) copy-start(s32[4]{0:T(128)} %len_ref.3) | copy-start | bytes 52
  94.0 141.7 %all-gather.10.cloned.1.call-start = ((), (), s32[]{:S(2)}) async-start(), calls=%async_computation.4 | async-start | bytes 5308416 | tf_op jit(solution)/shard_map/all_gather | solution.py:217
  95.5 0.6 copy-start.8
  96.1 58.7 %copy-start.2 = (bf16[256,3072]{1,0:T(8,128)(2,1)S(1)}, bf16[256,3072]{1,0:T(8,128)(2,1)}, u32[]{:S(2)}) copy-start(bf16[256,3072]{1,0:T(8,128)(2,1)} %param.8) | copy-start | bytes 4718596
  132.5 142.8 %reduce-scatter.2.cloned.1.call-start = ((), (), s32[]{:S(2)}) async-start(), calls=%async_computation.5 | async-start | bytes 1966080 | tf_op jit(solution)/shard_map/reduce_scatter | solution.py:272
Sparse Core Ops, SparseCore 0:
  9.2 41.6 all-gather.11
  57.2 36.7 all-gather.5
  95.9 58.8 all-gather.7
  156.5 39.2 all-gather.9
  240.9 34.3 reduce-scatter.1

commit v10 on v8

--- a/solution.py
+++ b/solution.py
@@ -38,7 +38,7 @@
     def kernel(req_ref, base_ref, limit_ref, len_ref, slot_ref, *refs):
         if carry_in:
             (q_ref, k_ref, v_ref, m0_ref, l0_ref, o0_ref,
-             num_ref, stats_ref, m_ref, l_ref, o_ref) = refs
+             num_ref, m_ref, l_ref, o_ref) = refs
         else:
             q_ref, k_ref, v_ref, m_ref, l_ref, o_ref = refs
         step = pl.program_id(0)
@@ -92,12 +92,25 @@
             @pl.when(step == pl.num_programs(0) - 1)
             def _():
                 split = q_len // out_rows
+                head_dim = o_ref.shape[2]
                 for r in range(len_ref.shape[0]):
                     for c in range(split):
                         cols = pl.ds(c * out_rows, out_rows)
-                        num_ref[r * split + c] = o_ref[r, :, :, cols].astype(jnp.bfloat16)
-                        stats_ref[r * split + c, :, 0:1] = m_ref[r, :, :, cols]
-                        stats_ref[r * split + c, :, 1:2] = l_ref[r, :, :, cols]
+                        group = r * split + c
+                        num_ref[group, :, 0:head_dim] = o_ref[r, :, :, cols].astype(jnp.bfloat16)
+                        pieces = []
+                        for stat in (m_ref[r, :, :, cols], l_ref[r, :, :, cols]):
+                            rest = stat
+                            for _ in range(3):
+                                part = rest.astype(jnp.bfloat16).astype(jnp.float32)
+                                pieces.append(part)
+                                rest = rest - part
+                        shape = (pieces[0].shape[0], 8, out_rows)
+                        row = lax.broadcasted_iota(jnp.int32, shape, 1)
+                        tail = jnp.zeros(shape, jnp.float32)
+                        for index, piece in enumerate(pieces):
+                            tail = jnp.where(row == index, piece, tail)
+                        num_ref[group, :, head_dim:head_dim + 8] = tail.astype(jnp.bfloat16)
 
     return kernel
 
@@ -131,11 +144,10 @@
         in_specs += [whole, whole, whole]
         args += list(carry)
         groups = req_count * q_len // out_rows
-        out_shape = (
-            jax.ShapeDtypeStruct((groups, head_count, head_dim, out_rows), jnp.bfloat16),
-            jax.ShapeDtypeStruct((groups, head_count, 2, out_rows), jnp.float32),
-        )
-        out_specs = (whole, whole)
+        out_shape = jax.ShapeDtypeStruct(
+            (groups, head_count, head_dim + 8, out_rows), jnp.bfloat16
+        )
+        out_specs = whole
         scratch = tuple(pltpu.VMEM(*a) for a in acc_shapes)
     grid_spec = pltpu.PrefetchScalarGridSpec(
         num_scalar_prefetch=5,
@@ -224,7 +236,7 @@
     )
     vals_new = kv_proj[:, 1].astype(jnp.bfloat16).reshape(slot_count, blk_len, head_count, HD)
     new_limit = jnp.full((slot_count,), beyond, jnp.int32)
-    sent_num, sent_stats = attend_blocks(
+    packed = attend_blocks(
         q_heads,
         jnp.transpose(keys_new, (0, 2, 1, 3)),
         jnp.transpose(vals_new, (0, 2, 3, 1)),
@@ -237,10 +249,11 @@
         out_rows=tok_rows,
     )
 
-    got_num = lax.all_to_all(sent_num, "wide", split_axis=0, concat_axis=0, tiled=True)
-    got_stats = lax.all_to_all(sent_stats, "wide", split_axis=0, concat_axis=0, tiled=True)
-    got_max = got_stats[:, :, 0:1]
-    got_den = got_stats[:, :, 1:2]
+    got = lax.all_to_all(packed, "wide", split_axis=0, concat_axis=0, tiled=True)
+    got_num = got[:, :, :HD]
+    tail = got[:, :, HD:HD + 6].astype(jnp.float32)
+    got_max = tail[:, :, 0:1] + tail[:, :, 1:2] + tail[:, :, 2:3]
+    got_den = tail[:, :, 3:4] + tail[:, :, 4:5] + tail[:, :, 5:6]
     top_max = jnp.max(got_max, axis=0)
     factor = jnp.exp(got_max - top_max[None])
     num_own = jnp.sum(got_num.astype(jnp.float32) * factor, axis=0)

time: 278 us -> 280 us (level)
  blocking collectives: 10.5 us -> 54.3 us
  waiting for transfers between devices: 117 us -> 78.3 us
  starting transfers between devices: 4 us -> 0.35 us
    all_to_all x1, blocking collectives: 10.5 us -> 54.3 us  [body(): lax.all_to_all(packed, 'wide', split_axis=0, concat_axis=0, tiled=True)]
    all_to_all x1 -> x0, waiting for transfers between devices: 39 us -> none  [body(): lax.all_to_all(sent_num, 'wide', split_axis=0, concat_axis=0, tiled=True)]
    all_to_all x1 -> x0, starting transfers between devices: 3.65 us -> none  [body(): lax.all_to_all(sent_num, 'wide', split_axis=0, concat_axis=0, tiled=True)]
  transfers between devices with their start and end apart: 6 -> 5, of which waited for: 5 -> 4; matrix products, arithmetic and copies ran while one was open for 26% -> 26% of each run, Pallas kernels for 17% -> 17%
where the time goes in v10:
time: 280 us; the launch traced here: 278 us
  waiting for transfers between devices  78.3 us (28%)
  local copies, waits for them, and re-layouts  61.3 us (22%)
  blocking collectives  54.3 us (19%)
  Pallas kernels  48 us (17%)
  matrix products  14.7 us (5%)
  between operations  13.4 us (5%)
  other arithmetic  8.09 us (3%)
    all_to_all x1, blocking collectives, body(): lax.all_to_all(packed, 'wide', split_axis=0, concat_axis=0, tiled=True)  54.3 us
    pallas_call x2, Pallas kernels, attend_blocks(): pl.pallas_call(attend_kernel(carry is not None, out_rows), out_shape=out_...  48 us
    reduce_scatter x1, waiting for transfers between devices, body(): lax.psum_scatter(out_part.astype(jnp.bfloat16), 'narrow', scatter_dimensi...  34.5 us
    slice x2, local copies, waits for them, and re-layouts, body(): cache_v[:, :, 1].reshape(cache_count, blk_len, head_count, HD)  24.3 us
    all_gather x1, waiting for transfers between devices, body(): w_kv = lax.all_gather(w_kv_local, 'wide', axis=0, tiled=True)  21.9 us
    slice x1, local copies, waits for them, and re-layouts, body(): cache[:, :, 0].reshape(cache_count, blk_len, head_count, HD)  18.4 us
    all_gather x1, waiting for transfers between devices, body(): all_queries = lax.all_gather(queries, 'wide', axis=1, tiled=True)  11.4 us
    another operation x2, local copies, waits for them, and re-layouts, body(): cache[:, :, 0].reshape(cache_count, blk_len, head_count, HD)  11.1 us
  transfers between devices with their start and end apart: 5, of which 4 were waited for; matrix products, arithmetic and copies ran while one was open for 26% of the time, Pallas kernels for 17%

profile of v10, /device:TPU:0, one launch (start us, length us, event | category | flops | bytes accessed | tf_op | source)
XLA Modules:
  0.0 278.5 jit_solution(13883413056271199995)
XLA Ops:
  6.5 2.0 slice.55
  8.6 0.7 and_select_fusion.3
  9.3 0.8 select_reduce_fusion.3
  10.3 18.4 %slice_reduce_fusion = bf16[32,64,768]{2,1,0:T(8,128)(2,1)S(1)} fusion(bf16[32,64,2,768]{3,2,1,0:T(2,128)(2,1)} %param.12), kind=kLoop, calls=%fused_computation.1 | loop fusion | bytes 6291456 | tf_op jit(solution)/shard_map/slice | solution.py:193
  28.8 5.5 %reshape_squeeze.9 = bf16[32,64,8,96]{3,2,1,0:T(8,128)(2,1)} reshape(bf16[32,64,768]{2,1,0:T(8,128)(2,1)S(1)} %slice_reduce_fusion) | data formatting | bytes 6291456 | tf_op jit(solution)/shard_map/reshape;squeeze | solution.py:193
  34.3 5.6 %copy.36 = bf16[32,64,8,96]{3,1,2,0:T(8,128)(2,1)} copy(bf16[32,64,8,96]{3,2,1,0:T(8,128)(2,1)} %reshape_squeeze.9) | data formatting | bytes 6291456 | tf_op jit(solution)/shard_map/reshape;squeeze | solution.py:193
  39.9 0.4 fusion
  40.6 10.3 %all-gather.12.cloned.1.call-done = bf16[3072,1,768]{2,0,1:T(8,128)(2,1)} async-done(((bf16[384,1,768]{2,0,1:T(8,128)(2,1)}), bf16[3072,1,768]{2,0,1:T(8,128)(2,1)}) %all-gather.12.cloned.1.call-update) | async-done | bytes 4718608 | tf_op jit(solution)/shard_map/all_gather | solution.py:185
  50.9 4.4 %fusion.7 = f32[256,768]{0,1:T(8,128)S(1)} fusion(bf16[3072,768]{1,0:T(8,128)(2,1)} %bitcast.48, bf16[256,3072]{1,0:T(8,128)(2,1)S(1)} %copy-done.1, f32[3072]{0:T(1024)S(1)} %convert_element_type.43, f32[256]{0:T(256)S(1)} %add_rsqrt_fusion), kind=kOutput, calls=%fused_computation.16 | convolution fusion | flops 1211105280 | bytes 7091200 | tf_op jit(solution)/shard_map/dot_general | solution.py:202
  55.7 0.3 copy.26
  56.0 1.1 maximum_bitcast_fusion
  57.2 1.1 slice.60
  58.3 8.8 %slice.59 = bf16[32,64,1,768]{3,2,1,0:T(2,128)(2,1)} slice(bf16[32,64,2,768]{3,2,1,0:T(2,128)(2,1)} %param.12), slice={[0:32], [0:64], [1:2], [0:768]} | slice | bytes 6291456 | tf_op jit(solution)/shard_map/slice | solution.py:212
  67.1 15.5 %copy.27 = bf16[32,64,1,768]{1,3,0,2:T(8,128)(2,1)} copy(bf16[32,64,1,768]{3,2,1,0:T(2,128)(2,1)} %slice.59) | data formatting | bytes 6291456 | tf_op jit(solution)/shard_map/slice | solution.py:212
  82.6 11.4 %all-gather.6.cloned.1.call-done.refs_0_ = bf16[8,32,64,96]{3,2,1,0:T(8,128)(2,1)} async-done(((bf16[8,4,64,96]{3,2,1,0:T(8,128)(2,1)}), bf16[8,32,64,96]{3,2,1,0:T(8,128)(2,1)}) %all-gather.6.cloned.1.call-update) | async-done | bytes 3145744 | tf_op jit(solution)/shard_map/all_gather | solution.py:209
  94.1 0.7 select_reduce_fusion.1.slot_ref
  95.0 0.6 fusion.13
  95.6 0.6 select_reduce_fusion.2.limit_ref
  96.2 36.3 %shard_map.82 = (f32[4,8,1,512]{3,2,1,0:T(1,128)}, f32[4,8,1,512]{3,2,1,0:T(1,128)}, f32[4,8,96,512]{3,2,1,0:T(8,128)}) custom-call(s32[32]{0:T(128)} %copy-done.8, s32[32]{0:T(128)} %get-tuple-element.43.base_ref, s32[32]{0:T(128)} %select_reduce_fusion.2.limit_ref, s32[4]{0:T(128)} %len_ref.3, s32[32]{0:T(128)} %select_reduce_fusion.1.slot_ref, ...), custom_call_target="tpu_custom_call" | custom-call | tf_op jit(solution)/shard_map/pallas_call | solution.py:159
  132.8 21.9 %all-gather.8.cloned.1.call-done = bf16[3072,2,768]{2,0,1:T(8,128)(2,1)} async-done(((bf16[384,2,768]{2,0,1:T(8,128)(2,1)}), bf16[3072,2,768]{2,0,1:T(8,128)(2,1)}) %all-gather.8.cloned.1.call-update) | async-done | bytes 9437200 | tf_op jit(solution)/shard_map/all_gather | solution.py:217
  154.7 5.4 %fusion.3 = f32[256,2,768]{2,0,1:T(8,128)S(1)} fusion(bf16[3072,2,768]{2,0,1:T(8,128)(2,1)} %all-gather.8.cloned.1.call-done, bf16[256,3072]{1,0:T(8,128)(2,1)S(1)} %copy-done.2, f32[3072]{0:T(1024)S(1)} %convert_element_type.43, f32[256]{0:T(256)S(1)} %add_rsqrt_fusion), kind=kOutput, calls=%fused_computation.9 | convolution fusion | flops 2419064832 | bytes 12596224 | tf_op jit(solution)/shard_map/tk,kcj->tcj/dot_general | solution.py:231
  160.8 0.3 copy.29
  161.4 0.4 copy.30
  161.7 0.6 convert_element_type.47
  162.3 1.2 copy.31
  163.6 1.1 maximum_bitcast_fusion.1.refs_1_
  164.6 0.5 broadcast_13_limit_ref.2.limit_ref
  165.1 11.7 %shard_map.83 = bf16[8,8,104,256]{3,2,1,0:T(8,128)(2,1)} custom-call(s32[4]{0:T(128)} %copy-done.6, s32[4]{0:T(128)} %copy-done.5, s32[4]{0:T(128)} %broadcast_13_limit_ref.2.limit_ref, s32[4]{0:T(128)} %len_ref.3, s32[32]{0:T(128)} %select_reduce_fusion.1.slot_ref, bf16[8,32,64,96]{3,2,1,0:T(8,128)(2,1)} %all-gather.6.cloned.1.call-done.refs_0_, ...), custom_call_target="tpu_custom_call" | custom-call | tf_op jit(solution)/shard_map/pallas_call | solution.py:159
  176.8 54.3 %all_to_all.5 = bf16[8,8,104,256]{3,2,1,0:T(8,128)(2,1)S(1)} all-to-all(bf16[8,8,104,256]{3,2,1,0:T(8,128)(2,1)} %shard_map.83), channel_id=1, replica_groups=mesh['wide'=8,'narrow'=4] {'wide'}, dimensions={0} | all-to-all | bytes 6815744 | tf_op jit(solution)/shard_map/all_to_all | solution.py:252
  231.6 0.7 multiply_reduce_fusion
  232.4 5.0 %convolution_convert_fusion = bf16[256,3072]{1,0:T(8,128)(2,1)} fusion(bf16[256,768]{0,1:T(8,128)(2,1)S(1)} %bitcast.45, bf16[3072,768]{1,0:T(8,128)(2,1)} %all-gather.10.cloned.1.call-done), kind=kOutput, calls=%fused_computation.5 | convolution fusion | flops 1208745984 | bytes 6684672 | tf_op jit(solution)/shard_map/dot_general | solution.py:265
  237.4 34.5 %reduce-scatter.2.cloned.1.call-done = bf16[256,768]{1,0:T(8,128)(2,1)} async-done(((bf16[256,3072]{1,0:T(8,128)(2,1)}), bf16[256,768]{1,0:T(8,128)(2,1)}) %reduce-scatter.2.cloned.1.call-update) | async-done | bytes 393232 | tf_op jit(solution)/shard_map/reduce_scatter | solution.py:268
  (53 shorter events, 2.9 us)
Async XLA Ops:
  6.5 44.4 %all-gather.12.cloned.1.call-start = ((), (), s32[]{:S(2)}) async-start(), calls=%async_computation.6 | async-start | bytes 5308416 | tf_op jit(solution)/shard_map/all_gather | solution.py:185
  8.5 85.4 %all-gather.6.cloned.1.call-start = ((), (), s32[]{:S(2)}) async-start(), calls=%async_computation.2 | async-start | bytes 4718592 | tf_op jit(solution)/shard_map/all_gather | solution.py:209
  9.3 19.5 %copy-start.6 = (s32[4]{0:T(128)}, s32[4]{0:T(128)S(1)}, u32[]{:S(2)}) copy-start(s32[4]{0:T(128)S(1)} %get-tuple-element.35.req_ref) | copy-start | bytes 52
  10.2 18.6 %copy-start.5 = (s32[4]{0:T(128)}, s32[4]{0:T(128)S(1)}, u32[]{:S(2)}) copy-start(s32[4]{0:T(128)S(1)} %fusion.12.base_ref) | copy-start | bytes 52
  34.3 5.6 %copy-start.3 = (bf16[3072]{0:T(1024)(128)(2,1)S(1)}, bf16[3072]{0:T(1024)(128)(2,1)}, u32[]{:S(2)}) copy-start(bf16[3072]{0:T(1024)(128)(2,1)} %param.9) | copy-start | bytes 18436
  34.3 5.6 %copy-start.1 = (bf16[256,3072]{1,0:T(8,128)(2,1)S(1)}, bf16[256,3072]{1,0:T(8,128)(2,1)}, u32[]{:S(2)}) copy-start(bf16[256,3072]{1,0:T(8,128)(2,1)} %param.8) | copy-start | bytes 4718596
  55.3 1.9 copy-start
  57.1 97.6 %all-gather.8.cloned.1.call-start = ((), (), s32[]{:S(2)}) async-start(), calls=%async_computation.3 | async-start | bytes 10616832 | tf_op jit(solution)/shard_map/all_gather | solution.py:217
  67.1 27.0 %copy-start.9 = (s32[32]{0:T(128)S(1)}, s32[32]{0:T(128)}, u32[]{:S(2)}) copy-start(s32[32]{0:T(128)} %param.14) | copy-start | bytes 388
  67.1 27.7 %copy-start.7 = (s32[256]{0:T(256)S(1)}, s32[256]{0:T(256)}, u32[]{:S(2)}) copy-start(s32[256]{0:T(256)} %param.15) | copy-start | bytes 3076
  67.1 28.5 %copy-start.4 = (s32[4]{0:T(128)S(1)}, s32[4]{0:T(128)}, u32[]{:S(2)}) copy-start(s32[4]{0:T(128)} %len_ref.3) | copy-start | bytes 52
  94.0 138.4 %all-gather.10.cloned.1.call-start = ((), (), s32[]{:S(2)}) async-start(), calls=%async_computation.4 | async-start | bytes 5308416 | tf_op jit(solution)/shard_map/all_gather | solution.py:229
  95.6 0.7 copy-start.8
  96.2 58.5 %copy-start.2 = (bf16[256,3072]{1,0:T(8,128)(2,1)S(1)}, bf16[256,3072]{1,0:T(8,128)(2,1)}, u32[]{:S(2)}) copy-start(bf16[256,3072]{1,0:T(8,128)(2,1)} %param.8) | copy-start | bytes 4718596
  132.6 139.4 %reduce-scatter.2.cloned.1.call-start = ((), (), s32[]{:S(2)}) async-start(), calls=%async_computation.5 | async-start | bytes 1966080 | tf_op jit(solution)/shard_map/reduce_scatter | solution.py:268
Sparse Core Ops, SparseCore 0:
  9.2 41.6 all-gather.11
  57.2 36.7 all-gather.5
  95.9 58.8 all-gather.7
  156.5 57.4 all-gather.9
  237.5 34.3 reduce-scatter.1

commit v11 on v8

--- a/solution.py
+++ b/solution.py
@@ -238,7 +238,8 @@
     )
 
     got_num = lax.all_to_all(sent_num, "wide", split_axis=0, concat_axis=0, tiled=True)
-    got_stats = lax.all_to_all(sent_stats, "wide", split_axis=0, concat_axis=0, tiled=True)
+    all_stats = lax.all_gather(sent_stats, "wide", axis=0, tiled=False)
+    got_stats = lax.dynamic_index_in_dim(all_stats, wide_index, axis=1, keepdims=False)
     got_max = got_stats[:, :, 0:1]
     got_den = got_stats[:, :, 1:2]
     top_max = jnp.max(got_max, axis=0)

time: 278 us -> 309 us (1.11)
  waiting for transfers between devices: 117 us -> 156 us
  blocking collectives: 10.5 us -> 0 us
    all_gather x1, waiting for transfers between devices: 0.02 us -> 35.1 us  [body(): part_out = lax.all_gather(w_out_local, 'wide', axis=0, tiled=True)]
    all_gather x0 -> x1, waiting for transfers between devices: none -> 29.7 us  [body(): all_stats = lax.all_gather(sent_stats, 'wide', axis=0, tiled=False)]
    all_to_all x1, waiting for transfers between devices: 39 us -> 11.3 us  [body(): lax.all_to_all(sent_num, 'wide', split_axis=0, concat_axis=0, tiled=True)]
    all_to_all x1 -> x0, blocking collectives: 10.5 us -> none  [body(): lax.all_to_all(sent_stats, 'wide', split_axis=0, concat_axis=0, tiled=True)]
  transfers between devices with their start and end apart: 6 -> 7, of which waited for: 5 -> 7; matrix products, arithmetic and copies ran while one was open for 26% -> 20% of each run, Pallas kernels for 17% -> 12%
where the time goes in v11:
time: 309 us; the launch traced here: 307 us
  waiting for transfers between devices  156 us (50%)
  local copies, waits for them, and re-layouts  64 us (21%)
  Pallas kernels  47.4 us (15%)
  matrix products  14.7 us (5%)
  between operations  13.7 us (4%)
  other arithmetic  7.68 us (2%)
  starting transfers between devices  4.05 us (1%)
    pallas_call x2, Pallas kernels, attend_blocks(): pl.pallas_call(attend_kernel(carry is not None, out_rows), out_shape=out_...  47.4 us
    reduce_scatter x1, waiting for transfers between devices, body(): lax.psum_scatter(out_part.astype(jnp.bfloat16), 'narrow', scatter_dimensi...  35.4 us
    all_gather x1, waiting for transfers between devices, body(): part_out = lax.all_gather(w_out_local, 'wide', axis=0, tiled=True)  35.1 us
    all_gather x1, waiting for transfers between devices, body(): all_stats = lax.all_gather(sent_stats, 'wide', axis=0, tiled=False)  29.7 us
    slice x2, local copies, waits for them, and re-layouts, body(): cache_v[:, :, 1].reshape(cache_count, blk_len, head_count, HD)  24.4 us
    all_gather x1, waiting for transfers between devices, body(): w_kv = lax.all_gather(w_kv_local, 'wide', axis=0, tiled=True)  22.2 us
    slice x1, local copies, waits for them, and re-layouts, body(): cache[:, :, 0].reshape(cache_count, blk_len, head_count, HD)  18.4 us
    all_to_all x1, waiting for transfers between devices, body(): lax.all_to_all(sent_num, 'wide', split_axis=0, concat_axis=0, tiled=True)  11.3 us
  transfers between devices with their start and end apart: 7, of which 7 were waited for; matrix products, arithmetic and copies ran while one was open for 20% of the time, Pallas kernels for 12%

profile of v11, /device:TPU:0, one launch (start us, length us, event | category | flops | bytes accessed | tf_op | source)
XLA Modules:
  0.0 307.5 jit_solution(9397334002588088730)
XLA Ops:
  6.5 2.0 slice.37
  8.6 0.7 and_select_fusion.3
  9.3 0.8 select_reduce_fusion.3
  10.3 18.4 %slice_reduce_fusion = bf16[32,64,768]{2,1,0:T(8,128)(2,1)S(1)} fusion(bf16[32,64,2,768]{3,2,1,0:T(2,128)(2,1)} %param.12), kind=kLoop, calls=%fused_computation.1 | loop fusion | bytes 6291456 | tf_op jit(solution)/shard_map/slice | solution.py:181
  28.8 5.5 %reshape_squeeze.9 = bf16[32,64,8,96]{3,2,1,0:T(8,128)(2,1)} reshape(bf16[32,64,768]{2,1,0:T(8,128)(2,1)S(1)} %slice_reduce_fusion) | data formatting | bytes 6291456 | tf_op jit(solution)/shard_map/reshape;squeeze | solution.py:181
  34.3 5.6 %copy.46 = bf16[32,64,8,96]{3,1,2,0:T(8,128)(2,1)} copy(bf16[32,64,8,96]{3,2,1,0:T(8,128)(2,1)} %reshape_squeeze.9) | data formatting | bytes 6291456 | tf_op jit(solution)/shard_map/reshape;squeeze | solution.py:181
  40.6 10.3 %all-gather.14.cloned.1.call-done = bf16[3072,1,768]{2,0,1:T(8,128)(2,1)} async-done(((bf16[384,1,768]{2,0,1:T(8,128)(2,1)}), bf16[3072,1,768]{2,0,1:T(8,128)(2,1)}) %all-gather.14.cloned.1.call-update) | async-done | bytes 4718608 | tf_op jit(solution)/shard_map/all_gather | solution.py:173
  50.9 4.4 %fusion.7 = f32[256,768]{0,1:T(8,128)S(1)} fusion(bf16[3072,768]{1,0:T(8,128)(2,1)} %bitcast.50, bf16[256,3072]{1,0:T(8,128)(2,1)S(1)} %copy-done.1, f32[3072]{0:T(1024)S(1)} %convert_element_type.40, f32[256]{0:T(256)S(1)} %add_rsqrt_fusion), kind=kOutput, calls=%fused_computation.16 | convolution fusion | flops 1211105280 | bytes 7091200 | tf_op jit(solution)/shard_map/dot_general | solution.py:190
  56.0 1.1 maximum_bitcast_fusion
  57.2 1.1 slice.42
  58.3 8.9 %slice.41 = bf16[32,64,1,768]{3,2,1,0:T(2,128)(2,1)} slice(bf16[32,64,2,768]{3,2,1,0:T(2,128)(2,1)} %param.12), slice={[0:32], [0:64], [1:2], [0:768]} | slice | bytes 6291456 | tf_op jit(solution)/shard_map/slice | solution.py:200
  67.2 15.5 %copy.38 = bf16[32,64,1,768]{1,3,0,2:T(8,128)(2,1)} copy(bf16[32,64,1,768]{3,2,1,0:T(2,128)(2,1)} %slice.41) | data formatting | bytes 6291456 | tf_op jit(solution)/shard_map/slice | solution.py:200
  82.7 11.3 %all-gather.8.cloned.1.call-done.refs_0_ = bf16[8,32,64,96]{3,2,1,0:T(8,128)(2,1)} async-done(((bf16[8,4,64,96]{3,2,1,0:T(8,128)(2,1)}), bf16[8,32,64,96]{3,2,1,0:T(8,128)(2,1)}) %all-gather.8.cloned.1.call-update) | async-done | bytes 3145744 | tf_op jit(solution)/shard_map/all_gather | solution.py:197
  94.3 0.6 select_reduce_fusion.1.slot_ref
  95.6 0.7 select_reduce_fusion.2.limit_ref
  96.3 36.3 %shard_map.82 = (f32[4,8,1,512]{3,2,1,0:T(1,128)}, f32[4,8,1,512]{3,2,1,0:T(1,128)}, f32[4,8,96,512]{3,2,1,0:T(8,128)}) custom-call(s32[32]{0:T(128)} %copy-done.8, s32[32]{0:T(128)} %get-tuple-element.45.base_ref, s32[32]{0:T(128)} %select_reduce_fusion.2.limit_ref, s32[4]{0:T(128)} %len_ref.3, s32[32]{0:T(128)} %select_reduce_fusion.1.slot_ref, ...), custom_call_target="tpu_custom_call" | custom-call | tf_op jit(solution)/shard_map/pallas_call | solution.py:147
  132.6 22.2 %all-gather.10.cloned.1.call-done = bf16[3072,2,768]{2,0,1:T(8,128)(2,1)} async-done(((bf16[384,2,768]{2,0,1:T(8,128)(2,1)}), bf16[3072,2,768]{2,0,1:T(8,128)(2,1)}) %all-gather.10.cloned.1.call-update) | async-done | bytes 9437200 | tf_op jit(solution)/shard_map/all_gather | solution.py:205
  154.8 5.4 %fusion.3 = f32[256,2,768]{2,0,1:T(8,128)S(1)} fusion(bf16[3072,2,768]{2,0,1:T(8,128)(2,1)} %all-gather.10.cloned.1.call-done, bf16[256,3072]{1,0:T(8,128)(2,1)S(1)} %copy-done.2, f32[3072]{0:T(1024)S(1)} %convert_element_type.40, f32[256]{0:T(256)S(1)} %add_rsqrt_fusion), kind=kOutput, calls=%fused_computation.9 | convolution fusion | flops 2419064832 | bytes 12596224 | tf_op jit(solution)/shard_map/tk,kcj->tcj/dot_general | solution.py:219
  161.8 0.6 convert_element_type.44
  162.3 1.3 copy.42
  163.7 1.2 maximum_bitcast_fusion.1.refs_1_
  165.3 11.1 %shard_map.83 = (bf16[8,8,96,256]{3,2,1,0:T(8,128)(2,1)}, f32[8,8,2,256]{3,2,1,0:T(2,128)}) custom-call(s32[4]{0:T(128)} %copy-done.6, s32[4]{0:T(128)} %copy-done.5, s32[4]{0:T(128)} %broadcast_13_limit_ref.2.limit_ref, s32[4]{0:T(128)} %len_ref.3, s32[32]{0:T(128)} %select_reduce_fusion.1.slot_ref, ...), custom_call_target="tpu_custom_call" | custom-call | tf_op jit(solution)/shard_map/pallas_call | solution.py:147
  176.4 1.6 copy.43
  178.1 0.5 all-gather.12.cloned.1.call-update
  178.6 3.7 %all-to-all-start = ((bf16[8,8,96,256]{3,2,1,0:T(8,128)(2,1)}), bf16[8,8,96,256]{3,2,1,0:T(8,128)(2,1)S(1)}, u32[]{:S(2)}, u32[]{:S(2)}) async-start(bf16[8,8,96,256]{3,2,1,0:T(8,128)(2,1)} %get-tuple-element.32), calls=%async_computation | async-start | bytes 6291456 | tf_op jit(solution)/shard_map/all_to_all | solution.py:240
  182.3 29.7 %all-gather.16.cloned.1.call-done = f32[64,8,2,256]{3,1,2,0:T(8,128)} async-done(((f32[8,8,2,256]{3,1,2,0:T(8,128)}), f32[64,8,2,256]{3,1,2,0:T(8,128)}) %all-gather.16.cloned.1.call-update) | async-done | bytes 1048592 | tf_op jit(solution)/shard_map/all_gather | solution.py:241
  212.0 0.9 dynamic-slice_bitcast_fusion
  213.0 11.3 %all-to-all-done = bf16[8,8,96,256]{3,2,1,0:T(8,128)(2,1)S(1)} async-done(((bf16[8,8,96,256]{3,2,1,0:T(8,128)(2,1)}), bf16[8,8,96,256]{3,2,1,0:T(8,128)(2,1)S(1)}, u32[]{:S(2)}, u32[]{:S(2)}) %all-to-all-start) | async-done | bytes 3145760 | tf_op jit(solution)/shard_map/all_to_all | solution.py:240
  224.3 0.7 multiply_reduce_fusion
  225.1 35.1 %all-gather.12.cloned.1.call-done = bf16[3072,768]{1,0:T(8,128)(2,1)} async-done(((bf16[384,768]{1,0:T(8,128)(2,1)}), bf16[3072,768]{1,0:T(8,128)(2,1)}) %all-gather.12.cloned.1.call-update) | async-done | bytes 4718608 | tf_op jit(solution)/shard_map/all_gather | solution.py:217
  260.2 4.9 %convolution_convert_fusion = bf16[256,3072]{1,0:T(8,128)(2,1)} fusion(bf16[256,768]{0,1:T(8,128)(2,1)S(1)} %bitcast.47, bf16[3072,768]{1,0:T(8,128)(2,1)} %all-gather.12.cloned.1.call-done), kind=kOutput, calls=%fused_computation.5 | convolution fusion | flops 1208745984 | bytes 6684672 | tf_op jit(solution)/shard_map/dot_general | solution.py:253
  265.2 35.4 %reduce-scatter.2.cloned.1.call-done = bf16[256,768]{1,0:T(8,128)(2,1)} async-done(((bf16[256,3072]{1,0:T(8,128)(2,1)}), bf16[256,768]{1,0:T(8,128)(2,1)}) %reduce-scatter.2.cloned.1.call-update) | async-done | bytes 393232 | tf_op jit(solution)/shard_map/reduce_scatter | solution.py:256
  (57 shorter events, 4.9 us)
Async XLA Ops:
  6.5 44.4 %all-gather.14.cloned.1.call-start = ((), (), s32[]{:S(2)}) async-start(), calls=%async_computation.6 | async-start | bytes 5308416 | tf_op jit(solution)/shard_map/all_gather | solution.py:173
  8.5 85.5 %all-gather.8.cloned.1.call-start = ((), (), s32[]{:S(2)}) async-start(), calls=%async_computation.2 | async-start | bytes 4718592 | tf_op jit(solution)/shard_map/all_gather | solution.py:197
  9.3 19.5 %copy-start.6 = (s32[4]{0:T(128)}, s32[4]{0:T(128)S(1)}, u32[]{:S(2)}) copy-start(s32[4]{0:T(128)S(1)} %get-tuple-element.35.req_ref) | copy-start | bytes 52
  10.2 18.6 %copy-start.5 = (s32[4]{0:T(128)}, s32[4]{0:T(128)S(1)}, u32[]{:S(2)}) copy-start(s32[4]{0:T(128)S(1)} %fusion.12.base_ref) | copy-start | bytes 52
  34.3 5.6 %copy-start.3 = (bf16[3072]{0:T(1024)(128)(2,1)S(1)}, bf16[3072]{0:T(1024)(128)(2,1)}, u32[]{:S(2)}) copy-start(bf16[3072]{0:T(1024)(128)(2,1)} %param.9) | copy-start | bytes 18436
  34.3 5.6 %copy-start.1 = (bf16[256,3072]{1,0:T(8,128)(2,1)S(1)}, bf16[256,3072]{1,0:T(8,128)(2,1)}, u32[]{:S(2)}) copy-start(bf16[256,3072]{1,0:T(8,128)(2,1)} %param.8) | copy-start | bytes 4718596
  55.3 1.9 copy-start
  57.1 97.6 %all-gather.10.cloned.1.call-start = ((), (), s32[]{:S(2)}) async-start(), calls=%async_computation.3 | async-start | bytes 10616832 | tf_op jit(solution)/shard_map/all_gather | solution.py:205
  67.2 27.1 %copy-start.9 = (s32[32]{0:T(128)S(1)}, s32[32]{0:T(128)}, u32[]{:S(2)}) copy-start(s32[32]{0:T(128)} %param.14) | copy-start | bytes 388
  67.2 27.7 %copy-start.7 = (s32[256]{0:T(256)S(1)}, s32[256]{0:T(256)}, u32[]{:S(2)}) copy-start(s32[256]{0:T(256)} %param.15) | copy-start | bytes 3076
  67.2 28.4 %copy-start.4 = (s32[4]{0:T(128)S(1)}, s32[4]{0:T(128)}, u32[]{:S(2)}) copy-start(s32[4]{0:T(128)} %len_ref.3) | copy-start | bytes 52
  94.0 118.0 %all-gather.16.cloned.1.call-start = ((), (), s32[]{:S(2)}) async-start(), calls=%async_computation.7 | async-start | bytes 1179648 | tf_op jit(solution)/shard_map/all_gather | solution.py:241
  95.6 0.7 copy-start.8
  96.3 58.5 %copy-start.2 = (bf16[256,3072]{1,0:T(8,128)(2,1)S(1)}, bf16[256,3072]{1,0:T(8,128)(2,1)}, u32[]{:S(2)}) copy-start(bf16[256,3072]{1,0:T(8,128)(2,1)} %param.8) | copy-start | bytes 4718596
  178.0 82.2 %all-gather.12.cloned.1.call-start = ((), (), s32[]{:S(2)}) async-start(), calls=%async_computation.4 | async-start | bytes 5308416 | tf_op jit(solution)/shard_map/all_gather | solution.py:217
  178.6 45.7 %all-to-all-start = ((bf16[8,8,96,256]{3,2,1,0:T(8,128)(2,1)}), bf16[8,8,96,256]{3,2,1,0:T(8,128)(2,1)S(1)}, u32[]{:S(2)}, u32[]{:S(2)}) async-start(bf16[8,8,96,256]{3,2,1,0:T(8,128)(2,1)} %get-tuple-element.32), calls=%async_computation | async-start | bytes 6291456 | tf_op jit(solution)/shard_map/all_to_all | solution.py:240
  182.3 118.3 %reduce-scatter.2.cloned.1.call-start = ((), (), s32[]{:S(2)}) async-start(), calls=%async_computation.5 | async-start | bytes 1966080 | tf_op jit(solution)/shard_map/reduce_scatter | solution.py:256
Sparse Core Ops, SparseCore 0:
  9.2 41.6 all-gather.13
  57.2 36.7 all-gather.7
  95.9 58.8 all-gather.9
  178.1 33.8 all-gather.15
  213.8 46.3 all-gather.11
  265.3 35.2 reduce-scatter.1

commit v12 on v8

--- a/solution.py
+++ b/solution.py
@@ -37,19 +37,14 @@
 def attend_kernel(carry_in, out_rows):
     def kernel(req_ref, base_ref, limit_ref, len_ref, slot_ref, *refs):
         if carry_in:
-            (q_ref, k_ref, v_ref, m0_ref, l0_ref, o0_ref,
-             num_ref, stats_ref, m_ref, l_ref, o_ref) = refs
+            (q_ref, k_ref, v_ref, m_ref, l_ref, o_ref, num_ref, stats_ref) = refs
         else:
             q_ref, k_ref, v_ref, m_ref, l_ref, o_ref = refs
         step = pl.program_id(0)
 
-        @pl.when(step == 0)
-        def _():
-            if carry_in:
-                m_ref[...] = m0_ref[...]
-                l_ref[...] = l0_ref[...]
-                o_ref[...] = o0_ref[...]
-            else:
+        if not carry_in:
+            @pl.when(step == 0)
+            def _():
                 m_ref[...] = jnp.full(m_ref.shape, negative, jnp.float32)
                 l_ref[...] = jnp.zeros(l_ref.shape, jnp.float32)
                 o_ref[...] = jnp.zeros(o_ref.shape, jnp.float32)
@@ -136,7 +131,7 @@
             jax.ShapeDtypeStruct((groups, head_count, 2, out_rows), jnp.float32),
         )
         out_specs = (whole, whole)
-        scratch = tuple(pltpu.VMEM(*a) for a in acc_shapes)
+        scratch = ()
     grid_spec = pltpu.PrefetchScalarGridSpec(
         num_scalar_prefetch=5,
         grid=(blk_count,),

time: 278 us -> 278 us (level)
  no operation moved by 1% of the time
where the time goes in v12:
time: 278 us; the launch traced here: 277 us
  waiting for transfers between devices  118 us (42%)
  local copies, waits for them, and re-layouts  61.5 us (22%)
  Pallas kernels  47 us (17%)
  matrix products  14.7 us (5%)
  between operations  13.4 us (5%)
  blocking collectives  10.4 us (4%)
  other arithmetic  7.8 us (3%)
  starting transfers between devices  4 us (1%)
    pallas_call x2, Pallas kernels, attend_blocks(): pl.pallas_call(attend_kernel(carry is not None, out_rows), out_shape=out_...  47 us
    all_to_all x1, waiting for transfers between devices, body(): lax.all_to_all(sent_num, 'wide', split_axis=0, concat_axis=0, tiled=True)  39.6 us
    reduce_scatter x1, waiting for transfers between devices, body(): lax.psum_scatter(out_part.astype(jnp.bfloat16), 'narrow', scatter_dimensi...  34.5 us
    slice x2, local copies, waits for them, and re-layouts, body(): cache_v[:, :, 1].reshape(cache_count, blk_len, head_count, HD)  24.4 us
    all_gather x1, waiting for transfers between devices, body(): w_kv = lax.all_gather(w_kv_local, 'wide', axis=0, tiled=True)  22.1 us
    slice x1, local copies, waits for them, and re-layouts, body(): cache[:, :, 0].reshape(cache_count, blk_len, head_count, HD)  18.4 us
    all_gather x1, waiting for transfers between devices, body(): all_queries = lax.all_gather(queries, 'wide', axis=1, tiled=True)  11.3 us
    another operation x2, local copies, waits for them, and re-layouts, body(): cache[:, :, 0].reshape(cache_count, blk_len, head_count, HD)  11.1 us
  transfers between devices with their start and end apart: 6, of which 5 were waited for; matrix products, arithmetic and copies ran while one was open for 26% of the time, Pallas kernels for 17%

profile of v12, /device:TPU:0, one launch (start us, length us, event | category | flops | bytes accessed | tf_op | source)
XLA Modules:
  0.0 276.7 jit_solution(9075824383812605742)
XLA Ops:
  6.5 2.0 slice.37
  8.6 0.7 and_select_fusion.3
  9.3 0.8 select_reduce_fusion.3
  10.3 18.4 %slice_reduce_fusion = bf16[32,64,768]{2,1,0:T(8,128)(2,1)S(1)} fusion(bf16[32,64,2,768]{3,2,1,0:T(2,128)(2,1)} %param.12), kind=kLoop, calls=%fused_computation.1 | loop fusion | bytes 6291456 | tf_op jit(solution)/shard_map/slice | solution.py:176
  28.8 5.5 %reshape_squeeze.9 = bf16[32,64,8,96]{3,2,1,0:T(8,128)(2,1)} reshape(bf16[32,64,768]{2,1,0:T(8,128)(2,1)S(1)} %slice_reduce_fusion) | data formatting | bytes 6291456 | tf_op jit(solution)/shard_map/reshape;squeeze | solution.py:176
  34.3 5.6 %copy.36 = bf16[32,64,8,96]{3,1,2,0:T(8,128)(2,1)} copy(bf16[32,64,8,96]{3,2,1,0:T(8,128)(2,1)} %reshape_squeeze.9) | data formatting | bytes 6291456 | tf_op jit(solution)/shard_map/reshape;squeeze | solution.py:176
  39.9 0.4 fusion
  40.6 10.3 %all-gather.12.cloned.1.call-done = bf16[3072,1,768]{2,0,1:T(8,128)(2,1)} async-done(((bf16[384,1,768]{2,0,1:T(8,128)(2,1)}), bf16[3072,1,768]{2,0,1:T(8,128)(2,1)}) %all-gather.12.cloned.1.call-update) | async-done | bytes 4718608 | tf_op jit(solution)/shard_map/all_gather | solution.py:168
  50.9 4.4 %fusion.7 = f32[256,768]{0,1:T(8,128)S(1)} fusion(bf16[3072,768]{1,0:T(8,128)(2,1)} %bitcast.48, bf16[256,3072]{1,0:T(8,128)(2,1)S(1)} %copy-done.1, f32[3072]{0:T(1024)S(1)} %convert_element_type.40, f32[256]{0:T(256)S(1)} %add_rsqrt_fusion), kind=kOutput, calls=%fused_computation.16 | convolution fusion | flops 1211105280 | bytes 7091200 | tf_op jit(solution)/shard_map/dot_general | solution.py:185
  56.0 1.1 maximum_bitcast_fusion
  57.2 1.1 slice.42
  58.3 8.9 %slice.41 = bf16[32,64,1,768]{3,2,1,0:T(2,128)(2,1)} slice(bf16[32,64,2,768]{3,2,1,0:T(2,128)(2,1)} %param.12), slice={[0:32], [0:64], [1:2], [0:768]} | slice | bytes 6291456 | tf_op jit(solution)/shard_map/slice | solution.py:195
  67.2 15.5 %copy.27 = bf16[32,64,1,768]{1,3,0,2:T(8,128)(2,1)} copy(bf16[32,64,1,768]{3,2,1,0:T(2,128)(2,1)} %slice.41) | data formatting | bytes 6291456 | tf_op jit(solution)/shard_map/slice | solution.py:195
  82.7 11.3 %all-gather.6.cloned.1.call-done.refs_0_ = bf16[8,32,64,96]{3,2,1,0:T(8,128)(2,1)} async-done(((bf16[8,4,64,96]{3,2,1,0:T(8,128)(2,1)}), bf16[8,32,64,96]{3,2,1,0:T(8,128)(2,1)}) %all-gather.6.cloned.1.call-update) | async-done | bytes 3145744 | tf_op jit(solution)/shard_map/all_gather | solution.py:192
  94.3 0.7 select_reduce_fusion.1.slot_ref
  95.1 0.5 fusion.12
  95.7 0.6 select_reduce_fusion.2.limit_ref
  96.3 36.3 %shard_map.82 = (f32[4,8,1,512]{3,2,1,0:T(1,128)}, f32[4,8,1,512]{3,2,1,0:T(1,128)}, f32[4,8,96,512]{3,2,1,0:T(8,128)}) custom-call(s32[32]{0:T(128)} %copy-done.8, s32[32]{0:T(128)} %get-tuple-element.45.base_ref, s32[32]{0:T(128)} %select_reduce_fusion.2.limit_ref, s32[4]{0:T(128)} %len_ref.3, s32[32]{0:T(128)} %select_reduce_fusion.1.slot_ref, ...), custom_call_target="tpu_custom_call" | custom-call | tf_op jit(solution)/shard_map/pallas_call | solution.py:142
  132.7 22.1 %all-gather.8.cloned.1.call-done = bf16[3072,2,768]{2,0,1:T(8,128)(2,1)} async-done(((bf16[384,2,768]{2,0,1:T(8,128)(2,1)}), bf16[3072,2,768]{2,0,1:T(8,128)(2,1)}) %all-gather.8.cloned.1.call-update) | async-done | bytes 9437200 | tf_op jit(solution)/shard_map/all_gather | solution.py:200
  154.8 5.4 %fusion.3 = f32[256,2,768]{2,0,1:T(8,128)S(1)} fusion(bf16[3072,2,768]{2,0,1:T(8,128)(2,1)} %all-gather.8.cloned.1.call-done, bf16[256,3072]{1,0:T(8,128)(2,1)S(1)} %copy-done.2, f32[3072]{0:T(1024)S(1)} %convert_element_type.40, f32[256]{0:T(256)S(1)} %add_rsqrt_fusion), kind=kOutput, calls=%fused_computation.9 | convolution fusion | flops 2419064832 | bytes 12596224 | tf_op jit(solution)/shard_map/tk,kcj->tcj/dot_general | solution.py:214
  161.4 0.4 copy.30
  161.8 0.6 convert_element_type.44
  162.3 1.2 copy.31
  163.6 1.1 maximum_bitcast_fusion.1.refs_1_
  164.7 0.5 broadcast_13_limit_ref.2.limit_ref
  165.2 10.7 %shard_map.83 = (bf16[8,8,96,256]{3,2,1,0:T(8,128)(2,1)}, f32[8,8,2,256]{3,2,1,0:T(2,128)}) custom-call(s32[4]{0:T(128)} %copy-done.6, s32[4]{0:T(128)} %copy-done.5, s32[4]{0:T(128)} %broadcast_13_limit_ref.2.limit_ref, s32[4]{0:T(128)} %len_ref.3, s32[32]{0:T(128)} %select_reduce_fusion.1.slot_ref, ...), custom_call_target="tpu_custom_call" | custom-call | tf_op jit(solution)/shard_map/pallas_call | solution.py:142
  175.8 10.4 %all_to_all.10 = f32[8,8,2,256]{3,2,1,0:T(2,128)S(1)} all-to-all(f32[8,8,2,256]{3,2,1,0:T(2,128)} %get-tuple-element.33), channel_id=1, replica_groups=mesh['wide'=8,'narrow'=4] {'wide'}, dimensions={0} | all-to-all | bytes 262144 | tf_op jit(solution)/shard_map/all_to_all | solution.py:236
  186.2 3.6 %all-to-all-start = ((bf16[8,8,96,256]{3,2,1,0:T(8,128)(2,1)}), bf16[8,8,96,256]{3,2,1,0:T(8,128)(2,1)S(1)}, u32[]{:S(2)}, u32[]{:S(2)}) async-start(bf16[8,8,96,256]{3,2,1,0:T(8,128)(2,1)} %get-tuple-element.32), calls=%async_computation | async-start | bytes 6291456 | tf_op jit(solution)/shard_map/all_to_all | solution.py:235
  190.2 39.6 %all-to-all-done = bf16[8,8,96,256]{3,2,1,0:T(8,128)(2,1)S(1)} async-done(((bf16[8,8,96,256]{3,2,1,0:T(8,128)(2,1)}), bf16[8,8,96,256]{3,2,1,0:T(8,128)(2,1)S(1)}, u32[]{:S(2)}, u32[]{:S(2)}) %all-to-all-start) | async-done | bytes 3145760 | tf_op jit(solution)/shard_map/all_to_all | solution.py:235
  229.8 0.7 multiply_reduce_fusion
  230.6 4.9 %convolution_convert_fusion = bf16[256,3072]{1,0:T(8,128)(2,1)} fusion(bf16[256,768]{0,1:T(8,128)(2,1)S(1)} %bitcast.45, bf16[3072,768]{1,0:T(8,128)(2,1)} %all-gather.10.cloned.1.call-done), kind=kOutput, calls=%fused_computation.5 | convolution fusion | flops 1208745984 | bytes 6684672 | tf_op jit(solution)/shard_map/dot_general | solution.py:247
  235.6 34.5 %reduce-scatter.2.cloned.1.call-done = bf16[256,768]{1,0:T(8,128)(2,1)} async-done(((bf16[256,3072]{1,0:T(8,128)(2,1)}), bf16[256,768]{1,0:T(8,128)(2,1)}) %reduce-scatter.2.cloned.1.call-update) | async-done | bytes 393232 | tf_op jit(solution)/shard_map/reduce_scatter | solution.py:250
  (54 shorter events, 3.3 us)
Async XLA Ops:
  6.5 44.4 %all-gather.12.cloned.1.call-start = ((), (), s32[]{:S(2)}) async-start(), calls=%async_computation.7 | async-start | bytes 5308416 | tf_op jit(solution)/shard_map/all_gather | solution.py:168
  8.5 85.5 %all-gather.6.cloned.1.call-start = ((), (), s32[]{:S(2)}) async-start(), calls=%async_computation.3 | async-start | bytes 4718592 | tf_op jit(solution)/shard_map/all_gather | solution.py:192
  9.3 19.5 %copy-start.6 = (s32[4]{0:T(128)}, s32[4]{0:T(128)S(1)}, u32[]{:S(2)}) copy-start(s32[4]{0:T(128)S(1)} %get-tuple-element.37.req_ref) | copy-start | bytes 52
  10.2 18.6 %copy-start.5 = (s32[4]{0:T(128)}, s32[4]{0:T(128)S(1)}, u32[]{:S(2)}) copy-start(s32[4]{0:T(128)S(1)} %fusion.11.base_ref) | copy-start | bytes 52
  34.3 5.6 %copy-start.3 = (bf16[3072]{0:T(1024)(128)(2,1)S(1)}, bf16[3072]{0:T(1024)(128)(2,1)}, u32[]{:S(2)}) copy-start(bf16[3072]{0:T(1024)(128)(2,1)} %param.9) | copy-start | bytes 18436
  34.3 5.6 %copy-start.1 = (bf16[256,3072]{1,0:T(8,128)(2,1)S(1)}, bf16[256,3072]{1,0:T(8,128)(2,1)}, u32[]{:S(2)}) copy-start(bf16[256,3072]{1,0:T(8,128)(2,1)} %param.8) | copy-start | bytes 4718596
  55.3 1.9 copy-start
  57.1 97.6 %all-gather.8.cloned.1.call-start = ((), (), s32[]{:S(2)}) async-start(), calls=%async_computation.4 | async-start | bytes 10616832 | tf_op jit(solution)/shard_map/all_gather | solution.py:200
  67.2 27.1 %copy-start.9 = (s32[32]{0:T(128)S(1)}, s32[32]{0:T(128)}, u32[]{:S(2)}) copy-start(s32[32]{0:T(128)} %param.14) | copy-start | bytes 388
  67.2 27.8 %copy-start.7 = (s32[256]{0:T(256)S(1)}, s32[256]{0:T(256)}, u32[]{:S(2)}) copy-start(s32[256]{0:T(256)} %param.15) | copy-start | bytes 3076
  67.2 28.5 %copy-start.4 = (s32[4]{0:T(128)S(1)}, s32[4]{0:T(128)}, u32[]{:S(2)}) copy-start(s32[4]{0:T(128)} %len_ref.3) | copy-start | bytes 52
  94.0 136.6 %all-gather.10.cloned.1.call-start = ((), (), s32[]{:S(2)}) async-start(), calls=%async_computation.5 | async-start | bytes 5308416 | tf_op jit(solution)/shard_map/all_gather | solution.py:212
  95.7 0.6 copy-start.8
  96.3 58.5 %copy-start.2 = (bf16[256,3072]{1,0:T(8,128)(2,1)S(1)}, bf16[256,3072]{1,0:T(8,128)(2,1)}, u32[]{:S(2)}) copy-start(bf16[256,3072]{1,0:T(8,128)(2,1)} %param.8) | copy-start | bytes 4718596
  186.2 43.5 %all-to-all-start = ((bf16[8,8,96,256]{3,2,1,0:T(8,128)(2,1)}), bf16[8,8,96,256]{3,2,1,0:T(8,128)(2,1)S(1)}, u32[]{:S(2)}, u32[]{:S(2)}) async-start(bf16[8,8,96,256]{3,2,1,0:T(8,128)(2,1)} %get-tuple-element.32), calls=%async_computation | async-start | bytes 6291456 | tf_op jit(solution)/shard_map/all_to_all | solution.py:235
  189.9 80.2 %reduce-scatter.2.cloned.1.call-start = ((), (), s32[]{:S(2)}) async-start(), calls=%async_computation.6 | async-start | bytes 1966080 | tf_op jit(solution)/shard_map/reduce_scatter | solution.py:250
Sparse Core Ops, SparseCore 0:
  9.2 41.6 all-gather.11
  57.2 36.7 all-gather.5
  95.9 58.8 all-gather.7
  156.5 42.4 all-gather.9
  235.7 34.3 reduce-scatter.1

commit v13 on v12

--- a/solution.py
+++ b/solution.py
@@ -54,9 +54,13 @@
         limit = limit_ref[step]
         qlen = len_ref[req]
         per_request = slot_ref.shape[0] // len_ref.shape[0]
-        queries = jnp.concatenate(
-            [q_ref[:, slot_ref[req * per_request + i]] for i in range(per_request)], axis=1
-        )
+        if carry_in:
+            queries = q_ref[0]
+        else:
+            queries = jnp.concatenate(
+                [q_ref[:, slot_ref[req * per_request + i]] for i in range(per_request)],
+                axis=1,
+            )
         keys = k_ref[0]
         vals = v_ref[0]
         blk_len = keys.shape[1]
@@ -101,14 +105,20 @@
     queries, keys, vals_t, blk_req, blk_base, blk_limit, lengths, slot_of,
     carry=None, out_rows=None,
 ):
-    head_count, _, blk_len, head_dim = queries.shape
+    _, head_count, blk_len, head_dim = keys.shape
     req_count = lengths.shape[0]
     q_len = slot_of.shape[0] // req_count * blk_len
     blk_count = keys.shape[0]
     vmem = pltpu.MemorySpace.VMEM
     whole = pl.BlockSpec(memory_space=vmem)
+    if carry is None:
+        q_spec = whole
+    else:
+        q_spec = pl.BlockSpec(
+            (1, head_count, q_len, head_dim), lambda j, req_ref, *_: (req_ref[j], 0, 0, 0)
+        )
     in_specs = [
-        whole,
+        q_spec,
         pl.BlockSpec((1, head_count, blk_len, head_dim), lambda j, *_: (j, 0, 0, 0)),
         pl.BlockSpec((1, head_count, head_dim, blk_len), lambda j, *_: (j, 0, 0, 0)),
     ]
@@ -208,7 +218,10 @@
     carry = attend_blocks(
         q_heads, cache_keys, cache_vals, cache_req, cache_base, cache_limit, lengths, slot_of
     )
-    carry, w_out_local = lax.optimization_barrier((carry, w_out))
+    q_req = jnp.transpose(
+        q_heads[:, slot_of.reshape(req_count, per_request)], (1, 0, 2, 3, 4)
+    ).reshape(req_count, head_count, fresh_len, HD)
+    carry, w_out_local, q_req = lax.optimization_barrier((carry, w_out, q_req))
     part_out = lax.all_gather(w_out_local, "wide", axis=0, tiled=True)
 
     kv_proj = jnp.einsum("tk,kcj->tcj", normed, w_kv, preferred_element_type=jnp.float32)
@@ -220,7 +233,7 @@
     vals_new = kv_proj[:, 1].astype(jnp.bfloat16).reshape(slot_count, blk_len, head_count, HD)
     new_limit = jnp.full((slot_count,), beyond, jnp.int32)
     sent_num, sent_stats = attend_blocks(
-        q_heads,
+        q_req,
         jnp.transpose(keys_new, (0, 2, 1, 3)),
         jnp.transpose(vals_new, (0, 2, 3, 1)),
         slot_req,

time: 278 us -> 278 us (level)
  local copies, waits for them, and re-layouts: 61.5 us -> 73.4 us
  waiting for transfers between devices: 118 us -> 109 us
    gather x0 -> x2, local copies, waits for them, and re-layouts: none -> 11.5 us  [body(): q_heads[:, slot_of.reshape(req_count, per_request)]]
    all_gather x1, waiting for transfers between devices: 22.1 us -> 11 us  [body(): w_kv = lax.all_gather(w_kv_local, 'wide', axis=0, tiled=True)]
  transfers between devices with their start and end apart: 6 -> 6, of which waited for: 5 -> 5; matrix products, arithmetic and copies ran while one was open for 26% -> 29% of each run, Pallas kernels for 17% -> 17%
where the time goes in v13:
time: 278 us; the launch traced here: 277 us
  waiting for transfers between devices  109 us (39%)
  local copies, waits for them, and re-layouts  73.4 us (26%)
  Pallas kernels  46.4 us (17%)
  matrix products  14.7 us (5%)
  between operations  13.4 us (5%)
  blocking collectives  10.2 us (4%)
  other arithmetic  5.95 us (2%)
  starting transfers between devices  4 us (1%)
    pallas_call x2, Pallas kernels, attend_blocks(): pl.pallas_call(attend_kernel(carry is not None, out_rows), out_shape=out_...  46.4 us
    all_to_all x1, waiting for transfers between devices, body(): lax.all_to_all(sent_num, 'wide', split_axis=0, concat_axis=0, tiled=True)  40.2 us
    reduce_scatter x1, waiting for transfers between devices, body(): lax.psum_scatter(out_part.astype(jnp.bfloat16), 'narrow', scatter_dimensi...  34.5 us
    slice x2, local copies, waits for them, and re-layouts, body(): cache_v[:, :, 1].reshape(cache_count, blk_len, head_count, HD)  24.3 us
    slice x1, local copies, waits for them, and re-layouts, body(): cache[:, :, 0].reshape(cache_count, blk_len, head_count, HD)  18.4 us
    gather x2, local copies, waits for them, and re-layouts, body(): q_heads[:, slot_of.reshape(req_count, per_request)]  11.5 us
    all_gather x1, waiting for transfers between devices, body(): all_queries = lax.all_gather(queries, 'wide', axis=1, tiled=True)  11.4 us
    all_gather x1, waiting for transfers between devices, body(): w_q = lax.all_gather(w_qkv[:, 0], 'wide', axis=0, tiled=True)  11.4 us
  transfers between devices with their start and end apart: 6, of which 5 were waited for; matrix products, arithmetic and copies ran while one was open for 29% of the time, Pallas kernels for 17%

profile of v13, /device:TPU:0, one launch (start us, length us, event | category | flops | bytes accessed | tf_op | source)
XLA Modules:
  0.0 276.7 jit_solution(16255035645511736175)
XLA Ops:
  6.5 2.0 slice.37
  8.6 18.4 %slice_reduce_fusion = bf16[32,64,768]{2,1,0:T(8,128)(2,1)S(1)} fusion(bf16[32,64,2,768]{3,2,1,0:T(2,128)(2,1)} %param.12), kind=kLoop, calls=%fused_computation.2 | loop fusion | bytes 6291456 | tf_op jit(solution)/shard_map/slice | solution.py:186
  27.0 5.5 %reshape_squeeze.9 = bf16[32,64,8,96]{3,2,1,0:T(8,128)(2,1)} reshape(bf16[32,64,768]{2,1,0:T(8,128)(2,1)S(1)} %slice_reduce_fusion) | data formatting | bytes 6291456 | tf_op jit(solution)/shard_map/reshape;squeeze | solution.py:186
  32.5 5.8 %copy.39 = bf16[32,64,8,96]{3,1,2,0:T(8,128)(2,1)} copy(bf16[32,64,8,96]{3,2,1,0:T(8,128)(2,1)} %reshape_squeeze.9) | data formatting | bytes 6291456 | tf_op jit(solution)/shard_map/reshape;squeeze | solution.py:186
  38.9 0.4 fusion
  39.5 11.4 %all-gather.12.cloned.1.call-done = bf16[3072,1,768]{2,0,1:T(8,128)(2,1)} async-done(((bf16[384,1,768]{2,0,1:T(8,128)(2,1)}), bf16[3072,1,768]{2,0,1:T(8,128)(2,1)}) %all-gather.12.cloned.1.call-update) | async-done | bytes 4718608 | tf_op jit(solution)/shard_map/all_gather | solution.py:178
  50.9 4.4 %fusion.7 = f32[256,768]{0,1:T(8,128)S(1)} fusion(bf16[3072,768]{1,0:T(8,128)(2,1)} %bitcast.56, bf16[256,3072]{1,0:T(8,128)(2,1)S(1)} %copy-done.1, f32[3072]{0:T(1024)S(1)} %convert_element_type.40, f32[256]{0:T(256)S(1)} %add_rsqrt_fusion), kind=kOutput, calls=%fused_computation.17 | convolution fusion | flops 1211105280 | bytes 7091200 | tf_op jit(solution)/shard_map/dot_general | solution.py:195
  56.0 1.1 maximum_bitcast_fusion
  57.2 1.1 slice.42
  58.3 8.8 %slice.41 = bf16[32,64,1,768]{3,2,1,0:T(2,128)(2,1)} slice(bf16[32,64,2,768]{3,2,1,0:T(2,128)(2,1)} %param.12), slice={[0:32], [0:64], [1:2], [0:768]} | slice | bytes 6291456 | tf_op jit(solution)/shard_map/slice | solution.py:205
  67.1 15.5 %copy.29 = bf16[32,64,1,768]{1,3,0,2:T(8,128)(2,1)} copy(bf16[32,64,1,768]{3,2,1,0:T(2,128)(2,1)} %slice.41) | data formatting | bytes 6291456 | tf_op jit(solution)/shard_map/slice | solution.py:205
  82.6 11.4 %all-gather.6.cloned.1.call-done.refs_0_ = bf16[8,32,64,96]{3,2,1,0:T(8,128)(2,1)} async-done(((bf16[8,4,64,96]{3,2,1,0:T(8,128)(2,1)}), bf16[8,32,64,96]{3,2,1,0:T(8,128)(2,1)}) %all-gather.6.cloned.1.call-update) | async-done | bytes 3145744 | tf_op jit(solution)/shard_map/all_gather | solution.py:202
  94.7 0.5 fusion.12
  95.3 0.7 select_reduce_fusion.2.limit_ref
  95.9 5.3 %gather_fusion = bf16[32,8,64,96]{3,2,1,0:T(8,128)(2,1)} fusion(bf16[8,32,64,96]{3,2,1,0:T(8,128)(2,1)} %all-gather.6.cloned.1.call-done.refs_0_, s32[1024]{0:T(1024)S(1)} %pad_clamp_fusion), kind=kCustom, calls=%fused_computation | custom fusion | bytes 6291584 | tf_op jit(solution)/shard_map/gather | solution.py:222
  101.3 6.2 %copy.30 = bf16[4,8,8,64,96]{4,3,1,2,0:T(8,128)(2,1)} copy(bf16[4,8,8,64,96]{4,3,2,1,0:T(8,128)(2,1)} %bitcast.46) | data formatting | bytes 6291456 | tf_op jit(solution)/shard_map/gather | solution.py:222
  107.5 36.2 %shard_map.82 = (f32[4,8,1,512]{3,2,1,0:T(1,128)}, f32[4,8,1,512]{3,2,1,0:T(1,128)}, f32[4,8,96,512]{3,2,1,0:T(8,128)}) custom-call(s32[32]{0:T(128)} %copy-done.9, s32[32]{0:T(128)} %get-tuple-element.47.base_ref, s32[32]{0:T(128)} %select_reduce_fusion.2.limit_ref, s32[4]{0:T(128)} %len_ref.3, s32[32]{0:T(128)} %copy-done.4, ...), custom_call_target="tpu_custom_call" | custom-call | tf_op jit(solution)/shard_map/pallas_call | solution.py:152
  143.7 11.0 %all-gather.8.cloned.1.call-done = bf16[3072,2,768]{2,0,1:T(8,128)(2,1)} async-done(((bf16[384,2,768]{2,0,1:T(8,128)(2,1)}), bf16[3072,2,768]{2,0,1:T(8,128)(2,1)}) %all-gather.8.cloned.1.call-update) | async-done | bytes 9437200 | tf_op jit(solution)/shard_map/all_gather | solution.py:210
  154.8 5.4 %fusion.3 = f32[256,2,768]{2,0,1:T(8,128)S(1)} fusion(bf16[3072,2,768]{2,0,1:T(8,128)(2,1)} %all-gather.8.cloned.1.call-done, bf16[256,3072]{1,0:T(8,128)(2,1)S(1)} %copy-done.2, f32[3072]{0:T(1024)S(1)} %convert_element_type.40, f32[256]{0:T(256)S(1)} %add_rsqrt_fusion), kind=kOutput, calls=%fused_computation.10 | convolution fusion | flops 2419064832 | bytes 12596224 | tf_op jit(solution)/shard_map/tk,kcj->tcj/dot_general | solution.py:227
  160.8 0.3 copy.33
  161.4 0.3 copy.32
  161.8 0.6 convert_element_type.44
  162.3 1.2 copy.34
  163.6 1.1 maximum_bitcast_fusion.1.refs_1_
  164.7 0.5 broadcast_13_limit_ref.2.limit_ref
  165.2 10.2 %shard_map.83 = (bf16[8,8,96,256]{3,2,1,0:T(8,128)(2,1)}, f32[8,8,2,256]{3,2,1,0:T(2,128)}) custom-call(s32[4]{0:T(128)} %copy-done.7, s32[4]{0:T(128)} %copy-done.6, s32[4]{0:T(128)} %broadcast_13_limit_ref.2.limit_ref, s32[4]{0:T(128)} %len_ref.3, s32[32]{0:T(128)} %copy-done.4, bf16[4,8,512,96]{3,2,1,0:T(8,128)(2,1)} %bitcast.47, ...), custom_call_target="tpu_custom_call" | custom-call | tf_op jit(solution)/shard_map/pallas_call | solution.py:152
  175.4 10.2 %all_to_all.10 = f32[8,8,2,256]{3,2,1,0:T(2,128)S(1)} all-to-all(f32[8,8,2,256]{3,2,1,0:T(2,128)} %get-tuple-element.35), channel_id=1, replica_groups=mesh['wide'=8,'narrow'=4] {'wide'}, dimensions={0} | all-to-all | bytes 262144 | tf_op jit(solution)/shard_map/all_to_all | solution.py:249
  185.6 3.6 %all-to-all-start = ((bf16[8,8,96,256]{3,2,1,0:T(8,128)(2,1)}), bf16[8,8,96,256]{3,2,1,0:T(8,128)(2,1)S(1)}, u32[]{:S(2)}, u32[]{:S(2)}) async-start(bf16[8,8,96,256]{3,2,1,0:T(8,128)(2,1)} %get-tuple-element.34), calls=%async_computation | async-start | bytes 6291456 | tf_op jit(solution)/shard_map/all_to_all | solution.py:248
  189.6 40.2 %all-to-all-done = bf16[8,8,96,256]{3,2,1,0:T(8,128)(2,1)S(1)} async-done(((bf16[8,8,96,256]{3,2,1,0:T(8,128)(2,1)}), bf16[8,8,96,256]{3,2,1,0:T(8,128)(2,1)S(1)}, u32[]{:S(2)}, u32[]{:S(2)}) %all-to-all-start) | async-done | bytes 3145760 | tf_op jit(solution)/shard_map/all_to_all | solution.py:248
  229.8 0.7 multiply_reduce_fusion
  230.6 4.9 %convolution_convert_fusion = bf16[256,3072]{1,0:T(8,128)(2,1)} fusion(bf16[256,768]{0,1:T(8,128)(2,1)S(1)} %bitcast.53, bf16[3072,768]{1,0:T(8,128)(2,1)} %all-gather.10.cloned.1.call-done), kind=kOutput, calls=%fused_computation.6 | convolution fusion | flops 1208745984 | bytes 6684672 | tf_op jit(solution)/shard_map/dot_general | solution.py:260
  235.6 34.5 %reduce-scatter.2.cloned.1.call-done = bf16[256,768]{1,0:T(8,128)(2,1)} async-done(((bf16[256,3072]{1,0:T(8,128)(2,1)}), bf16[256,768]{1,0:T(8,128)(2,1)}) %reduce-scatter.2.cloned.1.call-update) | async-done | bytes 393232 | tf_op jit(solution)/shard_map/reduce_scatter | solution.py:263
  (62 shorter events, 3.5 us)
Async XLA Ops:
  6.5 44.4 %all-gather.12.cloned.1.call-start = ((), (), s32[]{:S(2)}) async-start(), calls=%async_computation.7 | async-start | bytes 5308416 | tf_op jit(solution)/shard_map/all_gather | solution.py:178
  8.5 85.5 %all-gather.6.cloned.1.call-start = ((), (), s32[]{:S(2)}) async-start(), calls=%async_computation.3 | async-start | bytes 4718592 | tf_op jit(solution)/shard_map/all_gather | solution.py:202
  32.5 5.9 %copy-start.3 = (bf16[3072]{0:T(1024)(128)(2,1)S(1)}, bf16[3072]{0:T(1024)(128)(2,1)}, u32[]{:S(2)}) copy-start(bf16[3072]{0:T(1024)(128)(2,1)} %param.9) | copy-start | bytes 18436
  32.5 5.9 %copy-start.10 = (s32[32]{0:T(128)S(1)}, s32[32]{0:T(128)}, u32[]{:S(2)}) copy-start(s32[32]{0:T(128)} %param.14) | copy-start | bytes 388
  32.5 6.0 %copy-start.5 = (s32[4]{0:T(128)S(1)}, s32[4]{0:T(128)}, u32[]{:S(2)}) copy-start(s32[4]{0:T(128)} %len_ref.3) | copy-start | bytes 52
  32.5 6.3 %copy-start.1 = (bf16[256,3072]{1,0:T(8,128)(2,1)S(1)}, bf16[256,3072]{1,0:T(8,128)(2,1)}, u32[]{:S(2)}) copy-start(bf16[256,3072]{1,0:T(8,128)(2,1)} %param.8) | copy-start | bytes 4718596
  38.5 16.8 %copy-start.7 = (s32[4]{0:T(128)}, s32[4]{0:T(128)S(1)}, u32[]{:S(2)}) copy-start(s32[4]{0:T(128)S(1)} %get-tuple-element.39.req_ref) | copy-start | bytes 52
  38.7 16.6 %copy-start.6 = (s32[4]{0:T(128)}, s32[4]{0:T(128)S(1)}, u32[]{:S(2)}) copy-start(s32[4]{0:T(128)S(1)} %fusion.11.base_ref) | copy-start | bytes 52
  55.3 1.9 copy-start
  57.1 97.6 %all-gather.8.cloned.1.call-start = ((), (), s32[]{:S(2)}) async-start(), calls=%async_computation.4 | async-start | bytes 10616832 | tf_op jit(solution)/shard_map/all_gather | solution.py:210
  67.1 27.4 %copy-start.8 = (s32[256]{0:T(256)S(1)}, s32[256]{0:T(256)}, u32[]{:S(2)}) copy-start(s32[256]{0:T(256)} %param.15) | copy-start | bytes 3076
  94.0 136.6 %all-gather.10.cloned.1.call-start = ((), (), s32[]{:S(2)}) async-start(), calls=%async_computation.5 | async-start | bytes 5308416 | tf_op jit(solution)/shard_map/all_gather | solution.py:225
  94.4 6.9 %copy-start.4 = (s32[32]{0:T(128)}, s32[32]{0:T(128)S(1)}, u32[]{:S(2)}) copy-start(s32[32]{0:T(128)S(1)} %select_reduce_fusion.1.slot_ref) | copy-start | bytes 388
  95.3 6.0 %copy-start.9 = (s32[32]{0:T(128)}, s32[32]{0:T(128)S(1)}, u32[]{:S(2)}) copy-start(s32[32]{0:T(128)S(1)} %get-tuple-element.48.req_ref) | copy-start | bytes 388
  107.5 47.3 %copy-start.2 = (bf16[256,3072]{1,0:T(8,128)(2,1)S(1)}, bf16[256,3072]{1,0:T(8,128)(2,1)}, u32[]{:S(2)}) copy-start(bf16[256,3072]{1,0:T(8,128)(2,1)} %param.8) | copy-start | bytes 4718596
  185.6 44.2 %all-to-all-start = ((bf16[8,8,96,256]{3,2,1,0:T(8,128)(2,1)}), bf16[8,8,96,256]{3,2,1,0:T(8,128)(2,1)S(1)}, u32[]{:S(2)}, u32[]{:S(2)}) async-start(bf16[8,8,96,256]{3,2,1,0:T(8,128)(2,1)} %get-tuple-element.34), calls=%async_computation | async-start | bytes 6291456 | tf_op jit(solution)/shard_map/all_to_all | solution.py:248
  189.3 80.9 %reduce-scatter.2.cloned.1.call-start = ((), (), s32[]{:S(2)}) async-start(), calls=%async_computation.6 | async-start | bytes 1966080 | tf_op jit(solution)/shard_map/reduce_scatter | solution.py:263
Sparse Core Ops, SparseCore 0:
  9.2 41.6 all-gather.11
  57.2 36.7 all-gather.5
  95.9 58.8 all-gather.7
  156.5 43.0 all-gather.9
  235.7 34.3 reduce-scatter.1

commit v14 on v13

--- a/solution.py
+++ b/solution.py
@@ -193,13 +193,12 @@
     slot_pos = slot_start[:, None] + blk_idx[None, :]
     positions = slot_pos.reshape(tok_rows)
     q_proj = jnp.dot(normed, w_q, preferred_element_type=jnp.float32)
-    queries = jnp.transpose(
+    queries = (
         rotate(q_proj.reshape(tok_rows, head_count, HD), positions)
         .astype(jnp.bfloat16)
-        .reshape(slot_count, blk_len, head_count, HD),
-        (2, 0, 1, 3),
-    )
-    all_queries = lax.all_gather(queries, "wide", axis=1, tiled=True)
+        .reshape(tok_rows, lane_width)
+    )
+    all_queries = lax.all_gather(queries, "wide", axis=0, tiled=True)
     queries, cache_v = lax.optimization_barrier((queries, cache))
     cache_vals = jnp.transpose(
         cache_v[:, :, 1].reshape(cache_count, blk_len, head_count, HD), (0, 2, 3, 1)
@@ -213,7 +212,9 @@
     slot_of = jnp.sum(
         jnp.where(order[None, :] == block_ids[:, None], block_ids[None, :], 0), axis=1
     )
-    q_heads = all_queries
+    q_heads = jnp.transpose(
+        all_queries.reshape(block_total, blk_len, head_count, HD), (2, 0, 1, 3)
+    )
 
     carry = attend_blocks(
         q_heads, cache_keys, cache_vals, cache_req, cache_base, cache_limit, lengths, slot_of

time: 278 us -> 281 us (1.011)
  local copies, waits for them, and re-layouts: 73.4 us -> 93.5 us
  waiting for transfers between devices: 109 us -> 91.5 us
    reshape x0 -> x2, local copies, waits for them, and re-layouts: none -> 20 us  [body(): all_queries.reshape(block_total, blk_len, head_count, HD)]
    all_gather x1, waiting for transfers between devices: 11 us -> 0.02 us  [body(): w_kv = lax.all_gather(w_kv_local, 'wide', axis=0, tiled=True)]
    all_gather x1, waiting for transfers between devices: 11.4 us -> 6.81 us  [body(): all_queries = lax.all_gather(queries, 'wide', axis=0, tiled=True)]
  transfers between devices with their start and end apart: 6 -> 6, of which waited for: 5 -> 4; matrix products, arithmetic and copies ran while one was open for 29% -> 36% of each run, Pallas kernels for 17% -> 16%
where the time goes in v14:
time: 281 us; the launch traced here: 279 us
  local copies, waits for them, and re-layouts  93.5 us (33%)
  waiting for transfers between devices  91.5 us (33%)
  Pallas kernels  45.8 us (16%)
  matrix products  14.7 us (5%)
  between operations  13.4 us (5%)
  blocking collectives  10.6 us (4%)
  other arithmetic  5.56 us (2%)
  starting transfers between devices  4.22 us (2%)
    pallas_call x2, Pallas kernels, attend_blocks(): pl.pallas_call(attend_kernel(carry is not None, out_rows), out_shape=out_...  45.8 us
    all_to_all x1, waiting for transfers between devices, body(): lax.all_to_all(sent_num, 'wide', split_axis=0, concat_axis=0, tiled=True)  38.6 us
    reduce_scatter x1, waiting for transfers between devices, body(): lax.psum_scatter(out_part.astype(jnp.bfloat16), 'narrow', scatter_dimensi...  34.5 us
    slice x2, local copies, waits for them, and re-layouts, body(): cache_v[:, :, 1].reshape(cache_count, blk_len, head_count, HD)  24.3 us
    reshape x2, local copies, waits for them, and re-layouts, body(): all_queries.reshape(block_total, blk_len, head_count, HD)  20 us
    slice x1, local copies, waits for them, and re-layouts, body(): cache[:, :, 0].reshape(cache_count, blk_len, head_count, HD)  18.4 us
    gather x2, local copies, waits for them, and re-layouts, body(): q_heads[:, slot_of.reshape(req_count, per_request)]  11.5 us
    all_gather x1, waiting for transfers between devices, body(): w_q = lax.all_gather(w_qkv[:, 0], 'wide', axis=0, tiled=True)  11.4 us
  transfers between devices with their start and end apart: 6, of which 4 were waited for; matrix products, arithmetic and copies ran while one was open for 36% of the time, Pallas kernels for 16%

profile of v14, /device:TPU:0, one launch (start us, length us, event | category | flops | bytes accessed | tf_op | source)
XLA Modules:
  0.0 279.2 jit_solution(15602725875154239796)
XLA Ops:
  6.5 2.0 slice.37
  8.6 18.4 %slice_reduce_fusion = bf16[32,64,768]{2,1,0:T(8,128)(2,1)S(1)} fusion(bf16[32,64,2,768]{3,2,1,0:T(2,128)(2,1)} %param.12), kind=kLoop, calls=%fused_computation.2 | loop fusion | bytes 6291456 | tf_op jit(solution)/shard_map/slice | solution.py:186
  27.0 5.5 %reshape_squeeze.9 = bf16[32,64,8,96]{3,2,1,0:T(8,128)(2,1)} reshape(bf16[32,64,768]{2,1,0:T(8,128)(2,1)S(1)} %slice_reduce_fusion) | data formatting | bytes 6291456 | tf_op jit(solution)/shard_map/reshape;squeeze | solution.py:186
  32.6 5.8 %copy.37 = bf16[32,64,8,96]{3,1,2,0:T(8,128)(2,1)} copy(bf16[32,64,8,96]{3,2,1,0:T(8,128)(2,1)} %reshape_squeeze.9) | data formatting | bytes 6291456 | tf_op jit(solution)/shard_map/reshape;squeeze | solution.py:186
  38.9 0.4 fusion
  39.5 11.4 %all-gather.12.cloned.1.call-done = bf16[3072,1,768]{2,0,1:T(8,128)(2,1)} async-done(((bf16[384,1,768]{2,0,1:T(8,128)(2,1)}), bf16[3072,1,768]{2,0,1:T(8,128)(2,1)}) %all-gather.12.cloned.1.call-update) | async-done | bytes 4718608 | tf_op jit(solution)/shard_map/all_gather | solution.py:178
  50.9 4.4 %fusion.7 = f32[256,768]{0,1:T(8,128)S(1)} fusion(bf16[3072,768]{1,0:T(8,128)(2,1)} %bitcast.57, bf16[256,3072]{1,0:T(8,128)(2,1)S(1)} %copy-done.1, f32[3072]{0:T(1024)S(1)} %convert_element_type.43, f32[256]{0:T(256)S(1)} %add_rsqrt_fusion), kind=kOutput, calls=%fused_computation.16 | convolution fusion | flops 1211105280 | bytes 7091200 | tf_op jit(solution)/shard_map/dot_general | solution.py:195
  55.4 0.8 pad_maximum_fusion
  56.3 0.6 copy-done
  56.9 1.1 slice.42
  58.1 8.9 %slice.41 = bf16[32,64,1,768]{3,2,1,0:T(2,128)(2,1)} slice(bf16[32,64,2,768]{3,2,1,0:T(2,128)(2,1)} %param.12), slice={[0:32], [0:64], [1:2], [0:768]} | slice | bytes 6291456 | tf_op jit(solution)/shard_map/slice | solution.py:204
  67.0 15.4 %copy.23 = bf16[32,64,1,768]{1,3,0,2:T(8,128)(2,1)} copy(bf16[32,64,1,768]{3,2,1,0:T(2,128)(2,1)} %slice.41) | data formatting | bytes 6291456 | tf_op jit(solution)/shard_map/slice | solution.py:204
  82.4 6.8 %all-gather.6.cloned.1.call-done = bf16[2048,768]{0,1:T(8,128)(2,1)} async-done(((bf16[256,768]{0,1:T(8,128)(2,1)}), bf16[2048,768]{0,1:T(8,128)(2,1)}) %all-gather.6.cloned.1.call-update) | async-done | bytes 3145744 | tf_op jit(solution)/shard_map/all_gather | solution.py:201
  90.0 0.5 fusion.12
  90.5 0.6 select_reduce_fusion.2.limit_ref
  91.1 10.1 %reshape.178 = bf16[32,64,8,96]{1,0,3,2:T(8,128)(2,1)} reshape(bf16[2048,768]{0,1:T(8,128)(2,1)} %all-gather.6.cloned.1.call-done) | data formatting | bytes 6291456 | tf_op jit(solution)/shard_map/reshape | solution.py:216
  101.2 9.9 %copy.25 = bf16[32,64,8,96]{3,1,0,2:T(8,128)(2,1)} copy(bf16[32,64,8,96]{1,0,3,2:T(8,128)(2,1)} %reshape.178) | data formatting | bytes 6291456 | tf_op jit(solution)/shard_map/reshape | solution.py:216
  111.1 5.3 %gather_fusion = bf16[32,8,64,96]{3,2,1,0:T(8,128)(2,1)} fusion(bf16[8,32,64,96]{3,2,1,0:T(8,128)(2,1)} %bitcast.44, s32[1024]{0:T(1024)S(1)} %pad_clamp_fusion), kind=kCustom, calls=%fused_computation | custom fusion | bytes 6291584 | tf_op jit(solution)/shard_map/gather | solution.py:223
  116.5 6.2 %copy.26 = bf16[4,8,8,64,96]{4,3,1,2,0:T(8,128)(2,1)} copy(bf16[4,8,8,64,96]{4,3,2,1,0:T(8,128)(2,1)} %bitcast.48) | data formatting | bytes 6291456 | tf_op jit(solution)/shard_map/gather | solution.py:223
  122.7 36.0 %shard_map.82 = (f32[4,8,1,512]{3,2,1,0:T(1,128)}, f32[4,8,1,512]{3,2,1,0:T(1,128)}, f32[4,8,96,512]{3,2,1,0:T(8,128)}) custom-call(s32[32]{0:T(128)} %copy-done.8, s32[32]{0:T(128)} %get-tuple-element.47.base_ref, s32[32]{0:T(128)} %select_reduce_fusion.2.limit_ref, s32[4]{0:T(128)} %len_ref.3, s32[32]{0:T(128)} %copy-done.3, ...), custom_call_target="tpu_custom_call" | custom-call | tf_op jit(solution)/shard_map/pallas_call | solution.py:152
  158.7 5.4 %fusion.3 = f32[256,2,768]{2,0,1:T(8,128)S(1)} fusion(bf16[3072,2,768]{2,0,1:T(8,128)(2,1)} %all-gather.8.cloned.1.call-done, bf16[256,3072]{1,0:T(8,128)(2,1)S(1)} %copy-done.1, f32[3072]{0:T(1024)S(1)} %convert_element_type.43, f32[256]{0:T(256)S(1)} %add_rsqrt_fusion), kind=kOutput, calls=%fused_computation.10 | convolution fusion | flops 2419064832 | bytes 12596224 | tf_op jit(solution)/shard_map/tk,kcj->tcj/dot_general | solution.py:228
  165.7 0.6 convert_element_type.48
  166.3 1.2 copy.30
  167.5 1.1 maximum_bitcast_fusion.refs_1_
  168.6 0.5 broadcast_13_limit_ref.2.limit_ref
  169.1 9.8 %shard_map.83 = (bf16[8,8,96,256]{3,2,1,0:T(8,128)(2,1)}, f32[8,8,2,256]{3,2,1,0:T(2,128)}) custom-call(s32[4]{0:T(128)} %copy-done.6, s32[4]{0:T(128)} %copy-done.5, s32[4]{0:T(128)} %broadcast_13_limit_ref.2.limit_ref, s32[4]{0:T(128)} %len_ref.3, s32[32]{0:T(128)} %copy-done.3, bf16[4,8,512,96]{3,2,1,0:T(8,128)(2,1)} %bitcast.49, ...), custom_call_target="tpu_custom_call" | custom-call | tf_op jit(solution)/shard_map/pallas_call | solution.py:152
  178.9 10.6 %all_to_all.10 = f32[8,8,2,256]{3,2,1,0:T(2,128)S(1)} all-to-all(f32[8,8,2,256]{3,2,1,0:T(2,128)} %get-tuple-element.35), channel_id=1, replica_groups=mesh['wide'=8,'narrow'=4] {'wide'}, dimensions={0} | all-to-all | bytes 262144 | tf_op jit(solution)/shard_map/all_to_all | solution.py:250
  189.5 3.6 %all-to-all-start = ((bf16[8,8,96,256]{3,2,1,0:T(8,128)(2,1)}), bf16[8,8,96,256]{3,2,1,0:T(8,128)(2,1)S(1)}, u32[]{:S(2)}, u32[]{:S(2)}) async-start(bf16[8,8,96,256]{3,2,1,0:T(8,128)(2,1)} %get-tuple-element.34), calls=%async_computation | async-start | bytes 6291456 | tf_op jit(solution)/shard_map/all_to_all | solution.py:249
  193.7 38.6 %all-to-all-done = bf16[8,8,96,256]{3,2,1,0:T(8,128)(2,1)S(1)} async-done(((bf16[8,8,96,256]{3,2,1,0:T(8,128)(2,1)}), bf16[8,8,96,256]{3,2,1,0:T(8,128)(2,1)S(1)}, u32[]{:S(2)}, u32[]{:S(2)}) %all-to-all-start) | async-done | bytes 3145760 | tf_op jit(solution)/shard_map/all_to_all | solution.py:249
  232.3 0.7 multiply_reduce_fusion
  233.1 4.9 %convolution_convert_fusion = bf16[256,3072]{1,0:T(8,128)(2,1)} fusion(bf16[256,768]{0,1:T(8,128)(2,1)S(1)} %bitcast.54, bf16[3072,768]{1,0:T(8,128)(2,1)} %all-gather.10.cloned.1.call-done), kind=kOutput, calls=%fused_computation.6 | convolution fusion | flops 1208745984 | bytes 6684672 | tf_op jit(solution)/shard_map/dot_general | solution.py:261
  238.1 34.5 %reduce-scatter.2.cloned.1.call-done = bf16[256,768]{1,0:T(8,128)(2,1)} async-done(((bf16[256,3072]{1,0:T(8,128)(2,1)}), bf16[256,768]{1,0:T(8,128)(2,1)}) %reduce-scatter.2.cloned.1.call-update) | async-done | bytes 393232 | tf_op jit(solution)/shard_map/reduce_scatter | solution.py:264
  (60 shorter events, 3.9 us)
Async XLA Ops:
  6.5 44.4 %all-gather.12.cloned.1.call-start = ((), (), s32[]{:S(2)}) async-start(), calls=%async_computation.7 | async-start | bytes 5308416 | tf_op jit(solution)/shard_map/all_gather | solution.py:178
  8.5 80.7 %all-gather.6.cloned.1.call-start = ((), (), s32[]{:S(2)}) async-start(), calls=%async_computation.3 | async-start | bytes 3538944 | tf_op jit(solution)/shard_map/all_gather | solution.py:201
  32.5 5.9 %copy-start.2 = (bf16[3072]{0:T(1024)(128)(2,1)S(1)}, bf16[3072]{0:T(1024)(128)(2,1)}, u32[]{:S(2)}) copy-start(bf16[3072]{0:T(1024)(128)(2,1)} %param.9) | copy-start | bytes 18436
  32.5 5.9 %copy-start.9 = (s32[32]{0:T(128)S(1)}, s32[32]{0:T(128)}, u32[]{:S(2)}) copy-start(s32[32]{0:T(128)} %param.14) | copy-start | bytes 388
  32.5 6.0 %copy-start.4 = (s32[4]{0:T(128)S(1)}, s32[4]{0:T(128)}, u32[]{:S(2)}) copy-start(s32[4]{0:T(128)} %len_ref.3) | copy-start | bytes 52
  32.5 6.3 %copy-start.1 = (bf16[256,3072]{1,0:T(8,128)(2,1)S(1)}, bf16[256,3072]{1,0:T(8,128)(2,1)}, u32[]{:S(2)}) copy-start(bf16[256,3072]{1,0:T(8,128)(2,1)} %param.8) | copy-start | bytes 4718596
  38.5 16.8 %copy-start.6 = (s32[4]{0:T(128)}, s32[4]{0:T(128)S(1)}, u32[]{:S(2)}) copy-start(s32[4]{0:T(128)S(1)} %get-tuple-element.39.req_ref) | copy-start | bytes 52
  38.7 16.6 %copy-start.5 = (s32[4]{0:T(128)}, s32[4]{0:T(128)S(1)}, u32[]{:S(2)}) copy-start(s32[4]{0:T(128)S(1)} %fusion.11.base_ref) | copy-start | bytes 52
  55.3 1.6 copy-start
  56.2 102.4 %all-gather.8.cloned.1.call-start = ((), (), s32[]{:S(2)}) async-start(), calls=%async_computation.4 | async-start | bytes 10616832 | tf_op jit(solution)/shard_map/all_gather | solution.py:209
  67.0 22.8 %copy-start.7 = (s32[256]{0:T(256)S(1)}, s32[256]{0:T(256)}, u32[]{:S(2)}) copy-start(s32[256]{0:T(256)} %param.15) | copy-start | bytes 3076
  89.2 143.9 %all-gather.10.cloned.1.call-start = ((), (), s32[]{:S(2)}) async-start(), calls=%async_computation.5 | async-start | bytes 5308416 | tf_op jit(solution)/shard_map/all_gather | solution.py:226
  89.6 11.7 %copy-start.3 = (s32[32]{0:T(128)}, s32[32]{0:T(128)S(1)}, u32[]{:S(2)}) copy-start(s32[32]{0:T(128)S(1)} %select_reduce_fusion.1.slot_ref) | copy-start | bytes 388
  90.5 10.7 %copy-start.8 = (s32[32]{0:T(128)}, s32[32]{0:T(128)S(1)}, u32[]{:S(2)}) copy-start(s32[32]{0:T(128)S(1)} %get-tuple-element.48.req_ref) | copy-start | bytes 388
  189.5 42.8 %all-to-all-start = ((bf16[8,8,96,256]{3,2,1,0:T(8,128)(2,1)}), bf16[8,8,96,256]{3,2,1,0:T(8,128)(2,1)S(1)}, u32[]{:S(2)}, u32[]{:S(2)}) async-start(bf16[8,8,96,256]{3,2,1,0:T(8,128)(2,1)} %get-tuple-element.34), calls=%async_computation | async-start | bytes 6291456 | tf_op jit(solution)/shard_map/all_to_all | solution.py:249
  193.2 79.5 %reduce-scatter.2.cloned.1.call-start = ((), (), s32[]{:S(2)}) async-start(), calls=%async_computation.6 | async-start | bytes 1966080 | tf_op jit(solution)/shard_map/reduce_scatter | solution.py:264
Sparse Core Ops, SparseCore 0:
  9.2 41.6 all-gather.11
  56.4 32.8 all-gather.5
  91.1 58.8 all-gather.7
  158.8 41.9 all-gather.9
  238.2 34.3 reduce-scatter.1

commit v15 on v13

--- a/solution.py
+++ b/solution.py
@@ -245,6 +245,7 @@
         out_rows=tok_rows,
     )
 
+    out_t, sent_num = lax.optimization_barrier((jnp.transpose(part_out), sent_num))
     got_num = lax.all_to_all(sent_num, "wide", split_axis=0, concat_axis=0, tiled=True)
     got_stats = lax.all_to_all(sent_stats, "wide", split_axis=0, concat_axis=0, tiled=True)
     got_max = got_stats[:, :, 0:1]
@@ -258,7 +259,7 @@
         .reshape(tok_rows, lane_width)
     )
     out_part = lax.dot_general(
-        attention, part_out, (((1,), (1,)), ((), ())), preferred_element_type=jnp.float32
+        attention, out_t, (((1,), (0,)), ((), ())), preferred_element_type=jnp.float32
     )
     return lax.psum_scatter(
         out_part.astype(jnp.bfloat16), "narrow", scatter_dimension=1, tiled=True

time: 278 us -> 287 us (1.032)
  waiting for transfers between devices: 109 us -> 122 us
  blocking collectives: 10.2 us -> 0 us
  starting transfers between devices: 4 us -> 7.37 us
    all_gather x1, waiting for transfers between devices: 0.02 us -> 18 us  [body(): part_out = lax.all_gather(w_out_local, 'wide', axis=0, tiled=True)]
    all_to_all x1 -> x0, blocking collectives: 10.2 us -> none  [body(): lax.all_to_all(sent_stats, 'wide', split_axis=0, concat_axis=0, tiled=True)]
    all_to_all x0 -> x1, starting transfers between devices: none -> 3.37 us  [body(): lax.all_to_all(sent_stats, 'wide', split_axis=0, concat_axis=0, tiled=True)]
  transfers between devices with their start and end apart: 6 -> 7, of which waited for: 5 -> 6; matrix products, arithmetic and copies ran while one was open for 29% -> 29% of each run, Pallas kernels for 17% -> 16%
where the time goes in v15:
time: 287 us; the launch traced here: 285 us
  waiting for transfers between devices  122 us (43%)
  local copies, waits for them, and re-layouts  73.1 us (25%)
  Pallas kernels  46.5 us (16%)
  matrix products  14.7 us (5%)
  between operations  13.4 us (5%)
  other arithmetic  7.9 us (3%)
  starting transfers between devices  7.37 us (3%)
    pallas_call x2, Pallas kernels, attend_blocks(): pl.pallas_call(attend_kernel(carry is not None, out_rows), out_shape=out_...  46.5 us
    all_to_all x1, waiting for transfers between devices, body(): lax.all_to_all(sent_num, 'wide', split_axis=0, concat_axis=0, tiled=True)  37.5 us
    reduce_scatter x1, waiting for transfers between devices, body(): lax.psum_scatter(out_part.astype(jnp.bfloat16), 'narrow', scatter_dimensi...  34.6 us
    slice x2, local copies, waits for them, and re-layouts, body(): cache_v[:, :, 1].reshape(cache_count, blk_len, head_count, HD)  24.3 us
    slice x1, local copies, waits for them, and re-layouts, body(): cache[:, :, 0].reshape(cache_count, blk_len, head_count, HD)  18.4 us
    all_gather x1, waiting for transfers between devices, body(): part_out = lax.all_gather(w_out_local, 'wide', axis=0, tiled=True)  18 us
    gather x2, local copies, waits for them, and re-layouts, body(): q_heads[:, slot_of.reshape(req_count, per_request)]  11.5 us
    all_gather x1, waiting for transfers between devices, body(): all_queries = lax.all_gather(queries, 'wide', axis=1, tiled=True)  11.4 us
  transfers between devices with their start and end apart: 7, of which 6 were waited for; matrix products, arithmetic and copies ran while one was open for 29% of the time, Pallas kernels for 16%

profile of v15, /device:TPU:0, one launch (start us, length us, event | category | flops | bytes accessed | tf_op | source)
XLA Modules:
  0.0 285.2 jit_solution(9390485457183970394)
XLA Ops:
  6.5 2.0 slice.37
  8.6 0.7 and_select_fusion.1
  9.3 0.8 select_reduce_fusion.2
  10.3 0.7 convert_element_type.40
  11.0 18.4 %slice_reduce_fusion = bf16[32,64,768]{2,1,0:T(8,128)(2,1)S(1)} fusion(bf16[32,64,2,768]{3,2,1,0:T(2,128)(2,1)} %param.12), kind=kLoop, calls=%fused_computation.2 | loop fusion | bytes 6291456 | tf_op jit(solution)/shard_map/slice | solution.py:186
  29.5 5.5 %reshape_squeeze.9 = bf16[32,64,8,96]{3,2,1,0:T(8,128)(2,1)} reshape(bf16[32,64,768]{2,1,0:T(8,128)(2,1)S(1)} %slice_reduce_fusion) | data formatting | bytes 6291456 | tf_op jit(solution)/shard_map/reshape;squeeze | solution.py:186
  35.0 5.5 %copy.39 = bf16[32,64,8,96]{3,1,2,0:T(8,128)(2,1)} copy(bf16[32,64,8,96]{3,2,1,0:T(8,128)(2,1)} %reshape_squeeze.9) | data formatting | bytes 6291456 | tf_op jit(solution)/shard_map/reshape;squeeze | solution.py:186
  41.2 9.7 %all-gather.12.cloned.1.call-done = bf16[3072,1,768]{2,0,1:T(8,128)(2,1)} async-done(((bf16[384,1,768]{2,0,1:T(8,128)(2,1)}), bf16[3072,1,768]{2,0,1:T(8,128)(2,1)}) %all-gather.12.cloned.1.call-update) | async-done | bytes 4718608 | tf_op jit(solution)/shard_map/all_gather | solution.py:178
  50.9 4.4 %fusion.7 = f32[256,768]{0,1:T(8,128)S(1)} fusion(bf16[3072,768]{1,0:T(8,128)(2,1)} %bitcast.58, bf16[256,3072]{1,0:T(8,128)(2,1)S(1)} %copy-done.1, f32[3072]{0:T(1024)S(1)} %convert_element_type.40, f32[256]{0:T(256)S(1)} %add_rsqrt_fusion), kind=kOutput, calls=%fused_computation.17 | convolution fusion | flops 1211105280 | bytes 7091200 | tf_op jit(solution)/shard_map/dot_general | solution.py:195
  56.0 1.1 maximum_bitcast_fusion
  57.1 1.1 slice.42
  58.3 8.8 %slice.41 = bf16[32,64,1,768]{3,2,1,0:T(2,128)(2,1)} slice(bf16[32,64,2,768]{3,2,1,0:T(2,128)(2,1)} %param.12), slice={[0:32], [0:64], [1:2], [0:768]} | slice | bytes 6291456 | tf_op jit(solution)/shard_map/slice | solution.py:205
  67.1 15.5 %copy.29 = bf16[32,64,1,768]{1,3,0,2:T(8,128)(2,1)} copy(bf16[32,64,1,768]{3,2,1,0:T(2,128)(2,1)} %slice.41) | data formatting | bytes 6291456 | tf_op jit(solution)/shard_map/slice | solution.py:205
  82.6 11.4 %all-gather.6.cloned.1.call-done.refs_0_ = bf16[8,32,64,96]{3,2,1,0:T(8,128)(2,1)} async-done(((bf16[8,4,64,96]{3,2,1,0:T(8,128)(2,1)}), bf16[8,32,64,96]{3,2,1,0:T(8,128)(2,1)}) %all-gather.6.cloned.1.call-update) | async-done | bytes 3145744 | tf_op jit(solution)/shard_map/all_gather | solution.py:202
  95.3 0.6 select_reduce_fusion.3.limit_ref
  95.9 5.3 %gather_fusion = bf16[32,8,64,96]{3,2,1,0:T(8,128)(2,1)} fusion(bf16[8,32,64,96]{3,2,1,0:T(8,128)(2,1)} %all-gather.6.cloned.1.call-done.refs_0_, s32[1024]{0:T(1024)S(1)} %pad_clamp_fusion), kind=kCustom, calls=%fused_computation | custom fusion | bytes 6291584 | tf_op jit(solution)/shard_map/gather | solution.py:222
  101.2 6.2 %copy.30 = bf16[4,8,8,64,96]{4,3,1,2,0:T(8,128)(2,1)} copy(bf16[4,8,8,64,96]{4,3,2,1,0:T(8,128)(2,1)} %bitcast.47) | data formatting | bytes 6291456 | tf_op jit(solution)/shard_map/gather | solution.py:222
  107.4 36.2 %shard_map.82 = (f32[4,8,1,512]{3,2,1,0:T(1,128)}, f32[4,8,1,512]{3,2,1,0:T(1,128)}, f32[4,8,96,512]{3,2,1,0:T(8,128)}) custom-call(s32[32]{0:T(128)} %copy-done.8, s32[32]{0:T(128)} %get-tuple-element.51.base_ref, s32[32]{0:T(128)} %select_reduce_fusion.3.limit_ref, s32[4]{0:T(128)} %len_ref.3, s32[32]{0:T(128)} %copy-done.3, ...), custom_call_target="tpu_custom_call" | custom-call | tf_op jit(solution)/shard_map/pallas_call | solution.py:152
  143.7 11.0 %all-gather.10.cloned.1.call-done = bf16[3072,2,768]{2,0,1:T(8,128)(2,1)} async-done(((bf16[384,2,768]{2,0,1:T(8,128)(2,1)}), bf16[3072,2,768]{2,0,1:T(8,128)(2,1)}) %all-gather.10.cloned.1.call-update) | async-done | bytes 9437200 | tf_op jit(solution)/shard_map/all_gather | solution.py:210
  154.7 5.4 %fusion.3 = f32[256,2,768]{2,0,1:T(8,128)S(1)} fusion(bf16[3072,2,768]{2,0,1:T(8,128)(2,1)} %all-gather.10.cloned.1.call-done, bf16[256,3072]{1,0:T(8,128)(2,1)S(1)} %copy-done.2, f32[3072]{0:T(1024)S(1)} %convert_element_type.40, f32[256]{0:T(256)S(1)} %add_rsqrt_fusion), kind=kOutput, calls=%fused_computation.10 | convolution fusion | flops 2419064832 | bytes 12596224 | tf_op jit(solution)/shard_map/tk,kcj->tcj/dot_general | solution.py:227
  160.5 0.6 convert_element_type.44
  161.7 1.2 copy.34
  163.5 1.1 maximum_bitcast_fusion.1.refs_1_
  164.6 0.6 broadcast_13_limit_ref.2.limit_ref
  165.2 10.2 %shard_map.83 = (bf16[8,8,96,256]{3,2,1,0:T(8,128)(2,1)}, f32[8,8,2,256]{3,2,1,0:T(2,128)}) custom-call(s32[4]{0:T(128)} %copy-done.6, s32[4]{0:T(128)} %copy-done.5, s32[4]{0:T(128)} %broadcast_13_limit_ref.2.limit_ref, s32[4]{0:T(128)} %len_ref.3, s32[32]{0:T(128)} %copy-done.3, bf16[4,8,512,96]{3,2,1,0:T(8,128)(2,1)} %bitcast.48, ...), custom_call_target="tpu_custom_call" | custom-call | tf_op jit(solution)/shard_map/pallas_call | solution.py:152
  175.4 3.4 %all-to-all-start.1 = ((f32[8,8,2,256]{3,2,1,0:T(2,128)}), f32[8,8,2,256]{3,2,1,0:T(2,128)S(1)}, u32[]{:S(2)}, u32[]{:S(2)}) async-start(f32[8,8,2,256]{3,2,1,0:T(2,128)} %get-tuple-element.39), calls=%async_computation.1 | async-start | bytes 262144 | tf_op jit(solution)/shard_map/all_to_all | solution.py:250
  178.8 18.0 %all-gather.8.cloned.1.call-done = bf16[3072,768]{1,0:T(8,128)(2,1)} async-done(((bf16[384,768]{1,0:T(8,128)(2,1)}), bf16[3072,768]{1,0:T(8,128)(2,1)}) %all-gather.8.cloned.1.call-update) | async-done | bytes 4718608 | tf_op jit(solution)/shard_map/all_gather | solution.py:225
  196.8 3.6 %all-to-all-start = ((bf16[8,8,96,256]{3,2,1,0:T(8,128)(2,1)}), bf16[8,8,96,256]{3,2,1,0:T(8,128)(2,1)S(1)}, u32[]{:S(2)}, u32[]{:S(2)}) async-start(bf16[8,8,96,256]{3,2,1,0:T(8,128)(2,1)} %get-tuple-element.38), calls=%async_computation | async-start | bytes 6291456 | tf_op jit(solution)/shard_map/all_to_all | solution.py:249
  200.8 37.5 %all-to-all-done = bf16[8,8,96,256]{3,2,1,0:T(8,128)(2,1)S(1)} async-done(((bf16[8,8,96,256]{3,2,1,0:T(8,128)(2,1)}), bf16[8,8,96,256]{3,2,1,0:T(8,128)(2,1)S(1)}, u32[]{:S(2)}, u32[]{:S(2)}) %all-to-all-start) | async-done | bytes 3145760 | tf_op jit(solution)/shard_map/all_to_all | solution.py:249
  238.3 0.7 multiply_reduce_fusion
  239.1 4.9 %convolution_convert_fusion = bf16[256,3072]{1,0:T(8,128)(2,1)} fusion(bf16[256,768]{0,1:T(8,128)(2,1)S(1)} %bitcast.54, bf16[768,3072]{0,1:T(8,128)(2,1)} %bitcast.57), kind=kOutput, calls=%fused_computation.6 | convolution fusion | flops 1208745984 | bytes 6684672 | tf_op jit(solution)/shard_map/dot_general | solution.py:261
  244.1 34.6 %reduce-scatter.2.cloned.1.call-done = bf16[256,768]{1,0:T(8,128)(2,1)} async-done(((bf16[256,3072]{1,0:T(8,128)(2,1)}), bf16[256,768]{1,0:T(8,128)(2,1)}) %reduce-scatter.2.cloned.1.call-update) | async-done | bytes 393232 | tf_op jit(solution)/shard_map/reduce_scatter | solution.py:264
  (61 shorter events, 4.8 us)
Async XLA Ops:
  6.5 44.4 %all-gather.12.cloned.1.call-start = ((), (), s32[]{:S(2)}) async-start(), calls=%async_computation.7 | async-start | bytes 5308416 | tf_op jit(solution)/shard_map/all_gather | solution.py:178
  8.5 85.4 %all-gather.6.cloned.1.call-start = ((), (), s32[]{:S(2)}) async-start(), calls=%async_computation.3 | async-start | bytes 4718592 | tf_op jit(solution)/shard_map/all_gather | solution.py:202
  9.3 20.2 %copy-start.6 = (s32[4]{0:T(128)}, s32[4]{0:T(128)S(1)}, u32[]{:S(2)}) copy-start(s32[4]{0:T(128)S(1)} %get-tuple-element.43.req_ref) | copy-start | bytes 52
  10.2 19.3 %copy-start.5 = (s32[4]{0:T(128)}, s32[4]{0:T(128)S(1)}, u32[]{:S(2)}) copy-start(s32[4]{0:T(128)S(1)} %fusion.12.base_ref) | copy-start | bytes 52
  35.0 5.5 %copy-start.1 = (bf16[256,3072]{1,0:T(8,128)(2,1)S(1)}, bf16[256,3072]{1,0:T(8,128)(2,1)}, u32[]{:S(2)}) copy-start(bf16[256,3072]{1,0:T(8,128)(2,1)} %param.8) | copy-start | bytes 4718596
  55.3 1.9 copy-start
  57.1 97.7 %all-gather.10.cloned.1.call-start = ((), (), s32[]{:S(2)}) async-start(), calls=%async_computation.5 | async-start | bytes 10616832 | tf_op jit(solution)/shard_map/all_gather | solution.py:210
  67.1 27.1 %copy-start.9 = (s32[32]{0:T(128)S(1)}, s32[32]{0:T(128)}, u32[]{:S(2)}) copy-start(s32[32]{0:T(128)} %param.14) | copy-start | bytes 388
  67.1 27.4 %copy-start.7 = (s32[256]{0:T(256)S(1)}, s32[256]{0:T(256)}, u32[]{:S(2)}) copy-start(s32[256]{0:T(256)} %param.15) | copy-start | bytes 3076
  67.1 28.2 %copy-start.4 = (s32[4]{0:T(128)S(1)}, s32[4]{0:T(128)}, u32[]{:S(2)}) copy-start(s32[4]{0:T(128)} %len_ref.3) | copy-start | bytes 52
  94.0 102.8 %all-gather.8.cloned.1.call-start = ((), (), s32[]{:S(2)}) async-start(), calls=%async_computation.4 | async-start | bytes 5308416 | tf_op jit(solution)/shard_map/all_gather | solution.py:225
  94.3 6.9 %copy-start.3 = (s32[32]{0:T(128)}, s32[32]{0:T(128)S(1)}, u32[]{:S(2)}) copy-start(s32[32]{0:T(128)S(1)} %select_reduce_fusion.1.slot_ref) | copy-start | bytes 388
  95.3 6.0 %copy-start.8 = (s32[32]{0:T(128)}, s32[32]{0:T(128)S(1)}, u32[]{:S(2)}) copy-start(s32[32]{0:T(128)S(1)} %get-tuple-element.52.req_ref) | copy-start | bytes 388
  107.4 47.3 %copy-start.2 = (bf16[256,3072]{1,0:T(8,128)(2,1)S(1)}, bf16[256,3072]{1,0:T(8,128)(2,1)}, u32[]{:S(2)}) copy-start(bf16[256,3072]{1,0:T(8,128)(2,1)} %param.8) | copy-start | bytes 4718596
  175.4 21.4 %all-to-all-start.1 = ((f32[8,8,2,256]{3,2,1,0:T(2,128)}), f32[8,8,2,256]{3,2,1,0:T(2,128)S(1)}, u32[]{:S(2)}, u32[]{:S(2)}) async-start(f32[8,8,2,256]{3,2,1,0:T(2,128)} %get-tuple-element.39), calls=%async_computation.1 | async-start | bytes 262144 | tf_op jit(solution)/shard_map/all_to_all | solution.py:250
  196.8 41.5 %all-to-all-start = ((bf16[8,8,96,256]{3,2,1,0:T(8,128)(2,1)}), bf16[8,8,96,256]{3,2,1,0:T(8,128)(2,1)S(1)}, u32[]{:S(2)}, u32[]{:S(2)}) async-start(bf16[8,8,96,256]{3,2,1,0:T(8,128)(2,1)} %get-tuple-element.38), calls=%async_computation | async-start | bytes 6291456 | tf_op jit(solution)/shard_map/all_to_all | solution.py:249
  200.5 78.2 %reduce-scatter.2.cloned.1.call-start = ((), (), s32[]{:S(2)}) async-start(), calls=%async_computation.6 | async-start | bytes 1966080 | tf_op jit(solution)/shard_map/reduce_scatter | solution.py:264
Sparse Core Ops, SparseCore 0:
  9.2 41.6 all-gather.11
  57.2 36.7 all-gather.5
  95.9 58.8 all-gather.9
  156.5 40.3 all-gather.7
  244.2 34.4 reduce-scatter.1

commit v16 on v13

--- a/solution.py
+++ b/solution.py
@@ -246,9 +246,11 @@
     )
 
     got_num = lax.all_to_all(sent_num, "wide", split_axis=0, concat_axis=0, tiled=True)
-    got_stats = lax.all_to_all(sent_stats, "wide", split_axis=0, concat_axis=0, tiled=True)
-    got_max = got_stats[:, :, 0:1]
-    got_den = got_stats[:, :, 1:2]
+    got_stats = lax.all_to_all(
+        jnp.transpose(sent_stats, (0, 2, 1, 3)), "wide", split_axis=0, concat_axis=0, tiled=True
+    )
+    got_max = got_stats[:, 0][:, :, None]
+    got_den = got_stats[:, 1][:, :, None]
     top_max = jnp.max(got_max, axis=0)
     factor = jnp.exp(got_max - top_max[None])
     num_own = jnp.sum(got_num.astype(jnp.float32) * factor, axis=0)

time: 278 us -> 278 us (level)
  no operation moved by 1% of the time
where the time goes in v16:
time: 278 us; the launch traced here: 277 us
  waiting for transfers between devices  109 us (39%)
  local copies, waits for them, and re-layouts  73.4 us (26%)
  Pallas kernels  46.4 us (17%)
  matrix products  14.7 us (5%)
  between operations  13.4 us (5%)
  blocking collectives  10.2 us (4%)
  other arithmetic  5.99 us (2%)
  starting transfers between devices  4 us (1%)
    pallas_call x2, Pallas kernels, attend_blocks(): pl.pallas_call(attend_kernel(carry is not None, out_rows), out_shape=out_...  46.4 us
    all_to_all x1, waiting for transfers between devices, body(): lax.all_to_all(sent_num, 'wide', split_axis=0, concat_axis=0, tiled=True)  40.2 us
    reduce_scatter x1, waiting for transfers between devices, body(): lax.psum_scatter(out_part.astype(jnp.bfloat16), 'narrow', scatter_dimensi...  34.5 us
    slice x2, local copies, waits for them, and re-layouts, body(): cache_v[:, :, 1].reshape(cache_count, blk_len, head_count, HD)  24.3 us
    slice x1, local copies, waits for them, and re-layouts, body(): cache[:, :, 0].reshape(cache_count, blk_len, head_count, HD)  18.4 us
    gather x2, local copies, waits for them, and re-layouts, body(): q_heads[:, slot_of.reshape(req_count, per_request)]  11.5 us
    all_gather x1, waiting for transfers between devices, body(): all_queries = lax.all_gather(queries, 'wide', axis=1, tiled=True)  11.4 us
    all_gather x1, waiting for transfers between devices, body(): w_q = lax.all_gather(w_qkv[:, 0], 'wide', axis=0, tiled=True)  11.4 us
  transfers between devices with their start and end apart: 6, of which 5 were waited for; matrix products, arithmetic and copies ran while one was open for 29% of the time, Pallas kernels for 17%

profile of v16, /device:TPU:0, one launch (start us, length us, event | category | flops | bytes accessed | tf_op | source)
XLA Modules:
  0.0 276.7 jit_solution(3493509911677325265)
XLA Ops:
  6.5 2.0 slice.37
  8.6 18.4 %slice_reduce_fusion = bf16[32,64,768]{2,1,0:T(8,128)(2,1)S(1)} fusion(bf16[32,64,2,768]{3,2,1,0:T(2,128)(2,1)} %param.12), kind=kLoop, calls=%fused_computation.2 | loop fusion | bytes 6291456 | tf_op jit(solution)/shard_map/slice | solution.py:186
  27.0 5.5 %reshape_squeeze.9 = bf16[32,64,8,96]{3,2,1,0:T(8,128)(2,1)} reshape(bf16[32,64,768]{2,1,0:T(8,128)(2,1)S(1)} %slice_reduce_fusion) | data formatting | bytes 6291456 | tf_op jit(solution)/shard_map/reshape;squeeze | solution.py:186
  32.5 5.8 %copy.39 = bf16[32,64,8,96]{3,1,2,0:T(8,128)(2,1)} copy(bf16[32,64,8,96]{3,2,1,0:T(8,128)(2,1)} %reshape_squeeze.9) | data formatting | bytes 6291456 | tf_op jit(solution)/shard_map/reshape;squeeze | solution.py:186
  38.9 0.4 fusion
  39.5 11.4 %all-gather.12.cloned.1.call-done = bf16[3072,1,768]{2,0,1:T(8,128)(2,1)} async-done(((bf16[384,1,768]{2,0,1:T(8,128)(2,1)}), bf16[3072,1,768]{2,0,1:T(8,128)(2,1)}) %all-gather.12.cloned.1.call-update) | async-done | bytes 4718608 | tf_op jit(solution)/shard_map/all_gather | solution.py:178
  50.9 4.4 %fusion.7 = f32[256,768]{0,1:T(8,128)S(1)} fusion(bf16[3072,768]{1,0:T(8,128)(2,1)} %bitcast.72, bf16[256,3072]{1,0:T(8,128)(2,1)S(1)} %copy-done.1, f32[3072]{0:T(1024)S(1)} %convert_element_type.40, f32[256]{0:T(256)S(1)} %add_rsqrt_fusion), kind=kOutput, calls=%fused_computation.17 | convolution fusion | flops 1211105280 | bytes 7091200 | tf_op jit(solution)/shard_map/dot_general | solution.py:195
  56.0 1.1 maximum_bitcast_fusion
  57.2 1.1 slice.42
  58.3 8.8 %slice.41 = bf16[32,64,1,768]{3,2,1,0:T(2,128)(2,1)} slice(bf16[32,64,2,768]{3,2,1,0:T(2,128)(2,1)} %param.12), slice={[0:32], [0:64], [1:2], [0:768]} | slice | bytes 6291456 | tf_op jit(solution)/shard_map/slice | solution.py:205
  67.1 15.5 %copy.29 = bf16[32,64,1,768]{1,3,0,2:T(8,128)(2,1)} copy(bf16[32,64,1,768]{3,2,1,0:T(2,128)(2,1)} %slice.41) | data formatting | bytes 6291456 | tf_op jit(solution)/shard_map/slice | solution.py:205
  82.6 11.4 %all-gather.6.cloned.1.call-done.refs_0_ = bf16[8,32,64,96]{3,2,1,0:T(8,128)(2,1)} async-done(((bf16[8,4,64,96]{3,2,1,0:T(8,128)(2,1)}), bf16[8,32,64,96]{3,2,1,0:T(8,128)(2,1)}) %all-gather.6.cloned.1.call-update) | async-done | bytes 3145744 | tf_op jit(solution)/shard_map/all_gather | solution.py:202
  94.7 0.5 fusion.15
  95.3 0.7 select_reduce_fusion.2.limit_ref
  95.9 5.3 %gather_fusion = bf16[32,8,64,96]{3,2,1,0:T(8,128)(2,1)} fusion(bf16[8,32,64,96]{3,2,1,0:T(8,128)(2,1)} %all-gather.6.cloned.1.call-done.refs_0_, s32[1024]{0:T(1024)S(1)} %pad_clamp_fusion), kind=kCustom, calls=%fused_computation | custom fusion | bytes 6291584 | tf_op jit(solution)/shard_map/gather | solution.py:222
  101.3 6.2 %copy.30 = bf16[4,8,8,64,96]{4,3,1,2,0:T(8,128)(2,1)} copy(bf16[4,8,8,64,96]{4,3,2,1,0:T(8,128)(2,1)} %bitcast.62) | data formatting | bytes 6291456 | tf_op jit(solution)/shard_map/gather | solution.py:222
  107.5 36.2 %shard_map.82 = (f32[4,8,1,512]{3,2,1,0:T(1,128)}, f32[4,8,1,512]{3,2,1,0:T(1,128)}, f32[4,8,96,512]{3,2,1,0:T(8,128)}) custom-call(s32[32]{0:T(128)} %copy-done.9, s32[32]{0:T(128)} %get-tuple-element.47.base_ref, s32[32]{0:T(128)} %select_reduce_fusion.2.limit_ref, s32[4]{0:T(128)} %len_ref.3, s32[32]{0:T(128)} %copy-done.4, ...), custom_call_target="tpu_custom_call" | custom-call | tf_op jit(solution)/shard_map/pallas_call | solution.py:152
  143.7 11.0 %all-gather.8.cloned.1.call-done = bf16[3072,2,768]{2,0,1:T(8,128)(2,1)} async-done(((bf16[384,2,768]{2,0,1:T(8,128)(2,1)}), bf16[3072,2,768]{2,0,1:T(8,128)(2,1)}) %all-gather.8.cloned.1.call-update) | async-done | bytes 9437200 | tf_op jit(solution)/shard_map/all_gather | solution.py:210
  154.8 5.4 %fusion.3 = f32[256,2,768]{2,0,1:T(8,128)S(1)} fusion(bf16[3072,2,768]{2,0,1:T(8,128)(2,1)} %all-gather.8.cloned.1.call-done, bf16[256,3072]{1,0:T(8,128)(2,1)S(1)} %copy-done.2, f32[3072]{0:T(1024)S(1)} %convert_element_type.40, f32[256]{0:T(256)S(1)} %add_rsqrt_fusion), kind=kOutput, calls=%fused_computation.10 | convolution fusion | flops 2419064832 | bytes 12596224 | tf_op jit(solution)/shard_map/tk,kcj->tcj/dot_general | solution.py:227
  160.8 0.3 copy.33
  161.4 0.3 copy.32
  161.8 0.6 convert_element_type.44
  162.3 1.2 copy.34
  163.6 1.1 maximum_bitcast_fusion.1.refs_1_
  164.7 0.5 broadcast_13_limit_ref.2.limit_ref
  165.2 10.2 %shard_map.83 = (bf16[8,8,96,256]{3,2,1,0:T(8,128)(2,1)}, f32[8,8,2,256]{3,2,1,0:T(2,128)}) custom-call(s32[4]{0:T(128)} %copy-done.7, s32[4]{0:T(128)} %copy-done.6, s32[4]{0:T(128)} %broadcast_13_limit_ref.2.limit_ref, s32[4]{0:T(128)} %len_ref.3, s32[32]{0:T(128)} %copy-done.4, bf16[4,8,512,96]{3,2,1,0:T(8,128)(2,1)} %bitcast.63, ...), custom_call_target="tpu_custom_call" | custom-call | tf_op jit(solution)/shard_map/pallas_call | solution.py:152
  175.4 10.2 %all_to_all.10 = f32[8,2,8,256]{3,1,2,0:T(2,128)S(1)} all-to-all(f32[8,2,8,256]{3,1,2,0:T(2,128)} %bitcast.70), channel_id=1, replica_groups=mesh['wide'=8,'narrow'=4] {'wide'}, dimensions={0} | all-to-all | bytes 262144 | tf_op jit(solution)/shard_map/all_to_all | solution.py:249
  185.6 3.6 %all-to-all-start = ((bf16[8,8,96,256]{3,2,1,0:T(8,128)(2,1)}), bf16[8,8,96,256]{3,2,1,0:T(8,128)(2,1)S(1)}, u32[]{:S(2)}, u32[]{:S(2)}) async-start(bf16[8,8,96,256]{3,2,1,0:T(8,128)(2,1)} %get-tuple-element.34), calls=%async_computation | async-start | bytes 6291456 | tf_op jit(solution)/shard_map/all_to_all | solution.py:248
  189.6 40.2 %all-to-all-done = bf16[8,8,96,256]{3,2,1,0:T(8,128)(2,1)S(1)} async-done(((bf16[8,8,96,256]{3,2,1,0:T(8,128)(2,1)}), bf16[8,8,96,256]{3,2,1,0:T(8,128)(2,1)S(1)}, u32[]{:S(2)}, u32[]{:S(2)}) %all-to-all-start) | async-done | bytes 3145760 | tf_op jit(solution)/shard_map/all_to_all | solution.py:248
  229.8 0.7 multiply_reduce_fusion
  230.6 4.9 %convolution_convert_fusion = bf16[256,3072]{1,0:T(8,128)(2,1)} fusion(bf16[256,768]{0,1:T(8,128)(2,1)S(1)} %bitcast.69, bf16[3072,768]{1,0:T(8,128)(2,1)} %all-gather.10.cloned.1.call-done), kind=kOutput, calls=%fused_computation.6 | convolution fusion | flops 1208745984 | bytes 6684672 | tf_op jit(solution)/shard_map/dot_general | solution.py:262
  235.6 34.5 %reduce-scatter.2.cloned.1.call-done = bf16[256,768]{1,0:T(8,128)(2,1)} async-done(((bf16[256,3072]{1,0:T(8,128)(2,1)}), bf16[256,768]{1,0:T(8,128)(2,1)}) %reduce-scatter.2.cloned.1.call-update) | async-done | bytes 393232 | tf_op jit(solution)/shard_map/reduce_scatter | solution.py:265
  (62 shorter events, 3.6 us)
Async XLA Ops:
  6.5 44.4 %all-gather.12.cloned.1.call-start = ((), (), s32[]{:S(2)}) async-start(), calls=%async_computation.7 | async-start | bytes 5308416 | tf_op jit(solution)/shard_map/all_gather | solution.py:178
  8.5 85.5 %all-gather.6.cloned.1.call-start = ((), (), s32[]{:S(2)}) async-start(), calls=%async_computation.3 | async-start | bytes 4718592 | tf_op jit(solution)/shard_map/all_gather | solution.py:202
  32.5 5.9 %copy-start.3 = (bf16[3072]{0:T(1024)(128)(2,1)S(1)}, bf16[3072]{0:T(1024)(128)(2,1)}, u32[]{:S(2)}) copy-start(bf16[3072]{0:T(1024)(128)(2,1)} %param.9) | copy-start | bytes 18436
  32.5 5.9 %copy-start.10 = (s32[32]{0:T(128)S(1)}, s32[32]{0:T(128)}, u32[]{:S(2)}) copy-start(s32[32]{0:T(128)} %param.14) | copy-start | bytes 388
  32.5 6.0 %copy-start.5 = (s32[4]{0:T(128)S(1)}, s32[4]{0:T(128)}, u32[]{:S(2)}) copy-start(s32[4]{0:T(128)} %len_ref.3) | copy-start | bytes 52
  32.5 6.3 %copy-start.1 = (bf16[256,3072]{1,0:T(8,128)(2,1)S(1)}, bf16[256,3072]{1,0:T(8,128)(2,1)}, u32[]{:S(2)}) copy-start(bf16[256,3072]{1,0:T(8,128)(2,1)} %param.8) | copy-start | bytes 4718596
  38.5 16.8 %copy-start.7 = (s32[4]{0:T(128)}, s32[4]{0:T(128)S(1)}, u32[]{:S(2)}) copy-start(s32[4]{0:T(128)S(1)} %get-tuple-element.37.req_ref) | copy-start | bytes 52
  38.7 16.6 %copy-start.6 = (s32[4]{0:T(128)}, s32[4]{0:T(128)S(1)}, u32[]{:S(2)}) copy-start(s32[4]{0:T(128)S(1)} %fusion.14.base_ref) | copy-start | bytes 52
  55.3 1.9 copy-start
  57.1 97.6 %all-gather.8.cloned.1.call-start = ((), (), s32[]{:S(2)}) async-start(), calls=%async_computation.4 | async-start | bytes 10616832 | tf_op jit(solution)/shard_map/all_gather | solution.py:210
  67.1 27.4 %copy-start.8 = (s32[256]{0:T(256)S(1)}, s32[256]{0:T(256)}, u32[]{:S(2)}) copy-start(s32[256]{0:T(256)} %param.15) | copy-start | bytes 3076
  94.0 136.6 %all-gather.10.cloned.1.call-start = ((), (), s32[]{:S(2)}) async-start(), calls=%async_computation.5 | async-start | bytes 5308416 | tf_op jit(solution)/shard_map/all_gather | solution.py:225
  94.4 6.9 %copy-start.4 = (s32[32]{0:T(128)}, s32[32]{0:T(128)S(1)}, u32[]{:S(2)}) copy-start(s32[32]{0:T(128)S(1)} %select_reduce_fusion.1.slot_ref) | copy-start | bytes 388
  95.3 6.0 %copy-start.9 = (s32[32]{0:T(128)}, s32[32]{0:T(128)S(1)}, u32[]{:S(2)}) copy-start(s32[32]{0:T(128)S(1)} %get-tuple-element.48.req_ref) | copy-start | bytes 388
  107.5 47.3 %copy-start.2 = (bf16[256,3072]{1,0:T(8,128)(2,1)S(1)}, bf16[256,3072]{1,0:T(8,128)(2,1)}, u32[]{:S(2)}) copy-start(bf16[256,3072]{1,0:T(8,128)(2,1)} %param.8) | copy-start | bytes 4718596
  185.6 44.1 %all-to-all-start = ((bf16[8,8,96,256]{3,2,1,0:T(8,128)(2,1)}), bf16[8,8,96,256]{3,2,1,0:T(8,128)(2,1)S(1)}, u32[]{:S(2)}, u32[]{:S(2)}) async-start(bf16[8,8,96,256]{3,2,1,0:T(8,128)(2,1)} %get-tuple-element.34), calls=%async_computation | async-start | bytes 6291456 | tf_op jit(solution)/shard_map/all_to_all | solution.py:248
  189.3 80.8 %reduce-scatter.2.cloned.1.call-start = ((), (), s32[]{:S(2)}) async-start(), calls=%async_computation.6 | async-start | bytes 1966080 | tf_op jit(solution)/shard_map/reduce_scatter | solution.py:265
Sparse Core Ops, SparseCore 0:
  9.2 41.6 all-gather.11
  57.2 36.7 all-gather.5
  95.9 58.8 all-gather.7
  156.5 43.0 all-gather.9
  235.7 34.3 reduce-scatter.1

commit v17 on v13

--- a/solution.py
+++ b/solution.py
@@ -224,7 +224,9 @@
     carry, w_out_local, q_req = lax.optimization_barrier((carry, w_out, q_req))
     part_out = lax.all_gather(w_out_local, "wide", axis=0, tiled=True)
 
-    kv_proj = jnp.einsum("tk,kcj->tcj", normed, w_kv, preferred_element_type=jnp.float32)
+    kv_proj = jnp.dot(
+        normed, w_kv.reshape(w_kv.shape[0], 2 * lane_width), preferred_element_type=jnp.float32
+    ).reshape(tok_rows, 2, lane_width)
     keys_new = (
         rotate(kv_proj[:, 0].reshape(tok_rows, head_count, HD), positions)
         .astype(jnp.bfloat16)

time: 278 us -> 280 us (level)
  no operation moved by 1% of the time
where the time goes in v17:
time: 280 us; the launch traced here: 278 us
  waiting for transfers between devices  110 us (39%)
  local copies, waits for them, and re-layouts  73.7 us (26%)
  Pallas kernels  46.4 us (17%)
  matrix products  14.6 us (5%)
  between operations  13.4 us (5%)
  blocking collectives  10.2 us (4%)
  other arithmetic  5.9 us (2%)
  starting transfers between devices  4 us (1%)
    pallas_call x2, Pallas kernels, attend_blocks(): pl.pallas_call(attend_kernel(carry is not None, out_rows), out_shape=out_...  46.4 us
    all_to_all x1, waiting for transfers between devices, body(): lax.all_to_all(sent_num, 'wide', split_axis=0, concat_axis=0, tiled=True)  40.2 us
    reduce_scatter x1, waiting for transfers between devices, body(): lax.psum_scatter(out_part.astype(jnp.bfloat16), 'narrow', scatter_dimensi...  34.5 us
    slice x2, local copies, waits for them, and re-layouts, body(): cache_v[:, :, 1].reshape(cache_count, blk_len, head_count, HD)  24.3 us
    slice x1, local copies, waits for them, and re-layouts, body(): cache[:, :, 0].reshape(cache_count, blk_len, head_count, HD)  18.4 us
    all_gather x1, waiting for transfers between devices, body(): w_kv = lax.all_gather(w_kv_local, 'wide', axis=0, tiled=True)  12.8 us
    gather x2, local copies, waits for them, and re-layouts, body(): q_heads[:, slot_of.reshape(req_count, per_request)]  11.6 us
    another operation x2, local copies, waits for them, and re-layouts, body(): cache[:, :, 0].reshape(cache_count, blk_len, head_count, HD)  11.4 us
  transfers between devices with their start and end apart: 6, of which 5 were waited for; matrix products, arithmetic and copies ran while one was open for 29% of the time, Pallas kernels for 17%

profile of v17, /device:TPU:0, one launch (start us, length us, event | category | flops | bytes accessed | tf_op | source)
XLA Modules:
  0.0 278.4 jit_solution(3812062227423571878)
XLA Ops:
  6.5 2.0 slice.37
  8.6 18.4 %slice_reduce_fusion = bf16[32,64,768]{2,1,0:T(8,128)(2,1)S(1)} fusion(bf16[32,64,2,768]{3,2,1,0:T(2,128)(2,1)} %param.12), kind=kLoop, calls=%fused_computation.4 | loop fusion | bytes 6291456 | tf_op jit(solution)/shard_map/slice | solution.py:186
  27.0 5.5 %reshape_squeeze.9 = bf16[32,64,8,96]{3,2,1,0:T(8,128)(2,1)} reshape(bf16[32,64,768]{2,1,0:T(8,128)(2,1)S(1)} %slice_reduce_fusion) | data formatting | bytes 6291456 | tf_op jit(solution)/shard_map/reshape;squeeze | solution.py:186
  32.6 5.9 %copy.42 = bf16[32,64,8,96]{3,1,2,0:T(8,128)(2,1)} copy(bf16[32,64,8,96]{3,2,1,0:T(8,128)(2,1)} %reshape_squeeze.9) | data formatting | bytes 6291456 | tf_op jit(solution)/shard_map/reshape;squeeze | solution.py:186
  38.9 0.4 fusion.2
  39.5 11.3 %all-gather.12.cloned.1.call-done = bf16[3072,1,768]{2,0,1:T(8,128)(2,1)} async-done(((bf16[384,1,768]{2,0,1:T(8,128)(2,1)}), bf16[3072,1,768]{2,0,1:T(8,128)(2,1)}) %all-gather.12.cloned.1.call-update) | async-done | bytes 4718608 | tf_op jit(solution)/shard_map/all_gather | solution.py:178
  50.9 4.4 %fusion.8 = f32[256,768]{0,1:T(8,128)S(1)} fusion(bf16[3072,768]{1,0:T(8,128)(2,1)} %bitcast.62, bf16[256,3072]{1,0:T(8,128)(2,1)S(1)} %copy-done, f32[3072]{0:T(1024)S(1)} %convert_element_type.40, f32[256]{0:T(256)S(1)} %add_rsqrt_fusion), kind=kOutput, calls=%fused_computation.18 | convolution fusion | flops 1211105280 | bytes 7091200 | tf_op jit(solution)/shard_map/dot_general | solution.py:195
  56.0 1.1 maximum_bitcast_fusion
  57.2 1.4 copy.39
  58.6 8.8 %slice.41 = bf16[32,64,1,768]{3,2,1,0:T(2,128)(2,1)} slice(bf16[32,64,2,768]{3,2,1,0:T(2,128)(2,1)} %param.12), slice={[0:32], [0:64], [1:2], [0:768]} | slice | bytes 6291456 | tf_op jit(solution)/shard_map/slice | solution.py:205
  67.4 15.5 %copy.30 = bf16[32,64,1,768]{1,3,0,2:T(8,128)(2,1)} copy(bf16[32,64,1,768]{3,2,1,0:T(2,128)(2,1)} %slice.41) | data formatting | bytes 6291456 | tf_op jit(solution)/shard_map/slice | solution.py:205
  82.9 11.1 %all-gather.6.cloned.1.call-done.refs_0_ = bf16[8,32,64,96]{3,2,1,0:T(8,128)(2,1)} async-done(((bf16[8,4,64,96]{3,2,1,0:T(8,128)(2,1)}), bf16[8,32,64,96]{3,2,1,0:T(8,128)(2,1)}) %all-gather.6.cloned.1.call-update) | async-done | bytes 3145744 | tf_op jit(solution)/shard_map/all_gather | solution.py:202
  94.7 0.5 fusion.13
  95.3 0.6 select_reduce_fusion.2.limit_ref
  95.9 5.3 %gather_fusion = bf16[32,8,64,96]{3,2,1,0:T(8,128)(2,1)} fusion(bf16[8,32,64,96]{3,2,1,0:T(8,128)(2,1)} %all-gather.6.cloned.1.call-done.refs_0_, s32[1024]{0:T(1024)S(1)} %pad_clamp_fusion), kind=kCustom, calls=%fused_computation | custom fusion | bytes 6291584 | tf_op jit(solution)/shard_map/gather | solution.py:222
  101.2 6.2 %copy.32 = bf16[4,8,8,64,96]{4,3,1,2,0:T(8,128)(2,1)} copy(bf16[4,8,8,64,96]{4,3,2,1,0:T(8,128)(2,1)} %bitcast.52) | data formatting | bytes 6291456 | tf_op jit(solution)/shard_map/gather | solution.py:222
  107.5 36.2 %shard_map.82 = (f32[4,8,1,512]{3,2,1,0:T(1,128)}, f32[4,8,1,512]{3,2,1,0:T(1,128)}, f32[4,8,96,512]{3,2,1,0:T(8,128)}) custom-call(s32[32]{0:T(128)} %copy-done.8, s32[32]{0:T(128)} %get-tuple-element.47.base_ref, s32[32]{0:T(128)} %select_reduce_fusion.2.limit_ref, s32[4]{0:T(128)} %len_ref.3, s32[32]{0:T(128)} %copy-done.3, ...), custom_call_target="tpu_custom_call" | custom-call | tf_op jit(solution)/shard_map/pallas_call | solution.py:152
  143.7 12.8 %all-gather.8.cloned.1.call-done = bf16[3072,2,768]{0,2,1:T(8,128)(2,1)} async-done(((bf16[384,2,768]{0,2,1:T(8,128)(2,1)}), bf16[3072,2,768]{0,2,1:T(8,128)(2,1)}) %all-gather.8.cloned.1.call-update) | async-done | bytes 9437200 | tf_op jit(solution)/shard_map/all_gather | solution.py:210
  156.5 5.3 %fusion = f32[256,2,768]{2,0,1:T(8,128)S(1)} fusion(bf16[3072,2,768]{0,2,1:T(8,128)(2,1)} %all-gather.8.cloned.1.call-done, bf16[256,3072]{1,0:T(8,128)(2,1)S(1)} %copy-done.1, f32[3072]{0:T(1024)S(1)} %convert_element_type.40, f32[256]{0:T(256)S(1)} %add_rsqrt_fusion), kind=kOutput, calls=%fused_computation.1 | convolution fusion | flops 2419064832 | bytes 12596224 | tf_op jit(solution)/shard_map/dot_general | solution.py:227
  162.5 0.3 copy.35
  163.0 0.3 copy.34
  163.4 0.6 convert_element_type.44
  164.0 1.2 copy.36
  165.2 1.1 maximum_bitcast_fusion.1.refs_1_
  166.3 0.6 broadcast_13_limit_ref.2.limit_ref
  166.9 10.2 %shard_map.83 = (bf16[8,8,96,256]{3,2,1,0:T(8,128)(2,1)}, f32[8,8,2,256]{3,2,1,0:T(2,128)}) custom-call(s32[4]{0:T(128)} %copy-done.6, s32[4]{0:T(128)} %copy-done.5, s32[4]{0:T(128)} %broadcast_13_limit_ref.2.limit_ref, s32[4]{0:T(128)} %len_ref.3, s32[32]{0:T(128)} %copy-done.3, bf16[4,8,512,96]{3,2,1,0:T(8,128)(2,1)} %bitcast.53, ...), custom_call_target="tpu_custom_call" | custom-call | tf_op jit(solution)/shard_map/pallas_call | solution.py:152
  177.1 10.2 %all_to_all.10 = f32[8,8,2,256]{3,2,1,0:T(2,128)S(1)} all-to-all(f32[8,8,2,256]{3,2,1,0:T(2,128)} %get-tuple-element.35), channel_id=1, replica_groups=mesh['wide'=8,'narrow'=4] {'wide'}, dimensions={0} | all-to-all | bytes 262144 | tf_op jit(solution)/shard_map/all_to_all | solution.py:251
  187.3 3.6 %all-to-all-start = ((bf16[8,8,96,256]{3,2,1,0:T(8,128)(2,1)}), bf16[8,8,96,256]{3,2,1,0:T(8,128)(2,1)S(1)}, u32[]{:S(2)}, u32[]{:S(2)}) async-start(bf16[8,8,96,256]{3,2,1,0:T(8,128)(2,1)} %get-tuple-element.34), calls=%async_computation | async-start | bytes 6291456 | tf_op jit(solution)/shard_map/all_to_all | solution.py:250
  191.3 40.2 %all-to-all-done = bf16[8,8,96,256]{3,2,1,0:T(8,128)(2,1)S(1)} async-done(((bf16[8,8,96,256]{3,2,1,0:T(8,128)(2,1)}), bf16[8,8,96,256]{3,2,1,0:T(8,128)(2,1)S(1)}, u32[]{:S(2)}, u32[]{:S(2)}) %all-to-all-start) | async-done | bytes 3145760 | tf_op jit(solution)/shard_map/all_to_all | solution.py:250
  231.5 0.7 multiply_reduce_fusion
  232.4 4.9 %convolution_convert_fusion = bf16[256,3072]{1,0:T(8,128)(2,1)} fusion(bf16[256,768]{0,1:T(8,128)(2,1)S(1)} %bitcast.59, bf16[3072,768]{1,0:T(8,128)(2,1)} %all-gather.10.cloned.1.call-done), kind=kOutput, calls=%fused_computation.8 | convolution fusion | flops 1208745984 | bytes 6684672 | tf_op jit(solution)/shard_map/dot_general | solution.py:262
  237.3 34.5 %reduce-scatter.2.cloned.1.call-done = bf16[256,768]{1,0:T(8,128)(2,1)} async-done(((bf16[256,3072]{1,0:T(8,128)(2,1)}), bf16[256,768]{1,0:T(8,128)(2,1)}) %reduce-scatter.2.cloned.1.call-update) | async-done | bytes 393232 | tf_op jit(solution)/shard_map/reduce_scatter | solution.py:265
  (62 shorter events, 3.5 us)
Async XLA Ops:
  6.5 44.4 %all-gather.12.cloned.1.call-start = ((), (), s32[]{:S(2)}) async-start(), calls=%async_computation.7 | async-start | bytes 5308416 | tf_op jit(solution)/shard_map/all_gather | solution.py:178
  8.5 85.5 %all-gather.6.cloned.1.call-start = ((), (), s32[]{:S(2)}) async-start(), calls=%async_computation.3 | async-start | bytes 4718592 | tf_op jit(solution)/shard_map/all_gather | solution.py:202
  32.5 5.9 %copy-start.2 = (bf16[3072]{0:T(1024)(128)(2,1)S(1)}, bf16[3072]{0:T(1024)(128)(2,1)}, u32[]{:S(2)}) copy-start(bf16[3072]{0:T(1024)(128)(2,1)} %param.9) | copy-start | bytes 18436
  32.5 5.9 %copy-start.9 = (s32[32]{0:T(128)S(1)}, s32[32]{0:T(128)}, u32[]{:S(2)}) copy-start(s32[32]{0:T(128)} %param.14) | copy-start | bytes 388
  32.5 6.0 %copy-start.4 = (s32[4]{0:T(128)S(1)}, s32[4]{0:T(128)}, u32[]{:S(2)}) copy-start(s32[4]{0:T(128)} %len_ref.3) | copy-start | bytes 52
  32.5 6.3 %copy-start = (bf16[256,3072]{1,0:T(8,128)(2,1)S(1)}, bf16[256,3072]{1,0:T(8,128)(2,1)}, u32[]{:S(2)}) copy-start(bf16[256,3072]{1,0:T(8,128)(2,1)} %param.8) | copy-start | bytes 4718596
  38.5 16.8 %copy-start.6 = (s32[4]{0:T(128)}, s32[4]{0:T(128)S(1)}, u32[]{:S(2)}) copy-start(s32[4]{0:T(128)S(1)} %get-tuple-element.39.req_ref) | copy-start | bytes 52
  38.7 16.6 %copy-start.5 = (s32[4]{0:T(128)}, s32[4]{0:T(128)S(1)}, u32[]{:S(2)}) copy-start(s32[4]{0:T(128)S(1)} %fusion.12.base_ref) | copy-start | bytes 52
  55.4 1.7 slice-start
  57.1 99.4 %all-gather.8.cloned.1.call-start = ((), (), s32[]{:S(2)}) async-start(), calls=%async_computation.4 | async-start | bytes 10616832 | tf_op jit(solution)/shard_map/all_gather | solution.py:210
  67.4 27.1 %copy-start.7 = (s32[256]{0:T(256)S(1)}, s32[256]{0:T(256)}, u32[]{:S(2)}) copy-start(s32[256]{0:T(256)} %param.15) | copy-start | bytes 3076
  94.0 138.3 %all-gather.10.cloned.1.call-start = ((), (), s32[]{:S(2)}) async-start(), calls=%async_computation.5 | async-start | bytes 5308416 | tf_op jit(solution)/shard_map/all_gather | solution.py:225
  94.4 6.9 %copy-start.3 = (s32[32]{0:T(128)}, s32[32]{0:T(128)S(1)}, u32[]{:S(2)}) copy-start(s32[32]{0:T(128)S(1)} %select_reduce_fusion.1.slot_ref) | copy-start | bytes 388
  95.3 6.0 %copy-start.8 = (s32[32]{0:T(128)}, s32[32]{0:T(128)S(1)}, u32[]{:S(2)}) copy-start(s32[32]{0:T(128)S(1)} %get-tuple-element.48.req_ref) | copy-start | bytes 388
  107.5 49.0 %copy-start.1 = (bf16[256,3072]{1,0:T(8,128)(2,1)S(1)}, bf16[256,3072]{1,0:T(8,128)(2,1)}, u32[]{:S(2)}) copy-start(bf16[256,3072]{1,0:T(8,128)(2,1)} %param.8) | copy-start | bytes 4718596
  187.3 44.2 %all-to-all-start = ((bf16[8,8,96,256]{3,2,1,0:T(8,128)(2,1)}), bf16[8,8,96,256]{3,2,1,0:T(8,128)(2,1)S(1)}, u32[]{:S(2)}, u32[]{:S(2)}) async-start(bf16[8,8,96,256]{3,2,1,0:T(8,128)(2,1)} %get-tuple-element.34), calls=%async_computation | async-start | bytes 6291456 | tf_op jit(solution)/shard_map/all_to_all | solution.py:250
  191.0 80.9 %reduce-scatter.2.cloned.1.call-start = ((), (), s32[]{:S(2)}) async-start(), calls=%async_computation.6 | async-start | bytes 1966080 | tf_op jit(solution)/shard_map/reduce_scatter | solution.py:265
Sparse Core Ops, SparseCore 0:
  9.2 41.6 all-gather.11
  57.2 36.7 all-gather.5
  95.9 60.5 all-gather.7
  158.2 43.0 all-gather.9
  237.4 34.3 reduce-scatter.1
